TPU v7x, 256 devices: a whole 4x4x8 slice. The times are simulated.
256 devices in a mesh: grp: 8 (over x, core), dev: 32 (over z, y).
Axes of the slice: x: 4, y: 4, z: 8, core: 2. Of those that a mesh axis runs over, the one named last changes fastest.
Arguments:
- references: bfloat16 [192, 2048], P('dev'), may hold values from -4 to 4
- particles: bfloat16 [2048, 65536], P(None, ('grp', 'dev')), may hold values from -1300 to 1300
- defocus_bin: int32 [65536], P(('grp', 'dev')), may hold values from 0 to 63
- contrast_table: float32 [64, 32], replicated, may hold values from 0.1 to 1
- noise_power: float32 [32], replicated, may hold values from 300 to 3000
- class_prior: float32 [192], replicated, may hold values from -3 to 3
Outputs:
- new_references: float32 [192, 2048], P('dev')
- occupancy: float32 [192], P('dev')
All inputs are finite; a program needn't handle non-finite values.
Results may differ from a plain program's by a relative error of at most 0.0015.
Values may be sent and summed in bfloat16 or wider, within the bound.
No kernel may reach another device: no remote copies, remote signals or barrier semaphores. Data moves between devices by JAX's collectives and lax.ppermute only.
A program may use at most 64 MiB of HBM per device.

v0:
```python
import math

import jax
import jax.numpy as jnp
from jax import lax
from jax.sharding import PartitionSpec as P

Q = 32
M = 32
R = 128
CLS_DEV = 6


def angle_tables(cycle_freqs, count_turns):
    freq_index = jnp.arange(cycle_freqs, dtype=jnp.int32)
    turn_index = jnp.arange(count_turns, dtype=jnp.int32)
    wrapped = freq_index[:, None] * turn_index[None, :] % count_turns
    phases = 2.0 * math.pi / count_turns * wrapped.astype(jnp.float32)
    factor = jnp.where(freq_index == 0, 1.0, 2.0).astype(jnp.float32)[:, None]
    cosine = jnp.cos(phases)
    sine_part = jnp.sin(phases)
    score_table = jnp.stack([factor * cosine, factor * sine_part], 0).astype(jnp.bfloat16)
    turn_table = jnp.stack([cosine, sine_part], 0).astype(jnp.bfloat16)
    return (score_table, turn_table)


def particle_terms(particles, defocus_bin, contrast_table, noise_power):
    columns = particles.shape[1]
    cycle_count = contrast_table.shape[1]
    freq_count = particles.shape[0] // (2 * cycle_count)
    onehot = (
        defocus_bin[None, :] == jnp.arange(contrast_table.shape[0], dtype=jnp.int32)[:, None]
    ).astype(jnp.float32)
    contrast = jnp.dot(contrast_table.T, onehot, precision=lax.Precision.HIGHEST)
    scaled = contrast / noise_power[:, None]
    power_term = contrast * scaled
    weighted = (
        particles.astype(jnp.float32).reshape(freq_count, 2, cycle_count, columns)
        * scaled[None, None]
    ).astype(jnp.bfloat16)
    return (weighted.reshape(freq_count, 2 * cycle_count, columns), power_term)


def class_rows(class_block):
    classes = class_block.shape[0]
    class_grid = class_block.reshape(classes, M, 2, Q)
    real_part = class_grid[:, :, 0, :]
    imag_part = class_grid[:, :, 1, :]
    rows_real = jnp.concatenate([real_part, imag_part], -1)
    rows_imag = jnp.concatenate([-imag_part, real_part], -1)
    stacked = jnp.stack([rows_real, rows_imag], 0)
    factor = jnp.where(jnp.arange(M) == 0, 1.0, 2.0).astype(jnp.float32)
    squares = class_grid.astype(jnp.float32) ** 2
    cycle_power = jnp.sum(jnp.sum(squares, axis=2) * factor[None, :, None], axis=1)
    return (stacked, cycle_power)


def block_rows(total_rows):
    return CLS_DEV * math.gcd(total_rows // CLS_DEV, 4)


def local(references, particles, defocus_bin, contrast_table, noise_power, class_prior):
    weighted, power_term = particle_terms(particles, defocus_bin, contrast_table, noise_power)
    score_table, turn_table = angle_tables(M, R)
    columns = particles.shape[1]
    classes_total = CLS_DEV * lax.axis_size("dev")

    def block_scores(class_block, first_row):
        stacked, cycle_power = class_rows(class_block)
        prior_part = lax.dynamic_slice_in_dim(class_prior, first_row, class_block.shape[0], 0)
        crossed = jnp.einsum(
            "pkmc,mcb->pmkb", stacked, weighted, preferred_element_type=jnp.float32
        ).astype(jnp.bfloat16)
        scores = jnp.einsum(
            "pmkb,pmr->krb", crossed, score_table, preferred_element_type=jnp.float32
        )
        penalty = jnp.dot(cycle_power, power_term, precision=lax.Precision.HIGHEST)
        return scores - 0.5 * penalty[:, None, :] + prior_part[:, None, None]

    initial = (jnp.full((columns,), -1e30, jnp.float32), jnp.zeros((columns,), jnp.float32))
    empty_sums = (
        jnp.zeros((classes_total, 2 * M * Q), jnp.float32),
        jnp.zeros((classes_total, Q), jnp.float32),
        jnp.zeros((classes_total,), jnp.float32),
    )
    gathered = lax.all_gather(references, "dev", axis=0, tiled=True)
    height = block_rows(gathered.shape[0])
    block_count = gathered.shape[0] // height
    blocks = gathered.reshape(block_count, height, gathered.shape[1])

    def one_block(current, block_item):
        class_block, offset = block_item
        scores = block_scores(class_block, offset * height)
        block_max = jnp.max(scores, axis=(0, 1))
        new_max = jnp.maximum(current[0], block_max)
        block_total = jnp.sum(jnp.exp(scores - new_max[None, None, :]), axis=(0, 1))
        return ((new_max, current[1] * jnp.exp(current[0] - new_max) + block_total), None)

    result, unused = lax.scan(
        one_block, initial, (blocks, jnp.arange(block_count, dtype=jnp.int32))
    )
    log_norm = result[0] + jnp.log(result[1])
    add_height = block_rows(gathered.shape[0])
    block_count = gathered.shape[0] // add_height
    blocks = gathered.reshape(block_count, add_height, gathered.shape[1])

    def one_block(current, block_item):
        class_block, offset = block_item
        row_start = offset * add_height
        scores = block_scores(class_block, row_start)
        responsibility = jnp.exp(scores - log_norm[None, None, :]).astype(jnp.bfloat16)
        spectra = jnp.einsum(
            "krb,pmr->pmkb", responsibility, turn_table, preferred_element_type=jnp.float32
        ).astype(jnp.bfloat16)
        products = jnp.einsum(
            "pmkb,mcb->kpmc", spectra, weighted, preferred_element_type=jnp.float32
        )
        real_sum = products[:, 0, :, :Q] + products[:, 1, :, Q:]
        imag_sum = products[:, 0, :, Q:] - products[:, 1, :, :Q]
        numerator = jnp.stack([real_sum, imag_sum], 2).reshape(add_height, 2 * M * Q)
        class_weight = jnp.sum(responsibility.astype(jnp.float32), axis=1)
        cycle_sum = jnp.dot(class_weight, power_term.T, precision=lax.Precision.HIGHEST)
        class_mass = jnp.sum(class_weight, axis=1)
        updated = (
            lax.dynamic_update_slice_in_dim(current[0], numerator, row_start, 0),
            lax.dynamic_update_slice_in_dim(current[1], cycle_sum, row_start, 0),
            lax.dynamic_update_slice_in_dim(current[2], class_mass, row_start, 0),
        )
        return (updated, None)

    result, unused = lax.scan(
        one_block, empty_sums, (blocks, jnp.arange(block_count, dtype=jnp.int32))
    )
    numer_all, cycles_all, mass_all = result
    merged = lax.psum((numer_all, cycles_all, mass_all), ("grp", "dev"))
    own_start = lax.axis_index("dev") * CLS_DEV
    numerator = lax.dynamic_slice_in_dim(merged[0], own_start, CLS_DEV, 0)
    cycle_sum = lax.dynamic_slice_in_dim(merged[1], own_start, CLS_DEV, 0)
    class_mass = lax.dynamic_slice_in_dim(merged[2], own_start, CLS_DEV, 0)
    new_references = (numerator.reshape(CLS_DEV, M, 2, Q) / cycle_sum[:, None, None, :]).reshape(
        CLS_DEV, 2 * M * Q
    )
    particle_total = columns * lax.axis_size("grp") * lax.axis_size("dev")
    occupancy = class_mass * (classes_total / particle_total)
    return (new_references, occupancy)


def solution(mesh):
    return jax.shard_map(
        local,
        mesh=mesh,
        in_specs=(P("dev", None), P(None, ("grp", "dev")), P(("grp", "dev")), P(), P(), P()),
        out_specs=(P("dev", None), P("dev")),
        check_vma=False,
    )
```

profile of v0, /device:TPU:1, one launch (start us, length us, event | category | flops | bytes accessed | tf_op | source)
XLA Modules:
  0.0 525.0 jit_solution(9444845568496355798)
XLA Ops:
  7.5 43.4 %all-gather = bf16[32,6,2048]{2,1,0:T(8,128)(2,1)S(1)} all-gather(bf16[1,6,2048]{2,1,0:T(8,128)(2,1)} %bitcast.179), channel_id=1, replica_groups=mesh['grp'=8,'dev'=32] {'dev'}, dimensions={0}, use_global_device_ids=true | all-gather | bytes 811008 | tf_op jit(solution)/shard_map/all_gather | solution.py:86
  50.9 1.2 reshape.224
  52.9 1.2 fusion.39
  54.2 87.8 %while.28 = (s32[]{:T(128)}, f32[256]{0:T(256)S(1)}, f32[256]{0:T(256)S(1)}, bf16[8,24,2048]{2,1,0:T(8,128)(2,1)}, bf16[32,64,256]{2,1,0:T(8,128)(2,1)}, /*index...) while((s32[]{:T(128)}, f32[256]{0:T(256)S(1)}, ...), condition=%wide.region_5.6_spmd.clone, body=%wide.region_0.5_spmd.clone.sunk | while | flops 159947328 | bytes 10727242 | solution.py:99
  56.9 2.5 fusion.111
  60.7 1.2 multiply_reduce_fusion.10
  62.2 2.0 fusion.112
  67.9 2.5 fusion.111
  71.7 1.2 multiply_reduce_fusion.10
  73.2 2.0 fusion.112
  78.9 2.5 fusion.111
  82.7 1.2 multiply_reduce_fusion.10
  84.1 2.0 fusion.112
  89.9 2.5 fusion.111
  93.7 1.2 multiply_reduce_fusion.10
  95.1 2.0 fusion.112
  100.8 2.5 fusion.111
  104.6 1.2 multiply_reduce_fusion.10
  106.1 2.0 fusion.112
  111.8 2.5 fusion.111
  115.6 1.2 multiply_reduce_fusion.10
  117.1 2.0 fusion.112
  122.8 2.5 fusion.111
  126.6 1.2 multiply_reduce_fusion.10
  128.1 2.0 fusion.112
  133.8 2.5 fusion.111
  137.6 1.2 multiply_reduce_fusion.10
  139.0 2.0 fusion.112
  142.2 106.6 %while.27 = (s32[]{:T(128)}, f32[192,2048]{1,0:T(8,128)S(1)}, f32[192,32]{1,0:T(8,128)S(1)}, f32[192]{0:T(256)S(1)}, bf16[8,24,2048]{2,1,0:T(8,128)(2,1)}, /*ind...) while((s32[]{:T(128)}, f32[192,2048]{1,0:T(8,128)S(1)}, ...), condition=%wide.region_11.12_spmd, body=%wide.region_6.11_spmd.sunk | while | flops 313785664 | bytes 12832803 | solution.py:131
  145.2 1.6 fusion.101
  148.1 1.2 multiply_reduce_fusion.8
  149.6 1.3 convert_reduce_fusion.3
  151.3 2.0 convolution_bitcast_fusion.3
  158.5 1.6 fusion.101
  161.4 1.2 multiply_reduce_fusion.8
  162.9 1.3 convert_reduce_fusion.3
  164.6 2.0 convolution_bitcast_fusion.3
  171.8 1.6 fusion.101
  174.7 1.2 multiply_reduce_fusion.8
  176.2 1.3 convert_reduce_fusion.3
  177.9 2.0 convolution_bitcast_fusion.3
  185.1 1.6 fusion.101
  188.0 1.2 multiply_reduce_fusion.8
  189.5 1.3 convert_reduce_fusion.3
  191.2 2.0 convolution_bitcast_fusion.3
  198.4 1.6 fusion.101
  201.3 1.2 multiply_reduce_fusion.8
  202.8 1.3 convert_reduce_fusion.3
  204.5 2.0 convolution_bitcast_fusion.3
  211.7 1.6 fusion.101
  214.7 1.2 multiply_reduce_fusion.8
  216.1 1.3 convert_reduce_fusion.3
  217.8 2.0 convolution_bitcast_fusion.3
  225.0 1.6 fusion.101
  228.0 1.2 multiply_reduce_fusion.8
  229.4 1.3 convert_reduce_fusion.3
  231.1 2.0 convolution_bitcast_fusion.3
  238.3 1.6 fusion.101
  241.3 1.2 multiply_reduce_fusion.8
  242.7 1.3 convert_reduce_fusion.3
  244.4 2.0 convolution_bitcast_fusion.3
  250.0 87.2 %all-reduce = (f32[192,32]{1,0:T(8,128)S(1)}, f32[192]{0:T(256)S(1)}) all-reduce(f32[192,32]{1,0:T(8,128)S(1)} %get-tuple-element.117, f32[192]{0:T(256)S(1)} %get-tuple-element.118), channel_id=1, replica_groups=mesh['grp'=8,'dev'=32] {'grp','dev'}, use_global_device_ids=true, to_apply=%region_13.14 | all-reduce | flops 6336 | bytes 50688 | tf_op jit(solution)/shard_map/psum | solution.py:135
  338.2 178.5 %all-reduce.3.cloned.1.call-done = f32[192,2048]{1,0:T(8,128)} async-done(((f32[192,2048]{1,0:T(8,128)}), f32[192,2048]{1,0:T(8,128)}) %all-reduce.3.cloned.1.call-update) | async-done | bytes 1572880 | tf_op jit(solution)/shard_map/psum | solution.py:135
  516.6 1.5 dynamic-slice_divide_fusion
  (309 shorter events, 92.4 us)
Async XLA Ops:
  7.2 44.9 %copy-start = (f32[64,32]{0,1:T(8,128)S(1)}, f32[64,32]{0,1:T(8,128)}, u32[]{:S(2)}) copy-start(f32[64,32]{0,1:T(8,128)} %param.13) | copy-start | bytes 24580
  7.2 45.7 %copy-start.2 = (bf16[2048,256]{1,0:T(8,128)(2,1)S(1)}, bf16[2048,256]{1,0:T(8,128)(2,1)}, u32[]{:S(2)}) copy-start(bf16[2048,256]{1,0:T(8,128)(2,1)} %param.11) | copy-start | bytes 3145732
  7.2 47.0 %copy-start.3 = (f32[192]{0:T(256)S(1)}, f32[192]{0:T(256)}, u32[]{:S(2)}) copy-start(f32[192]{0:T(256)} %param.15) | copy-start | bytes 2308
  7.2 509.4 %all-reduce.3.cloned.1.call-start = ((), (), s32[]{:S(2)}) async-start(), calls=%async_computation | async-start | bytes 3145728 | tf_op jit(solution)/shard_map/psum | solution.py:135
  248.9 1.1 copy-start.1
Sparse Core Ops, SparseCore 0:
  250.2 266.4 all-reduce.2
where the time goes:
time: 528 us; the launch traced here: 525 us
  waiting for transfers between devices  178 us (34%)
  blocking collectives  131 us (25%)
  matrix products  82.1 us (16%)
  local copies, waits for them, and re-layouts  64.7 us (12%)
  other arithmetic  42.8 us (8%)
  between operations  14.2 us (3%)
  loops' own time  12.1 us (2%)
    psum x1, waiting for transfers between devices, local(): merged = lax.psum((numer_all, cycles_all, mass_all), ('grp', 'dev'))  178 us
    psum x1, blocking collectives, local(): merged = lax.psum((numer_all, cycles_all, mass_all), ('grp', 'dev'))  87.2 us
    all_gather x1, blocking collectives, local(): gathered = lax.all_gather(references, 'dev', axis=0, tiled=True)  43.4 us
    dot_general x16, matrix products, block_scores(): jnp.einsum('pkmc,mcb->pmkb', stacked, weighted, preferred_element_type=jn...  32.7 us
    dot_general x16, matrix products, block_scores(): jnp.einsum('pmkb,pmr->krb', crossed, score_table, preferred_element_type=...  26.3 us
    dynamic_slice x32, local copies, waits for them, and re-layouts, local(): lax.scan(one_block, initial, (blocks, jnp.arange(block_count, dtype=jnp.i...  23.9 us
    reduce_sum x16, other arithmetic, class_rows(): jnp.sum(squares, axis=2) * factor[None, :, None]  18.6 us
    dot_general x8, matrix products, one_block(): jnp.einsum('pmkb,mcb->kpmc', spectra, weighted, preferred_element_type=jn...  15.7 us
  transfers between devices with their start and end apart: 1, of which 1 were waited for; matrix products, arithmetic and copies ran while one was open for 0% of the time, Pallas kernels for 0%

commit v1 on v0

--- a/solution.py
+++ b/solution.py
@@ -132,11 +132,16 @@
         one_block, empty_sums, (blocks, jnp.arange(block_count, dtype=jnp.int32))
     )
     numer_all, cycles_all, mass_all = result
-    merged = lax.psum((numer_all, cycles_all, mass_all), ("grp", "dev"))
-    own_start = lax.axis_index("dev") * CLS_DEV
-    numerator = lax.dynamic_slice_in_dim(merged[0], own_start, CLS_DEV, 0)
-    cycle_sum = lax.dynamic_slice_in_dim(merged[1], own_start, CLS_DEV, 0)
-    class_mass = lax.dynamic_slice_in_dim(merged[2], own_start, CLS_DEV, 0)
+    width = numer_all.shape[1]
+    packed = jnp.concatenate(
+        [numer_all, cycles_all, mass_all[:, None], jnp.zeros((classes_total, 95), jnp.float32)], 1
+    )
+    packed = packed.reshape(lax.axis_size("dev"), CLS_DEV, packed.shape[1])
+    own = lax.psum_scatter(packed, "dev", scatter_dimension=0, tiled=False)
+    own = lax.psum(own, "grp")
+    numerator = own[:, :width]
+    cycle_sum = own[:, width : width + Q]
+    class_mass = own[:, width + Q]
     new_references = (numerator.reshape(CLS_DEV, M, 2, Q) / cycle_sum[:, None, None, :]).reshape(
         CLS_DEV, 2 * M * Q
     )

time: 528 us -> 497 us (0.941)
  blocking collectives: 131 us -> 70.3 us
  waiting for transfers between devices: 178 us -> 204 us
    unnamed x1 -> x2, waiting for transfers between devices: 0.02 us -> 204 us
    psum x1 -> x0, waiting for transfers between devices: 178 us -> none  [local(): merged = lax.psum((numer_all, cycles_all, mass_all), ('grp', 'dev'))]
    psum x1, blocking collectives: 87.2 us -> 26.9 us  [local(): own = lax.psum(own, 'grp')]
where the time goes in v1:
time: 497 us; the launch traced here: 494 us
  waiting for transfers between devices  204 us (41%)
  matrix products  82.1 us (17%)
  blocking collectives  70.3 us (14%)
  local copies, waits for them, and re-layouts  68.5 us (14%)
  other arithmetic  42 us (8%)
  between operations  14.2 us (3%)
  loops' own time  12.1 us (2%)
    unnamed x2, waiting for transfers between devices  204 us
    all_gather x1, blocking collectives, local(): gathered = lax.all_gather(references, 'dev', axis=0, tiled=True)  43.4 us
    dot_general x16, matrix products, block_scores(): jnp.einsum('pkmc,mcb->pmkb', stacked, weighted, preferred_element_type=jn...  32.7 us
    psum x1, blocking collectives, local(): own = lax.psum(own, 'grp')  26.9 us
    dot_general x16, matrix products, block_scores(): jnp.einsum('pmkb,pmr->krb', crossed, score_table, preferred_element_type=...  26.3 us
    dynamic_slice x32, local copies, waits for them, and re-layouts, local(): lax.scan(one_block, initial, (blocks, jnp.arange(block_count, dtype=jnp.i...  23.9 us
    reduce_sum x16, other arithmetic, class_rows(): jnp.sum(squares, axis=2) * factor[None, :, None]  18.6 us
    dot_general x8, matrix products, one_block(): jnp.einsum('pmkb,mcb->kpmc', spectra, weighted, preferred_element_type=jn...  15.7 us
  transfers between devices with their start and end apart: 1, of which 1 were waited for; matrix products, arithmetic and copies ran while one was open for 0% of the time, Pallas kernels for 0%

profile of v1, /device:TPU:1, one launch (start us, length us, event | category | flops | bytes accessed | tf_op | source)
XLA Modules:
  0.0 493.6 jit_solution(4730013904374642111)
XLA Ops:
  7.5 43.4 %all-gather = bf16[32,6,2048]{2,1,0:T(8,128)(2,1)S(1)} all-gather(bf16[1,6,2048]{2,1,0:T(8,128)(2,1)} %bitcast.182), channel_id=1, replica_groups=mesh['grp'=8,'dev'=32] {'dev'}, dimensions={0}, use_global_device_ids=true | all-gather | bytes 811008 | tf_op jit(solution)/shard_map/all_gather | solution.py:86
  50.9 1.2 reshape.232
  52.9 1.2 fusion.39
  54.2 87.8 %while.28 = (s32[]{:T(128)}, f32[256]{0:T(256)S(1)}, f32[256]{0:T(256)S(1)}, bf16[8,24,2048]{2,1,0:T(8,128)(2,1)}, bf16[32,64,256]{2,1,0:T(8,128)(2,1)}, /*index...) while((s32[]{:T(128)}, f32[256]{0:T(256)S(1)}, ...), condition=%wide.region_5.6_spmd.clone, body=%wide.region_0.5_spmd.clone.sunk | while | flops 159947328 | bytes 10727242 | solution.py:99
  56.9 2.5 fusion.112
  60.7 1.2 multiply_reduce_fusion.10
  62.2 2.0 fusion.113
  67.9 2.5 fusion.112
  71.7 1.2 multiply_reduce_fusion.10
  73.2 2.0 fusion.113
  78.9 2.5 fusion.112
  82.7 1.2 multiply_reduce_fusion.10
  84.1 2.0 fusion.113
  89.9 2.5 fusion.112
  93.7 1.2 multiply_reduce_fusion.10
  95.1 2.0 fusion.113
  100.8 2.5 fusion.112
  104.6 1.2 multiply_reduce_fusion.10
  106.1 2.0 fusion.113
  111.8 2.5 fusion.112
  115.6 1.2 multiply_reduce_fusion.10
  117.1 2.0 fusion.113
  122.8 2.5 fusion.112
  126.6 1.2 multiply_reduce_fusion.10
  128.1 2.0 fusion.113
  133.8 2.5 fusion.112
  137.6 1.2 multiply_reduce_fusion.10
  139.0 2.0 fusion.113
  142.2 106.6 %while.27 = (s32[]{:T(128)}, f32[192,2048]{1,0:T(8,128)S(1)}, f32[192,32]{1,0:T(8,128)S(1)}, f32[192]{0:T(256)S(1)}, bf16[8,24,2048]{2,1,0:T(8,128)(2,1)}, /*ind...) while((s32[]{:T(128)}, f32[192,2048]{1,0:T(8,128)S(1)}, ...), condition=%wide.region_11.12_spmd, body=%wide.region_6.11_spmd.sunk | while | flops 313785664 | bytes 12832803 | solution.py:131
  145.2 1.6 fusion.102
  148.1 1.2 multiply_reduce_fusion.8
  149.6 1.3 convert_reduce_fusion.3
  151.3 2.0 convolution_bitcast_fusion.3
  158.5 1.6 fusion.102
  161.4 1.2 multiply_reduce_fusion.8
  162.9 1.3 convert_reduce_fusion.3
  164.6 2.0 convolution_bitcast_fusion.3
  171.8 1.6 fusion.102
  174.7 1.2 multiply_reduce_fusion.8
  176.2 1.3 convert_reduce_fusion.3
  177.9 2.0 convolution_bitcast_fusion.3
  185.1 1.6 fusion.102
  188.0 1.2 multiply_reduce_fusion.8
  189.5 1.3 convert_reduce_fusion.3
  191.1 2.0 convolution_bitcast_fusion.3
  198.4 1.6 fusion.102
  201.3 1.2 multiply_reduce_fusion.8
  202.8 1.3 convert_reduce_fusion.3
  204.4 2.0 convolution_bitcast_fusion.3
  211.7 1.6 fusion.102
  214.6 1.2 multiply_reduce_fusion.8
  216.1 1.3 convert_reduce_fusion.3
  217.7 2.0 convolution_bitcast_fusion.3
  225.0 1.6 fusion.102
  227.9 1.2 multiply_reduce_fusion.8
  229.4 1.3 convert_reduce_fusion.3
  231.0 2.0 convolution_bitcast_fusion.3
  238.3 1.6 fusion.102
  242.7 1.3 convert_reduce_fusion.3
  244.3 2.0 convolution_bitcast_fusion.3
  249.9 1.5 concatenate.22
  251.7 2.2 concatenate.25
  253.9 204.3 %reduce-scatter.4.cloned.1.call-done = f32[1,6,2176]{2,1,0:T(8,128)} async-done(((f32[32,6,2176]{2,1,0:T(8,128)}), f32[1,6,2176]{2,1,0:T(8,128)}) %reduce-scatter.4.cloned.1.call-update) | async-done | bytes 52240
  458.2 26.9 %psum.7 = f32[6,2176]{1,0:T(8,128)S(1)} all-reduce(f32[6,2176]{1,0:T(8,128)} %bitcast.181), channel_id=1, replica_groups=mesh['grp'=8,'dev'=32] {'grp'}, use_global_device_ids=true, to_apply=%region_13.14 | all-reduce | flops 13056 | bytes 104448 | tf_op jit(solution)/shard_map/psum | solution.py:141
  (314 shorter events, 94.5 us)
Async XLA Ops:
  7.2 44.9 %copy-start = (f32[64,32]{0,1:T(8,128)S(1)}, f32[64,32]{0,1:T(8,128)}, u32[]{:S(2)}) copy-start(f32[64,32]{0,1:T(8,128)} %param.13) | copy-start | bytes 24580
  7.2 45.7 %copy-start.2 = (bf16[2048,256]{1,0:T(8,128)(2,1)S(1)}, bf16[2048,256]{1,0:T(8,128)(2,1)}, u32[]{:S(2)}) copy-start(bf16[2048,256]{1,0:T(8,128)(2,1)} %param.11) | copy-start | bytes 3145732
  7.2 47.0 %copy-start.3 = (f32[192]{0:T(256)S(1)}, f32[192]{0:T(256)}, u32[]{:S(2)}) copy-start(f32[192]{0:T(256)} %param.15) | copy-start | bytes 2308
  7.2 451.0 %reduce-scatter.4.cloned.1.call-start = ((), (), s32[]{:S(2)}) async-start(), calls=%async_computation.1 | async-start | bytes 2297856
  248.8 1.2 copy-start.1
Sparse Core Ops, SparseCore 0:
  254.0 204.1 reduce-scatter.3

commit v2 on v1

--- a/solution.py
+++ b/solution.py
@@ -83,7 +83,11 @@
         jnp.zeros((classes_total, Q), jnp.float32),
         jnp.zeros((classes_total,), jnp.float32),
     )
-    gathered = lax.all_gather(references, "dev", axis=0, tiled=True)
+    dev_count = lax.axis_size("dev")
+    copies = jnp.broadcast_to(references[None], (dev_count,) + references.shape)
+    gathered = lax.all_to_all(copies, "dev", 0, 0, tiled=True).reshape(
+        dev_count * references.shape[0], references.shape[1]
+    )
     height = block_rows(gathered.shape[0])
     block_count = gathered.shape[0] // height
     blocks = gathered.reshape(block_count, height, gathered.shape[1])
@@ -136,9 +140,9 @@
     packed = jnp.concatenate(
         [numer_all, cycles_all, mass_all[:, None], jnp.zeros((classes_total, 95), jnp.float32)], 1
     )
-    packed = packed.reshape(lax.axis_size("dev"), CLS_DEV, packed.shape[1])
-    own = lax.psum_scatter(packed, "dev", scatter_dimension=0, tiled=False)
-    own = lax.psum(own, "grp")
+    packed = packed.reshape(dev_count, CLS_DEV, packed.shape[1])
+    own = jnp.sum(lax.all_to_all(packed, "dev", 0, 0, tiled=True), 0)
+    own = jnp.sum(lax.all_gather(own, "grp", axis=0, tiled=False), 0)
     numerator = own[:, :width]
     cycle_sum = own[:, width : width + Q]
     class_mass = own[:, width + Q]

time: 497 us -> 323 us (0.65)
  waiting for transfers between devices: 204 us -> 24.5 us
  between operations: 14.2 us -> 0.85 us
  starting transfers between devices: 0.04 us -> 12.2 us
  blocking collectives: 70.3 us -> 76 us
    unnamed x2 -> x0, waiting for transfers between devices: 204 us -> none
    all_to_all x0 -> x1, blocking collectives: none -> 59 us  [local(): own = jnp.sum(lax.all_to_all(packed, 'dev', 0, 0, tiled=True), 0)]
    psum x1 -> x0, blocking collectives: 26.9 us -> none  [local(): own = lax.psum(own, 'grp')]
    all_gather x1, blocking collectives: 43.4 us -> 17 us  [local(): own = jnp.sum(lax.all_gather(own, 'grp', axis=0, tiled=False), 0)]
    all_to_all x0 -> x1, waiting for transfers between devices: none -> 24.5 us  [local(): lax.all_to_all(copies, 'dev', 0, 0, tiled=True)]
    all_to_all x0 -> x1, starting transfers between devices: none -> 12.2 us  [local(): lax.all_to_all(copies, 'dev', 0, 0, tiled=True)]
where the time goes in v2:
time: 323 us; the launch traced here: 321 us
  matrix products  81.5 us (25%)
  blocking collectives  76 us (24%)
  local copies, waits for them, and re-layouts  69.8 us (22%)
  other arithmetic  43.8 us (14%)
  waiting for transfers between devices  24.5 us (8%)
  starting transfers between devices  12.2 us (4%)
  loops' own time  12.1 us (4%)
    all_to_all x1, blocking collectives, local(): own = jnp.sum(lax.all_to_all(packed, 'dev', 0, 0, tiled=True), 0)  59 us
    dot_general x16, matrix products, block_scores(): jnp.einsum('pkmc,mcb->pmkb', stacked, weighted, preferred_element_type=jn...  32.7 us
    dot_general x16, matrix products, block_scores(): jnp.einsum('pmkb,pmr->krb', crossed, score_table, preferred_element_type=...  26.3 us
    all_to_all x1, waiting for transfers between devices, local(): lax.all_to_all(copies, 'dev', 0, 0, tiled=True)  24.5 us
    dynamic_slice x32, local copies, waits for them, and re-layouts, local(): lax.scan(one_block, initial, (blocks, jnp.arange(block_count, dtype=jnp.i...  23.9 us
    reduce_sum x16, other arithmetic, class_rows(): jnp.sum(squares, axis=2) * factor[None, :, None]  18.6 us
    all_gather x1, blocking collectives, local(): own = jnp.sum(lax.all_gather(own, 'grp', axis=0, tiled=False), 0)  17 us
    dot_general x8, matrix products, one_block(): jnp.einsum('pmkb,mcb->kpmc', spectra, weighted, preferred_element_type=jn...  15.7 us
  transfers between devices with their start and end apart: 1, of which 1 were waited for; matrix products, arithmetic and copies ran while one was open for 0% of the time, Pallas kernels for 0%

profile of v2, /device:TPU:1, one launch (start us, length us, event | category | flops | bytes accessed | tf_op | source)
XLA Modules:
  0.0 320.7 jit_solution(2379513048824179625)
XLA Ops:
  0.7 2.0 broadcast_in_dim.64
  2.7 12.2 %all-to-all-start = ((bf16[32,6,2048]{2,1,0:T(8,128)(2,1)}), bf16[32,6,2048]{2,1,0:T(8,128)(2,1)S(1)}, u32[]{:S(2)}, u32[]{:S(2)}) async-start(bf16[32,6,2048]{2,1,0:T(8,128)(2,1)} %broadcast_in_dim.64), calls=%async_computation | async-start | bytes 2097152 | tf_op jit(solution)/shard_map/all_to_all | solution.py:88
  15.3 1.2 fusion.39
  16.5 24.5 %all-to-all-done = bf16[32,6,2048]{2,1,0:T(8,128)(2,1)S(1)} async-done(((bf16[32,6,2048]{2,1,0:T(8,128)(2,1)}), bf16[32,6,2048]{2,1,0:T(8,128)(2,1)S(1)}, u32[]{:S(2)}, u32[]{:S(2)}) %all-to-all-start) | async-done | bytes 786464 | tf_op jit(solution)/shard_map/all_to_all | solution.py:88
  41.1 1.2 reshape_reshape.4
  42.3 87.8 %while.28 = (s32[]{:T(128)}, f32[256]{0:T(256)S(1)}, f32[256]{0:T(256)S(1)}, bf16[8,24,2048]{2,1,0:T(8,128)(2,1)}, bf16[32,64,256]{2,1,0:T(8,128)(2,1)}, /*index...) while((s32[]{:T(128)}, f32[256]{0:T(256)S(1)}, ...), condition=%wide.region_5.6_spmd.clone, body=%wide.region_0.5_spmd.clone.sunk | while | flops 159947328 | bytes 10727242 | solution.py:103
  45.0 2.5 fusion.112
  48.8 1.2 multiply_reduce_fusion.10
  50.3 2.0 fusion.113
  56.0 2.5 fusion.112
  59.8 1.2 multiply_reduce_fusion.10
  61.3 2.0 fusion.113
  67.0 2.5 fusion.112
  70.8 1.2 multiply_reduce_fusion.10
  72.2 2.0 fusion.113
  78.0 2.5 fusion.112
  81.8 1.2 multiply_reduce_fusion.10
  83.2 2.0 fusion.113
  89.0 2.5 fusion.112
  92.7 1.2 multiply_reduce_fusion.10
  94.2 2.0 fusion.113
  99.9 2.5 fusion.112
  103.7 1.2 multiply_reduce_fusion.10
  105.2 2.0 fusion.113
  110.9 2.5 fusion.112
  114.7 1.2 multiply_reduce_fusion.10
  116.2 2.0 fusion.113
  121.9 2.5 fusion.112
  125.7 1.2 multiply_reduce_fusion.10
  127.1 2.0 fusion.113
  130.3 106.6 %while.27 = (s32[]{:T(128)}, f32[192,2048]{1,0:T(8,128)S(1)}, f32[192,32]{1,0:T(8,128)S(1)}, f32[192]{0:T(256)S(1)}, bf16[8,24,2048]{2,1,0:T(8,128)(2,1)}, /*ind...) while((s32[]{:T(128)}, f32[192,2048]{1,0:T(8,128)S(1)}, ...), condition=%wide.region_11.12_spmd, body=%wide.region_6.11_spmd.sunk | while | flops 313785664 | bytes 12832803 | solution.py:135
  133.3 1.6 fusion.102
  136.2 1.2 multiply_reduce_fusion.8
  137.7 1.3 convert_reduce_fusion.3
  139.4 2.0 convolution_bitcast_fusion.3
  146.6 1.6 fusion.102
  149.5 1.2 multiply_reduce_fusion.8
  151.0 1.3 convert_reduce_fusion.3
  152.7 2.0 convolution_bitcast_fusion.3
  159.9 1.6 fusion.102
  162.8 1.2 multiply_reduce_fusion.8
  164.3 1.3 convert_reduce_fusion.3
  166.0 2.0 convolution_bitcast_fusion.3
  173.2 1.6 fusion.102
  176.1 1.2 multiply_reduce_fusion.8
  177.6 1.3 convert_reduce_fusion.3
  179.3 2.0 convolution_bitcast_fusion.3
  186.5 1.6 fusion.102
  190.9 1.3 convert_reduce_fusion.3
  192.6 2.0 convolution_bitcast_fusion.3
  199.8 1.6 fusion.102
  204.2 1.3 convert_reduce_fusion.3
  205.9 2.0 convolution_bitcast_fusion.3
  213.1 1.6 fusion.102
  217.5 1.3 convert_reduce_fusion.3
  219.2 2.0 convolution_bitcast_fusion.3
  226.4 1.6 fusion.102
  230.8 1.3 convert_reduce_fusion.3
  232.5 2.0 convolution_bitcast_fusion.3
  236.9 1.6 concatenate.22
  238.7 2.5 concatenate.25
  241.3 59.0 %all_to_all.10 = f32[32,6,2176]{2,1,0:T(8,128)} all-to-all(f32[32,6,2176]{2,1,0:T(8,128)S(1)} %concatenate.25), channel_id=1, replica_groups=mesh['grp'=8,'dev'=32] {'dev'}, dimensions={0} | all-to-all | bytes 3342336 | tf_op jit(solution)/shard_map/all_to_all | solution.py:144
  300.3 1.8 reduce_sum.81
  302.1 17.0 %all-gather.1 = f32[8,6,2176]{2,1,0:T(8,128)S(1)} all-gather(f32[1,6,2176]{2,1,0:T(8,128)S(1)} %bitcast.178), channel_id=2, replica_groups=mesh['grp'=8,'dev'=32] {'grp'}, dimensions={0}, use_global_device_ids=true | all-gather | bytes 470016 | tf_op jit(solution)/shard_map/all_gather | solution.py:145
  (318 shorter events, 96.2 us)
Async XLA Ops:
  0.6 14.5 %copy-start = (f32[64,32]{0,1:T(8,128)S(1)}, f32[64,32]{0,1:T(8,128)}, u32[]{:S(2)}) copy-start(f32[64,32]{0,1:T(8,128)} %param.13) | copy-start | bytes 24580
  0.6 14.5 %copy-start.2 = (s32[256]{0:T(256)S(1)}, s32[256]{0:T(256)}, u32[]{:S(2)}) copy-start(s32[256]{0:T(256)} %param.12) | copy-start | bytes 3076
  0.7 14.5 %copy-start.4 = (f32[32]{0:T(128)S(1)}, f32[32]{0:T(128)}, u32[]{:S(2)}) copy-start(f32[32]{0:T(128)} %param.14) | copy-start | bytes 388
  0.7 14.6 %copy-start.1 = (bf16[2048,256]{1,0:T(8,128)(2,1)S(1)}, bf16[2048,256]{1,0:T(8,128)(2,1)}, u32[]{:S(2)}) copy-start(bf16[2048,256]{1,0:T(8,128)(2,1)} %param.11) | copy-start | bytes 3145732
  2.7 39.6 %copy-start.3 = (f32[192]{0:T(256)S(1)}, f32[192]{0:T(256)}, u32[]{:S(2)}) copy-start(f32[192]{0:T(256)} %param.15) | copy-start | bytes 2308
  2.7 38.4 %all-to-all-start = ((bf16[32,6,2048]{2,1,0:T(8,128)(2,1)}), bf16[32,6,2048]{2,1,0:T(8,128)(2,1)S(1)}, u32[]{:S(2)}, u32[]{:S(2)}) async-start(bf16[32,6,2048]{2,1,0:T(8,128)(2,1)} %broadcast_in_dim.64), calls=%async_computation | async-start | bytes 2097152 | tf_op jit(solution)/shard_map/all_to_all | solution.py:88

commit v3 on v2

v3 whole, which is shorter than its diff:
```python
import functools
import math

import jax
import jax.numpy as jnp
from jax import lax
from jax.experimental import pallas as pl
from jax.experimental.pallas import tpu as pltpu
from jax.sharding import PartitionSpec as P

Q = 32
M = 32
R = 128
CLS_DEV = 6
CLS_STEP = 8


def angle_tables(cycle_freqs, count_turns):
    freq_index = jnp.arange(cycle_freqs, dtype=jnp.int32)
    turn_index = jnp.arange(count_turns, dtype=jnp.int32)
    wrapped = freq_index[:, None] * turn_index[None, :] % count_turns
    phases = 2.0 * math.pi / count_turns * wrapped.astype(jnp.float32)
    factor = jnp.where(freq_index == 0, 1.0, 2.0).astype(jnp.float32)[:, None]
    cosine = jnp.cos(phases)
    sine_part = jnp.sin(phases)
    score_table = jnp.stack([factor * cosine, factor * sine_part], 0).astype(jnp.bfloat16)
    turn_table = jnp.stack([cosine, sine_part], 0).astype(jnp.bfloat16)
    return (score_table, turn_table)


def particle_terms(particles, defocus_bin, contrast_table, noise_power):
    columns = particles.shape[1]
    cycle_count = contrast_table.shape[1]
    freq_count = particles.shape[0] // (2 * cycle_count)
    onehot = (
        defocus_bin[None, :] == jnp.arange(contrast_table.shape[0], dtype=jnp.int32)[:, None]
    ).astype(jnp.float32)
    contrast = jnp.dot(contrast_table.T, onehot, precision=lax.Precision.HIGHEST)
    scaled = contrast / noise_power[:, None]
    power_term = contrast * scaled
    weighted = (
        particles.astype(jnp.float32).reshape(freq_count, 2, cycle_count, columns)
        * scaled[None, None]
    ).astype(jnp.bfloat16)
    return (weighted.reshape(freq_count, 2 * cycle_count, columns), power_term)


def class_rows(class_block):
    classes = class_block.shape[0]
    class_grid = class_block.reshape(classes, M, 2, Q)
    real_part = class_grid[:, :, 0, :]
    imag_part = class_grid[:, :, 1, :]
    rows_real = jnp.concatenate([real_part, imag_part], -1)
    rows_imag = jnp.concatenate([-imag_part, real_part], -1)
    stacked = jnp.stack([rows_real, rows_imag], 0)
    factor = jnp.where(jnp.arange(M) == 0, 1.0, 2.0).astype(jnp.float32)
    squares = class_grid.astype(jnp.float32) ** 2
    cycle_power = jnp.sum(jnp.sum(squares, axis=2) * factor[None, :, None], axis=1)
    return (stacked, cycle_power)


def block_scores(table_ref, crossed_ref, half_ref, prior_ref):
    raw = jnp.dot(table_ref[...], crossed_ref[...], preferred_element_type=jnp.float32)
    return raw - half_ref[...] + prior_ref[...]


def norm_kernel(cols, table_ref, crossed_ref, half_ref, prior_ref, out_ref, top_ref, total_ref):
    step = pl.program_id(0)

    @pl.when(step == 0)
    def _():
        top_ref[...] = jnp.full(top_ref.shape, -1e30, jnp.float32)
        total_ref[...] = jnp.zeros(total_ref.shape, jnp.float32)

    scores = block_scores(table_ref, crossed_ref, half_ref, prior_ref)
    parts = [scores[:, j * cols : (j + 1) * cols] for j in range(scores.shape[1] // cols)]
    block_top = functools.reduce(jnp.maximum, [jnp.max(s, axis=0, keepdims=True) for s in parts])
    old_top = top_ref[...]
    new_top = jnp.maximum(old_top, block_top)
    block_total = functools.reduce(
        jnp.add, [jnp.sum(jnp.exp(s - new_top), axis=0, keepdims=True) for s in parts]
    )
    total_ref[...] = total_ref[...] * jnp.exp(old_top - new_top) + block_total
    top_ref[...] = new_top

    @pl.when(step == pl.num_programs(0) - 1)
    def _():
        out_ref[...] = top_ref[...] + jnp.log(total_ref[...])


def spectra_kernel(
    table_ref, crossed_ref, half_ref, prior_ref, norm_ref, turn_ref, spectra_ref, weight_ref
):
    scores = block_scores(table_ref, crossed_ref, half_ref, prior_ref)
    responsibility = jnp.exp(scores - norm_ref[...]).astype(jnp.bfloat16)
    spectra_ref[...] = jnp.dot(
        turn_ref[...], responsibility, preferred_element_type=jnp.float32
    ).astype(jnp.bfloat16)
    weight_ref[...] = jnp.sum(responsibility.astype(jnp.float32), axis=0, keepdims=True)


def local(references, particles, defocus_bin, contrast_table, noise_power, class_prior):
    weighted, power_term = particle_terms(particles, defocus_bin, contrast_table, noise_power)
    score_table, turn_table = angle_tables(M, R)
    columns = particles.shape[1]
    dev_count = lax.axis_size("dev")
    classes_total = CLS_DEV * dev_count

    copies = jnp.broadcast_to(references[None], (dev_count,) + references.shape)
    gathered = lax.all_to_all(copies, "dev", 0, 0, tiled=True).reshape(
        dev_count * references.shape[0], references.shape[1]
    )
    stacked, cycle_power = class_rows(gathered)
    crossed = jnp.einsum(
        "pkmc,mcb->mpkb", stacked, weighted, preferred_element_type=jnp.float32
    ).astype(jnp.bfloat16)
    rows = 2 * M
    width = classes_total * columns
    crossed = crossed.reshape(rows, width)
    penalty = jnp.dot(cycle_power, power_term, precision=lax.Precision.HIGHEST)
    half = (0.5 * penalty).reshape(1, width)
    prior = jnp.broadcast_to(class_prior[:, None], (classes_total, columns)).reshape(1, width)
    table = jnp.transpose(score_table, (2, 1, 0)).reshape(R, rows)
    turn = jnp.transpose(turn_table, (1, 0, 2)).reshape(rows, R)

    block = CLS_STEP * columns
    steps = width // block
    table_spec = pl.BlockSpec((R, rows), lambda i: (0, 0))
    crossed_spec = pl.BlockSpec((rows, block), lambda i: (0, i))
    row_spec = pl.BlockSpec((1, block), lambda i: (0, i))
    log_norm = pl.pallas_call(
        functools.partial(norm_kernel, columns),
        grid=(steps,),
        in_specs=[table_spec, crossed_spec, row_spec, row_spec],
        out_specs=pl.BlockSpec((1, columns), lambda i: (0, 0)),
        out_shape=jax.ShapeDtypeStruct((1, columns), jnp.float32),
        scratch_shapes=[pltpu.VMEM((1, columns), jnp.float32)] * 2,
        compiler_params=pltpu.CompilerParams(dimension_semantics=("arbitrary",)),
    )(table, crossed, half, prior)
    norm_row = jnp.tile(log_norm, (1, classes_total))
    spectra, class_weight = pl.pallas_call(
        spectra_kernel,
        grid=(steps,),
        in_specs=[
            table_spec,
            crossed_spec,
            row_spec,
            row_spec,
            row_spec,
            pl.BlockSpec((rows, R), lambda i: (0, 0)),
        ],
        out_specs=[crossed_spec, row_spec],
        out_shape=[
            jax.ShapeDtypeStruct((rows, width), jnp.bfloat16),
            jax.ShapeDtypeStruct((1, width), jnp.float32),
        ],
        compiler_params=pltpu.CompilerParams(dimension_semantics=("arbitrary",)),
    )(table, crossed, half, prior, norm_row, turn)

    spectra = spectra.reshape(M, 2, classes_total, columns)
    products = jnp.einsum(
        "mpkb,mcb->kpmc", spectra, weighted, preferred_element_type=jnp.float32
    )
    real_sum = products[:, 0, :, :Q] + products[:, 1, :, Q:]
    imag_sum = products[:, 0, :, Q:] - products[:, 1, :, :Q]
    numer_all = jnp.stack([real_sum, imag_sum], 2).reshape(classes_total, 2 * M * Q)
    class_weight = class_weight.reshape(classes_total, columns)
    cycles_all = jnp.dot(class_weight, power_term.T, precision=lax.Precision.HIGHEST)
    mass_all = jnp.sum(class_weight, axis=1)

    width = numer_all.shape[1]
    packed = jnp.concatenate(
        [numer_all, cycles_all, mass_all[:, None], jnp.zeros((classes_total, 95), jnp.float32)], 1
    )
    packed = packed.reshape(dev_count, CLS_DEV, packed.shape[1])
    own = jnp.sum(lax.all_to_all(packed, "dev", 0, 0, tiled=True), 0)
    own = jnp.sum(lax.all_gather(own, "grp", axis=0, tiled=False), 0)
    numerator = own[:, :width]
    cycle_sum = own[:, width : width + Q]
    class_mass = own[:, width + Q]
    new_references = (numerator.reshape(CLS_DEV, M, 2, Q) / cycle_sum[:, None, None, :]).reshape(
        CLS_DEV, 2 * M * Q
    )
    particle_total = columns * lax.axis_size("grp") * lax.axis_size("dev")
    occupancy = class_mass * (classes_total / particle_total)
    return (new_references, occupancy)


def solution(mesh):
    return jax.shard_map(
        local,
        mesh=mesh,
        in_specs=(P("dev", None), P(None, ("grp", "dev")), P(("grp", "dev")), P(), P(), P()),
        out_specs=(P("dev", None), P("dev")),
        check_vma=False,
    )
```

time: 323 us -> 248 us (0.77)
  matrix products: 81.5 us -> 4.93 us
  Pallas kernels: 0 us -> 39.9 us
  other arithmetic: 43.8 us -> 23.8 us
  loops' own time: 12.1 us -> 0 us
  local copies, waits for them, and re-layouts: 69.8 us -> 65.2 us
    dot_general x72 -> x4, matrix products: 81.3 us -> 4.78 us  [the longest x1 2.16 us: local(): jnp.einsum('mpkb,mcb->kpmc', spectra, weighted, preferred_element_type=jn...]
    pallas_call x0 -> x2, Pallas kernels: none -> 39.9 us  [the longest x1 21.3 us: local(): pl.pallas_call(spectra_kernel, grid=(steps,), in_specs=[table_spec, cross...]
    unnamed x10 -> x25, local copies, waits for them, and re-layouts: 0.03 us -> 27.3 us
    dynamic_slice x48 -> x0, local copies, waits for them, and re-layouts: 25.1 us -> none  [the longest x32 23.9 us: local(): lax.scan(one_block, initial, (blocks, jnp.arange(block_count, dtype=jnp.i...]
    another operation x2 -> x0, loops' own time: 12.1 us -> none  [the longest x1 6.45 us: local(): lax.scan(one_block, empty_sums, (blocks, jnp.arange(block_count, dtype=jn...]
    reshape x24 -> x2, local copies, waits for them, and re-layouts: 12.2 us -> 0.78 us  [the longest x1 0.72 us: local(): table = jnp.transpose(score_table, (2, 1, 0)).reshape(R, rows)]
    reduce_sum x16 -> x1, other arithmetic: 18.6 us -> 11 us  [class_rows(): jnp.sum(squares, axis=2) * factor[None, :, None]]
    reduce_sum x8 -> x1, other arithmetic: 7.2 us -> 0.11 us  [local(): mass_all = jnp.sum(class_weight, axis=1)]
  transfers between devices with their start and end apart: 1 -> 1, of which waited for: 1 -> 1; matrix products, arithmetic and copies ran while one was open for 0% -> 1% of each run, Pallas kernels for 0% -> 0%
where the time goes in v3:
time: 248 us; the launch traced here: 246 us
  blocking collectives  76 us (31%)
  local copies, waits for them, and re-layouts  65.2 us (26%)
  Pallas kernels  39.9 us (16%)
  other arithmetic  23.8 us (10%)
  waiting for transfers between devices  23.5 us (9%)
  starting transfers between devices  12.2 us (5%)
  matrix products  4.93 us (2%)
    all_to_all x1, blocking collectives, local(): own = jnp.sum(lax.all_to_all(packed, 'dev', 0, 0, tiled=True), 0)  59 us
    unnamed x25, local copies, waits for them, and re-layouts  27.3 us
    all_to_all x1, waiting for transfers between devices, local(): lax.all_to_all(copies, 'dev', 0, 0, tiled=True)  23.5 us
    pallas_call x1, Pallas kernels, local(): pl.pallas_call(spectra_kernel, grid=(steps,), in_specs=[table_spec, cross...  21.3 us
    pallas_call x1, Pallas kernels, local(): pl.pallas_call(functools.partial(norm_kernel, columns), grid=(steps,), in...  18.6 us
    all_gather x1, blocking collectives, local(): own = jnp.sum(lax.all_gather(own, 'grp', axis=0, tiled=False), 0)  17 us
    all_to_all x1, starting transfers between devices, local(): lax.all_to_all(copies, 'dev', 0, 0, tiled=True)  12.2 us
    concatenate x3, local copies, waits for them, and re-layouts, local(): jnp.concatenate([numer_all, cycles_all, mass_all[:, None], jnp.zeros((cla...  11.3 us
  transfers between devices with their start and end apart: 1, of which 1 were waited for; matrix products, arithmetic and copies ran while one was open for 1% of the time, Pallas kernels for 0%

profile of v3, /device:TPU:1, one launch (start us, length us, event | category | flops | bytes accessed | tf_op | source)
XLA Modules:
  0.0 246.3 jit_solution(14897528673877512725)
XLA Ops:
  0.6 0.0 copy-start
  0.6 0.0 copy-start.6
  0.7 0.0 copy-start.5
  0.7 0.0 copy-start.7
  0.7 1.9 broadcast_in_dim.18
  2.6 12.2 %all-to-all-start = ((bf16[32,6,2048]{2,1,0:T(8,128)(2,1)}), bf16[32,6,2048]{2,1,0:T(8,128)(2,1)}, u32[]{:S(2)}, u32[]{:S(2)}) async-start(bf16[32,6,2048]{2,1,0:T(8,128)(2,1)} %broadcast_in_dim.18), calls=%async_computation | async-start | bytes 2097152 | tf_op jit(solution)/shard_map/all_to_all | solution.py:110
  14.8 0.1 multiply_convert_fusion.1
  14.9 0.7 copy.80.table_ref
  15.7 0.1 fusion.25
  15.8 0.6 copy.79
  16.4 0.0 copy-done.6
  16.4 0.1 broadcast_bitcast_fusion.1
  16.5 0.9 copy.94
  17.4 0.0 copy-done
  17.4 0.0 copy-done.5
  17.4 0.0 copy-done.7
  17.4 0.2 broadcast_divide_fusion
  17.5 23.5 %all-to-all-done = bf16[32,6,2048]{2,1,0:T(8,128)(2,1)} async-done(((bf16[32,6,2048]{2,1,0:T(8,128)(2,1)}), bf16[32,6,2048]{2,1,0:T(8,128)(2,1)}, u32[]{:S(2)}, u32[]{:S(2)}) %all-to-all-start) | async-done | bytes 786464 | tf_op jit(solution)/shard_map/all_to_all | solution.py:110
  41.0 3.6 %reshape_reshape.3 = bf16[192,32,2,32]{3,2,1,0:T(2,128)(2,1)S(1)} reshape(bf16[32,6,2048]{2,1,0:T(8,128)(2,1)} %all-to-all-done) | data formatting | bytes 1572864 | tf_op jit(solution)/shard_map/reshape;reshape | solution.py:50
  44.6 11.0 %multiply_reduce_fusion = f32[192,32,32]{2,1,0:T(8,128)} fusion(bf16[192,32,2,32]{3,2,1,0:T(2,128)(2,1)S(1)} %reshape_reshape.3), kind=kLoop, calls=%fused_computation | loop fusion | flops 983040 | bytes 1572864 | tf_op jit(solution)/shard_map/reduce_sum | solution.py:58
  55.6 8.2 %fusion.29 = (bf16[192,32,1,32]{3,2,1,0:T(2,128)(2,1)}, bf16[192,32,1,32]{3,2,1,0:T(2,128)(2,1)}) fusion(bf16[192,32,2,32]{3,2,1,0:T(2,128)(2,1)S(1)} %reshape_reshape.3), kind=kLoop, calls=%fused_computation.55 | loop fusion | bytes 1572864 | tf_op jit(solution)/shard_map/slice | solution.py:52
  63.8 3.7 %copy.77 = f32[192,32,32]{0,2,1:T(8,128)} copy(f32[192,32,32]{2,1,0:T(8,128)} %multiply_reduce_fusion) | data formatting | bytes 1572864 | tf_op jit(solution)/shard_map/reduce_sum | solution.py:58
  67.5 0.0 copy-start.2
  67.5 1.5 multiply_reduce_fusion.1
  69.0 0.4 fusion.4
  69.4 0.9 copy.93
  70.3 7.6 %copy.89 = bf16[192,32,1,32]{0,3,1,2:T(8,128)(2,1)} copy(bf16[192,32,1,32]{3,2,1,0:T(2,128)(2,1)} %get-tuple-element.6) | data formatting | bytes 786432
  77.9 1.9 bitcast_negate_fusion
  79.8 0.0 copy-done.2
  79.8 5.2 %copy.88 = bf16[192,32,1,32]{0,3,1,2:T(8,128)(2,1)} copy(bf16[192,32,1,32]{3,2,1,0:T(2,128)(2,1)S(1)} %copy-done.2) | data formatting | bytes 786432
  85.0 2.1 maximum_bitcast_fusion
  87.1 0.0 copy-done.3
  87.1 1.9 convolution_convert_fusion
  89.0 6.6 %copy.92 = bf16[8,8,192,256]{3,1,2,0:T(8,128)(2,1)} copy(bf16[8,8,192,256]{3,2,1,0:T(8,128)(2,1)S(1)} %bitcast.71) | data formatting | bytes 12582912
  95.6 18.6 %shard_map.77 = f32[1,256]{1,0:T(1,128)} custom-call(bf16[128,64]{1,0:T(8,128)(2,1)} %copy.80.table_ref, bf16[64,49152]{1,0:T(8,128)(2,1)} %bitcast.69, f32[1,49152]{1,0:T(1,128)} %bitcast.80, f32[1,49152]{1,0:T(1,128)} %bitcast.78), custom_call_target="tpu_custom_call" | custom-call | tf_op jit(solution)/shard_map/pallas_call | solution.py:131
  114.2 0.7 broadcast_bitcast_fusion
  114.9 0.9 copy.95
  115.8 21.3 %shard_map.78 = (bf16[64,49152]{1,0:T(8,128)(2,1)}, f32[1,49152]{1,0:T(1,128)}) custom-call(bf16[128,64]{1,0:T(8,128)(2,1)} %copy.80.table_ref, bf16[64,49152]{1,0:T(8,128)(2,1)} %bitcast.70, f32[1,49152]{1,0:T(1,128)} %bitcast.81, f32[1,49152]{1,0:T(1,128)} %bitcast.79, f32[1,49152]{1,0:T(1,128)} %bitcast.83, bf16[64,128]{1,0:T(8,128)(2,1)} %bitcast.87), custom_call_target="tpu_custom_call" | custom-call | tf_op jit(solution)/shard_map/pallas_call | solution.py:141
  137.0 4.5 %copy.96 = bf16[8,8,192,256]{3,2,1,0:T(8,128)(2,1)S(1)} copy(bf16[8,8,192,256]{3,1,2,0:T(8,128)(2,1)} %bitcast.73) | data formatting | bytes 12582912
  141.5 2.2 convolution_bitcast_fusion
  143.6 0.1 fusion.6
  143.8 1.1 fusion.8
  144.9 0.5 broadcast.235
  145.4 0.0 copy-done.4
  145.4 1.1 reduce.8
  146.6 0.1 dot_general.24
  146.6 0.4 fusion.11
  147.0 0.1 copy.85
  147.1 0.1 reshape.241
  147.1 0.1 reduce_sum.47
  147.3 0.2 concatenate.19
  147.5 1.4 pad_maximum_fusion
  148.9 6.7 %copy.83 = f32[192,32,2,32]{3,2,1,0:T(2,128)} copy(f32[192,32,2,32]{0,3,1,2:T(8,128)S(1)} %pad_maximum_fusion) | data formatting | bytes 3145728 | tf_op jit(solution)/shard_map/stack | solution.py:166
  155.7 8.6 %concatenate.16 = f32[32,6,2048]{2,1,0:T(8,128)} reshape(f32[192,32,2,32]{3,2,1,0:T(2,128)} %copy.83) | data formatting | bytes 3145728 | tf_op jit(solution)/shard_map/concatenate | solution.py:172
  164.2 2.5 %concatenate.18 = f32[32,6,2176]{2,1,0:T(8,128)S(1)} concatenate(f32[32,6,2048]{2,1,0:T(8,128)} %concatenate.16, f32[32,6,32]{2,1,0:T(8,128)S(1)} %copy.85, f32[32,6,1]{2,1,0:T(8,128)S(1)} %concatenate.19, f32[32,6,95]{2,1,0:T(8,128)S(1)} %broadcast_in_dim.20), dimensions={2} | concatenate | bytes 3342336 | tf_op jit(solution)/shard_map/concatenate | solution.py:172
  166.8 0.0 copy-start.1
  166.8 59.0 %all_to_all.10 = f32[32,6,2176]{2,1,0:T(8,128)} all-to-all(f32[32,6,2176]{2,1,0:T(8,128)S(1)} %concatenate.18), channel_id=1, replica_groups=mesh['grp'=8,'dev'=32] {'dev'}, dimensions={0} | all-to-all | bytes 3342336 | tf_op jit(solution)/shard_map/all_to_all | solution.py:176
  225.8 1.8 reduce_sum.48
  227.5 17.0 %all-gather.1 = f32[8,6,2176]{2,1,0:T(8,128)S(1)} all-gather(f32[1,6,2176]{2,1,0:T(8,128)S(1)} %bitcast.86), channel_id=2, replica_groups=mesh['grp'=8,'dev'=32] {'grp'}, dimensions={0}, use_global_device_ids=true | all-gather | bytes 470016 | tf_op jit(solution)/shard_map/all_gather | solution.py:177
  244.6 0.7 fusion.27
  245.3 0.1 div.21
  245.4 0.2 div.22
  245.6 0.6 slice_divide_fusion
  246.3 0.0 copy-done.1
  (10 shorter events, 0.1 us)
Async XLA Ops:
  0.6 16.7 %copy-start = (f32[64,32]{0,1:T(8,128)S(1)}, f32[64,32]{0,1:T(8,128)}, u32[]{:S(2)}) copy-start(f32[64,32]{0,1:T(8,128)} %param.9) | copy-start | bytes 24580
  0.6 15.7 %copy-start.6 = (f32[192]{0:T(256)S(1)}, f32[192]{0:T(256)}, u32[]{:S(2)}) copy-start(f32[192]{0:T(256)} %param.11) | copy-start | bytes 2308
  0.7 16.7 %copy-start.5 = (f32[32]{0:T(128)S(1)}, f32[32]{0:T(128)}, u32[]{:S(2)}) copy-start(f32[32]{0:T(128)} %param.10) | copy-start | bytes 388
  0.7 16.7 %copy-start.7 = (s32[256]{0:T(256)S(1)}, s32[256]{0:T(256)}, u32[]{:S(2)}) copy-start(s32[256]{0:T(256)} %param.8) | copy-start | bytes 3076
  2.6 38.4 %all-to-all-start = ((bf16[32,6,2048]{2,1,0:T(8,128)(2,1)}), bf16[32,6,2048]{2,1,0:T(8,128)(2,1)}, u32[]{:S(2)}, u32[]{:S(2)}) async-start(bf16[32,6,2048]{2,1,0:T(8,128)(2,1)} %broadcast_in_dim.18), calls=%async_computation | async-start | bytes 2097152 | tf_op jit(solution)/shard_map/all_to_all | solution.py:110
  67.5 12.3 %copy-start.2 = (bf16[192,32,1,32]{3,2,1,0:T(2,128)(2,1)S(1)}, bf16[192,32,1,32]{3,2,1,0:T(2,128)(2,1)}, u32[]{:S(2)}) copy-start(bf16[192,32,1,32]{3,2,1,0:T(2,128)(2,1)} %get-tuple-element.7) | copy-start | bytes 1179652
  85.0 2.1 copy-start.3
  143.6 1.8 copy-start.4
  166.8 79.5 %copy-start.1 = (f32[64,32]{0,1:T(8,128)S(1)}, f32[64,32]{0,1:T(8,128)}, u32[]{:S(2)}) copy-start(f32[64,32]{0,1:T(8,128)} %param.9) | copy-start | bytes 24580

commit v4 on v3

--- a/solution.py
+++ b/solution.py
@@ -45,26 +45,15 @@
     return (weighted.reshape(freq_count, 2 * cycle_count, columns), power_term)
 
 
-def class_rows(class_block):
-    classes = class_block.shape[0]
-    class_grid = class_block.reshape(classes, M, 2, Q)
-    real_part = class_grid[:, :, 0, :]
-    imag_part = class_grid[:, :, 1, :]
-    rows_real = jnp.concatenate([real_part, imag_part], -1)
-    rows_imag = jnp.concatenate([-imag_part, real_part], -1)
-    stacked = jnp.stack([rows_real, rows_imag], 0)
-    factor = jnp.where(jnp.arange(M) == 0, 1.0, 2.0).astype(jnp.float32)
-    squares = class_grid.astype(jnp.float32) ** 2
-    cycle_power = jnp.sum(jnp.sum(squares, axis=2) * factor[None, :, None], axis=1)
-    return (stacked, cycle_power)
-
-
-def block_scores(table_ref, crossed_ref, half_ref, prior_ref):
-    raw = jnp.dot(table_ref[...], crossed_ref[...], preferred_element_type=jnp.float32)
+def block_scores(table_ref, real_ref, imag_ref, half_ref, prior_ref):
+    raw = jnp.dot(table_ref[0], real_ref[...], preferred_element_type=jnp.float32)
+    raw = raw + jnp.dot(table_ref[1], imag_ref[...], preferred_element_type=jnp.float32)
     return raw - half_ref[...] + prior_ref[...]
 
 
-def norm_kernel(cols, table_ref, crossed_ref, half_ref, prior_ref, out_ref, top_ref, total_ref):
+def norm_kernel(
+    cols, table_ref, real_ref, imag_ref, half_ref, prior_ref, out_ref, top_ref, total_ref
+):
     step = pl.program_id(0)
 
     @pl.when(step == 0)
@@ -72,7 +61,7 @@
         top_ref[...] = jnp.full(top_ref.shape, -1e30, jnp.float32)
         total_ref[...] = jnp.zeros(total_ref.shape, jnp.float32)
 
-    scores = block_scores(table_ref, crossed_ref, half_ref, prior_ref)
+    scores = block_scores(table_ref, real_ref, imag_ref, half_ref, prior_ref)
     parts = [scores[:, j * cols : (j + 1) * cols] for j in range(scores.shape[1] // cols)]
     block_top = functools.reduce(jnp.maximum, [jnp.max(s, axis=0, keepdims=True) for s in parts])
     old_top = top_ref[...]
@@ -89,9 +78,9 @@
 
 
 def spectra_kernel(
-    table_ref, crossed_ref, half_ref, prior_ref, norm_ref, turn_ref, spectra_ref, weight_ref
+    table_ref, real_ref, imag_ref, half_ref, prior_ref, norm_ref, turn_ref, spectra_ref, weight_ref
 ):
-    scores = block_scores(table_ref, crossed_ref, half_ref, prior_ref)
+    scores = block_scores(table_ref, real_ref, imag_ref, half_ref, prior_ref)
     responsibility = jnp.exp(scores - norm_ref[...]).astype(jnp.bfloat16)
     spectra_ref[...] = jnp.dot(
         turn_ref[...], responsibility, preferred_element_type=jnp.float32
@@ -106,37 +95,42 @@
     dev_count = lax.axis_size("dev")
     classes_total = CLS_DEV * dev_count
 
-    copies = jnp.broadcast_to(references[None], (dev_count,) + references.shape)
-    gathered = lax.all_to_all(copies, "dev", 0, 0, tiled=True).reshape(
-        dev_count * references.shape[0], references.shape[1]
-    )
-    stacked, cycle_power = class_rows(gathered)
-    crossed = jnp.einsum(
-        "pkmc,mcb->mpkb", stacked, weighted, preferred_element_type=jnp.float32
-    ).astype(jnp.bfloat16)
-    rows = 2 * M
+    own_rows = jnp.transpose(references.reshape(CLS_DEV, M, 2 * Q), (1, 0, 2))
+    copies = jnp.broadcast_to(own_rows[None], (dev_count,) + own_rows.shape)
+    gathered = lax.all_to_all(copies, "dev", 0, 0, tiled=True)
+    grid_rows = jnp.transpose(gathered, (1, 0, 2, 3)).reshape(M, classes_total, 2 * Q)
+    factor = jnp.where(jnp.arange(M) == 0, 1.0, 2.0).astype(jnp.float32)
+    squares = jnp.sum(grid_rows.astype(jnp.float32) ** 2 * factor[:, None, None], axis=0)
+    cycle_power = squares[:, :Q] + squares[:, Q:]
+    swapped = jnp.concatenate([weighted[:, Q:], -weighted[:, :Q]], 1)
+    rows = M
     width = classes_total * columns
-    crossed = crossed.reshape(rows, width)
+    crossed_real = jnp.einsum(
+        "mkc,mcb->mkb", grid_rows, weighted, preferred_element_type=jnp.float32
+    ).astype(jnp.bfloat16).reshape(rows, width)
+    crossed_imag = jnp.einsum(
+        "mkc,mcb->mkb", grid_rows, swapped, preferred_element_type=jnp.float32
+    ).astype(jnp.bfloat16).reshape(rows, width)
     penalty = jnp.dot(cycle_power, power_term, precision=lax.Precision.HIGHEST)
     half = (0.5 * penalty).reshape(1, width)
     prior = jnp.broadcast_to(class_prior[:, None], (classes_total, columns)).reshape(1, width)
-    table = jnp.transpose(score_table, (2, 1, 0)).reshape(R, rows)
-    turn = jnp.transpose(turn_table, (1, 0, 2)).reshape(rows, R)
+    table = jnp.transpose(score_table, (0, 2, 1))
+    turn = turn_table.reshape(2 * M, R)
 
     block = CLS_STEP * columns
     steps = width // block
-    table_spec = pl.BlockSpec((R, rows), lambda i: (0, 0))
+    table_spec = pl.BlockSpec((2, R, rows), lambda i: (0, 0, 0))
     crossed_spec = pl.BlockSpec((rows, block), lambda i: (0, i))
     row_spec = pl.BlockSpec((1, block), lambda i: (0, i))
     log_norm = pl.pallas_call(
         functools.partial(norm_kernel, columns),
         grid=(steps,),
-        in_specs=[table_spec, crossed_spec, row_spec, row_spec],
+        in_specs=[table_spec, crossed_spec, crossed_spec, row_spec, row_spec],
         out_specs=pl.BlockSpec((1, columns), lambda i: (0, 0)),
         out_shape=jax.ShapeDtypeStruct((1, columns), jnp.float32),
         scratch_shapes=[pltpu.VMEM((1, columns), jnp.float32)] * 2,
         compiler_params=pltpu.CompilerParams(dimension_semantics=("arbitrary",)),
-    )(table, crossed, half, prior)
+    )(table, crossed_real, crossed_imag, half, prior)
     norm_row = jnp.tile(log_norm, (1, classes_total))
     spectra, class_weight = pl.pallas_call(
         spectra_kernel,
@@ -144,26 +138,25 @@
         in_specs=[
             table_spec,
             crossed_spec,
+            crossed_spec,
             row_spec,
             row_spec,
             row_spec,
-            pl.BlockSpec((rows, R), lambda i: (0, 0)),
+            pl.BlockSpec((2 * rows, R), lambda i: (0, 0)),
         ],
-        out_specs=[crossed_spec, row_spec],
+        out_specs=[pl.BlockSpec((2 * rows, block), lambda i: (0, i)), row_spec],
         out_shape=[
-            jax.ShapeDtypeStruct((rows, width), jnp.bfloat16),
+            jax.ShapeDtypeStruct((2 * rows, width), jnp.bfloat16),
             jax.ShapeDtypeStruct((1, width), jnp.float32),
         ],
         compiler_params=pltpu.CompilerParams(dimension_semantics=("arbitrary",)),
-    )(table, crossed, half, prior, norm_row, turn)
+    )(table, crossed_real, crossed_imag, half, prior, norm_row, turn)
 
-    spectra = spectra.reshape(M, 2, classes_total, columns)
-    products = jnp.einsum(
-        "mpkb,mcb->kpmc", spectra, weighted, preferred_element_type=jnp.float32
-    )
-    real_sum = products[:, 0, :, :Q] + products[:, 1, :, Q:]
-    imag_sum = products[:, 0, :, Q:] - products[:, 1, :, :Q]
-    numer_all = jnp.stack([real_sum, imag_sum], 2).reshape(classes_total, 2 * M * Q)
+    spectra = spectra.reshape(2, M, classes_total, columns)
+    numer_all = jnp.einsum(
+        "mkb,mcb->kmc", spectra[0], weighted, preferred_element_type=jnp.float32
+    ) + jnp.einsum("mkb,mcb->kmc", spectra[1], swapped, preferred_element_type=jnp.float32)
+    numer_all = numer_all.reshape(classes_total, 2 * M * Q)
     class_weight = class_weight.reshape(classes_total, columns)
     cycles_all = jnp.dot(class_weight, power_term.T, precision=lax.Precision.HIGHEST)
     mass_all = jnp.sum(class_weight, axis=1)

time: 248 us -> 199 us (0.80)
  local copies, waits for them, and re-layouts: 65.2 us -> 33.1 us
  other arithmetic: 23.8 us -> 7.12 us
  waiting for transfers between devices: 23.5 us -> 17.2 us
  Pallas kernels: 39.9 us -> 44 us
  matrix products: 4.93 us -> 7.9 us
    reduce_sum x2 -> x1, other arithmetic: 12.5 us -> 0.77 us  [local(): jnp.sum(grid_rows.astype(jnp.float32) ** 2 * factor[:, None, None], axis=0)]
    unnamed x25 -> x28, local copies, waits for them, and re-layouts: 27.3 us -> 17 us
    another operation x2 -> x1, local copies, waits for them, and re-layouts: 10.4 us -> 0.74 us  [angle_tables(): jnp.stack([factor * cosine, factor * sine_part], 0).astype(jnp.bfloat16)]
    concatenate x3, local copies, waits for them, and re-layouts: 11.3 us -> 4.83 us  [local(): jnp.concatenate([numer_all, cycles_all, mass_all[:, None], jnp.zeros((cla...]
    all_to_all x1, waiting for transfers between devices: 23.5 us -> 17.2 us  [local(): gathered = lax.all_to_all(copies, 'dev', 0, 0, tiled=True)]
    slice x1, local copies, waits for them, and re-layouts: 8.24 us -> 3.25 us  [local(): spectra[1]]
    reduce_sum x1, local copies, waits for them, and re-layouts: 3.67 us -> 0.01 us  [local(): jnp.sum(grid_rows.astype(jnp.float32) ** 2 * factor[:, None, None], axis=0)]
    add x0 -> x1, local copies, waits for them, and re-layouts: none -> 3.17 us  [local(): jnp.einsum('mkb,mcb->kmc', spectra[0], weighted, preferred_element_type=j...]
  transfers between devices with their start and end apart: 1 -> 1, of which waited for: 1 -> 1; matrix products, arithmetic and copies ran while one was open for 1% -> 2% of each run, Pallas kernels for 0% -> 0%
where the time goes in v4:
time: 199 us; the launch traced here: 198 us
  blocking collectives  75.4 us (38%)
  Pallas kernels  44 us (22%)
  local copies, waits for them, and re-layouts  33.1 us (17%)
  waiting for transfers between devices  17.2 us (9%)
  starting transfers between devices  12.1 us (6%)
  matrix products  7.9 us (4%)
  other arithmetic  7.12 us (4%)
    all_to_all x1, blocking collectives, local(): own = jnp.sum(lax.all_to_all(packed, 'dev', 0, 0, tiled=True), 0)  58.2 us
    pallas_call x1, Pallas kernels, local(): pl.pallas_call(spectra_kernel, grid=(steps,), in_specs=[table_spec, cross...  23.4 us
    pallas_call x1, Pallas kernels, local(): pl.pallas_call(functools.partial(norm_kernel, columns), grid=(steps,), in...  20.6 us
    all_gather x1, blocking collectives, local(): own = jnp.sum(lax.all_gather(own, 'grp', axis=0, tiled=False), 0)  17.2 us
    all_to_all x1, waiting for transfers between devices, local(): gathered = lax.all_to_all(copies, 'dev', 0, 0, tiled=True)  17.2 us
    unnamed x28, local copies, waits for them, and re-layouts  17 us
    all_to_all x1, starting transfers between devices, local(): gathered = lax.all_to_all(copies, 'dev', 0, 0, tiled=True)  12.1 us
    concatenate x3, local copies, waits for them, and re-layouts, local(): jnp.concatenate([numer_all, cycles_all, mass_all[:, None], jnp.zeros((cla...  4.83 us
  transfers between devices with their start and end apart: 1, of which 1 were waited for; matrix products, arithmetic and copies ran while one was open for 2% of the time, Pallas kernels for 0%

profile of v4, /device:TPU:1, one launch (start us, length us, event | category | flops | bytes accessed | tf_op | source)
XLA Modules:
  0.0 197.7 jit_solution(8624437899862472304)
XLA Ops:
  0.6 0.0 copy-start
  0.6 0.0 copy-start.6
  0.7 0.9 reshape.208
  1.5 0.0 copy-start.5
  1.5 0.0 copy-start.7
  1.6 0.0 copy-start.3
  1.6 0.3 broadcast_bitcast_fusion.2
  1.9 1.9 reshape.235
  3.8 12.1 %all-to-all-start = ((bf16[32,2,6144]{2,1,0:T(2,128)(2,1)}), bf16[32,2,6144]{2,1,0:T(2,128)(2,1)}, u32[]{:S(2)}, u32[]{:S(2)}) async-start(bf16[32,2,6144]{2,1,0:T(2,128)(2,1)} %reshape.235), calls=%async_computation | async-start | bytes 1572864 | tf_op jit(solution)/shard_map/all_to_all | solution.py:100
  16.0 0.1 multiply_convert_fusion.1
  16.1 0.7 copy.19
  16.8 0.0 copy-done.6
  16.8 0.1 broadcast_bitcast_fusion.1
  16.9 0.9 copy.29
  17.8 0.1 fusion.17
  17.9 0.6 pad_maximum_fusion.4
  18.5 0.0 copy-done
  18.5 0.0 copy-done.5
  18.5 0.0 copy-done.7
  18.5 0.1 broadcast_divide_fusion
  18.7 0.0 copy-done.3
  18.7 0.3 fusion
  19.0 0.9 fusion.23
  19.9 17.2 %all-to-all-done = bf16[32,2,6144]{2,1,0:T(2,128)(2,1)} async-done(((bf16[32,2,6144]{2,1,0:T(2,128)(2,1)}), bf16[32,2,6144]{2,1,0:T(2,128)(2,1)}, u32[]{:S(2)}, u32[]{:S(2)}) %all-to-all-start) | async-done | bytes 786464 | tf_op jit(solution)/shard_map/all_to_all | solution.py:100
  37.0 3.0 %reshape.236 = bf16[32,6,32,64]{3,2,1,0:T(8,128)(2,1)S(1)} reshape(bf16[32,2,6144]{2,1,0:T(2,128)(2,1)} %all-to-all-done) | data formatting | bytes 1572864
  40.0 0.8 multiply_reduce_fusion
  40.8 2.2 %copy.20 = bf16[32,192,64]{1,2,0:T(8,128)(2,1)} copy(bf16[32,192,64]{2,0,1:T(8,128)(2,1)S(1)} %bitcast.57) | data formatting | bytes 1572864 | tf_op jit(solution)/shard_map/reshape | solution.py:101
  43.0 2.4 %convolution_convert_fusion.1 = bf16[32,256,192]{1,2,0:T(8,128)(2,1)S(1)} fusion(bf16[32,64,256]{2,1,0:T(8,128)(2,1)S(1)} %fusion, bf16[32,192,64]{1,2,0:T(8,128)(2,1)} %copy.20), kind=kOutput, calls=%fused_computation.2 | convolution fusion | flops 202899456 | bytes 4980736 | tf_op jit(solution)/shard_map/mkc,mcb->mkb/dot_general | solution.py:108
  45.3 0.0 copy-done.1
  45.3 0.0 copy-done.2
  45.4 1.0 convolution_convert_fusion
  46.4 3.4 %copy.27 = bf16[4,8,192,256]{3,1,2,0:T(8,128)(2,1)} copy(bf16[4,8,192,256]{3,2,1,0:T(8,128)(2,1)S(1)} %bitcast.60) | data formatting | bytes 6291456
  49.8 3.5 %copy.26 = bf16[4,8,192,256]{3,1,2,0:T(8,128)(2,1)} copy(bf16[4,8,192,256]{3,2,1,0:T(8,128)(2,1)S(1)} %bitcast.58) | data formatting | bytes 6291456
  53.3 0.4 fusion.1
  53.7 0.9 copy.28
  54.6 20.6 %shard_map.77 = f32[1,256]{1,0:T(1,128)} custom-call(bf16[2,128,32]{2,1,0:T(8,128)(2,1)} %bitcast.71, bf16[32,49152]{1,0:T(8,128)(2,1)} %bitcast.55, bf16[32,49152]{1,0:T(8,128)(2,1)} %bitcast.53, f32[1,49152]{1,0:T(1,128)} %bitcast.66, f32[1,49152]{1,0:T(1,128)} %bitcast.64), custom_call_target="tpu_custom_call" | custom-call | tf_op jit(solution)/shard_map/pallas_call | solution.py:125
  75.2 0.6 broadcast_bitcast_fusion
  75.8 0.9 copy.30
  76.7 23.4 %shard_map.78 = (bf16[64,49152]{1,0:T(8,128)(2,1)}, f32[1,49152]{1,0:T(1,128)}) custom-call(bf16[2,128,32]{2,1,0:T(8,128)(2,1)} %bitcast.72, bf16[32,49152]{1,0:T(8,128)(2,1)} %bitcast.56, bf16[32,49152]{1,0:T(8,128)(2,1)} %bitcast.54, f32[1,49152]{1,0:T(1,128)} %bitcast.67, f32[1,49152]{1,0:T(1,128)} %bitcast.65, f32[1,49152]{1,0:T(1,128)} %bitcast.70, ...), custom_call_target="tpu_custom_call" | custom-call | tf_op jit(solution)/shard_map/pallas_call | solution.py:135
  100.1 3.3 %fusion.22 = (bf16[32,49152]{1,0:T(8,128)(2,1)S(1)}, bf16[32,49152]{1,0:T(8,128)(2,1)S(1)}) fusion(bf16[64,49152]{1,0:T(8,128)(2,1)} %get-tuple-element.4), kind=kLoop, calls=%fused_computation.46 | loop fusion | bytes 12582912 | tf_op jit(solution)/shard_map/slice | solution.py:158
  103.4 0.7 copy.31
  104.2 1.1 fusion.24
  105.3 0.7 copy.32
  106.0 2.5 %add_bitcast_fusion = f32[192,32,64]{0,2,1:T(8,128)} fusion(f32[32,64,192]{2,1,0:T(8,128)S(1)} %fusion.24, bf16[32,192,256]{2,1,0:T(8,128)(2,1)S(1)} %bitcast.62, bf16[32,32,256]{2,1,0:T(8,128)(2,1)S(1)} %copy-done.2, bf16[32,32,256]{2,1,0:T(8,128)(2,1)S(1)} %get-tuple-element.8), kind=kOutput, calls=%fused_computation.5 | convolution fusion | flops 203816960 | bytes 7340032 | tf_op jit(solution)/shard_map/mkb,mcb->kmc/dot_general | solution.py:158
  108.5 3.2 %copy.22 = f32[192,32,64]{2,1,0:T(8,128)S(1)} copy(f32[192,32,64]{0,2,1:T(8,128)} %add_bitcast_fusion) | data formatting | bytes 3145728 | tf_op jit(solution)/shard_map/add | solution.py:156
  111.7 0.0 copy-start.4
  111.7 2.1 %concatenate.12 = f32[32,6,2048]{2,1,0:T(8,128)} reshape(f32[192,32,64]{2,1,0:T(8,128)S(1)} %copy.22) | data formatting | bytes 3145728 | tf_op jit(solution)/shard_map/concatenate | solution.py:165
  113.8 0.5 broadcast.236
  114.3 0.0 copy-done.4
  114.3 1.1 reduce.9
  115.4 0.1 dot_general.32
  115.5 0.4 fusion.2
  115.8 0.1 copy.24
  115.9 0.1 reshape.214
  116.0 0.1 reduce_sum.40
  116.1 0.2 concatenate.15
  116.3 2.5 %concatenate.14 = f32[32,6,2176]{2,1,0:T(8,128)S(1)} concatenate(f32[32,6,2048]{2,1,0:T(8,128)} %concatenate.12, f32[32,6,32]{2,1,0:T(8,128)S(1)} %copy.24, f32[32,6,1]{2,1,0:T(8,128)S(1)} %concatenate.15, f32[32,6,95]{2,1,0:T(8,128)S(1)} %broadcast_in_dim.20), dimensions={2} | concatenate | bytes 3342336 | tf_op jit(solution)/shard_map/concatenate | solution.py:165
  118.9 58.2 %all_to_all.10 = f32[32,6,2176]{2,1,0:T(8,128)} all-to-all(f32[32,6,2176]{2,1,0:T(8,128)S(1)} %concatenate.14), channel_id=1, replica_groups=mesh['grp'=8,'dev'=32] {'dev'}, dimensions={0} | all-to-all | bytes 3342336 | tf_op jit(solution)/shard_map/all_to_all | solution.py:169
  177.1 1.8 reduce_sum.41
  178.9 17.2 %all-gather.1 = f32[8,6,2176]{2,1,0:T(8,128)S(1)} all-gather(f32[1,6,2176]{2,1,0:T(8,128)S(1)} %bitcast.73), channel_id=2, replica_groups=mesh['grp'=8,'dev'=32] {'grp'}, dimensions={0}, use_global_device_ids=true | all-gather | bytes 470016 | tf_op jit(solution)/shard_map/all_gather | solution.py:170
  196.1 0.7 fusion.19
  196.8 0.1 div.21
  196.9 0.2 div.22
  197.1 0.6 slice_divide_fusion
  (9 shorter events, 0.1 us)
Async XLA Ops:
  0.6 17.9 %copy-start = (f32[64,32]{0,1:T(8,128)S(1)}, f32[64,32]{0,1:T(8,128)}, u32[]{:S(2)}) copy-start(f32[64,32]{0,1:T(8,128)} %param.9) | copy-start | bytes 24580
  0.6 16.2 %copy-start.6 = (f32[192]{0:T(256)S(1)}, f32[192]{0:T(256)}, u32[]{:S(2)}) copy-start(f32[192]{0:T(256)} %param.11) | copy-start | bytes 2308
  1.5 17.0 %copy-start.5 = (f32[32]{0:T(128)S(1)}, f32[32]{0:T(128)}, u32[]{:S(2)}) copy-start(f32[32]{0:T(128)} %param.10) | copy-start | bytes 388
  1.5 17.0 %copy-start.7 = (s32[256]{0:T(256)S(1)}, s32[256]{0:T(256)}, u32[]{:S(2)}) copy-start(s32[256]{0:T(256)} %param.8) | copy-start | bytes 3076
  1.6 17.1 %copy-start.3 = (bf16[2048,256]{1,0:T(8,128)(2,1)S(1)}, bf16[2048,256]{1,0:T(8,128)(2,1)}, u32[]{:S(2)}) copy-start(bf16[2048,256]{1,0:T(8,128)(2,1)} %param.7) | copy-start | bytes 3145732
  3.8 33.2 %all-to-all-start = ((bf16[32,2,6144]{2,1,0:T(2,128)(2,1)}), bf16[32,2,6144]{2,1,0:T(2,128)(2,1)}, u32[]{:S(2)}, u32[]{:S(2)}) async-start(bf16[32,2,6144]{2,1,0:T(2,128)(2,1)} %reshape.235), calls=%async_computation | async-start | bytes 1572864 | tf_op jit(solution)/shard_map/all_to_all | solution.py:100
  43.0 2.4 %copy-start.1 = (bf16[32,192,64]{1,2,0:T(8,128)(2,1)S(1)}, bf16[32,192,64]{1,2,0:T(8,128)(2,1)}, u32[]{:S(2)}) copy-start(bf16[32,192,64]{1,2,0:T(8,128)(2,1)} %copy.20) | copy-start | bytes 2359300
  43.0 2.4 %copy-start.2 = (bf16[32,32,256]{2,1,0:T(8,128)(2,1)S(1)}, bf16[32,32,256]{2,1,0:T(8,128)(2,1)}, u32[]{:S(2)}) copy-start(bf16[32,32,256]{2,1,0:T(8,128)(2,1)} %get-tuple-element.9) | copy-start | bytes 1572868
  111.7 2.6 %copy-start.4 = (f32[1,49152]{1,0:T(1,128)S(1)}, f32[1,49152]{1,0:T(1,128)}, u32[]{:S(2)}) copy-start(f32[1,49152]{1,0:T(1,128)} %get-tuple-element.5) | copy-start | bytes 589828

commit v5 on v4

--- a/solution.py
+++ b/solution.py
@@ -13,6 +13,8 @@
 R = 128
 CLS_DEV = 6
 CLS_STEP = 8
+GRP = ("x", "core")
+DEV = ("z", "y")
 
 
 def angle_tables(cycle_freqs, count_turns):
@@ -92,12 +94,12 @@
     weighted, power_term = particle_terms(particles, defocus_bin, contrast_table, noise_power)
     score_table, turn_table = angle_tables(M, R)
     columns = particles.shape[1]
-    dev_count = lax.axis_size("dev")
+    dev_count = lax.axis_size(DEV)
     classes_total = CLS_DEV * dev_count
 
     own_rows = jnp.transpose(references.reshape(CLS_DEV, M, 2 * Q), (1, 0, 2))
     copies = jnp.broadcast_to(own_rows[None], (dev_count,) + own_rows.shape)
-    gathered = lax.all_to_all(copies, "dev", 0, 0, tiled=True)
+    gathered = lax.all_to_all(copies, DEV, 0, 0, tiled=True)
     grid_rows = jnp.transpose(gathered, (1, 0, 2, 3)).reshape(M, classes_total, 2 * Q)
     factor = jnp.where(jnp.arange(M) == 0, 1.0, 2.0).astype(jnp.float32)
     squares = jnp.sum(grid_rows.astype(jnp.float32) ** 2 * factor[:, None, None], axis=0)
@@ -165,25 +167,35 @@
     packed = jnp.concatenate(
         [numer_all, cycles_all, mass_all[:, None], jnp.zeros((classes_total, 95), jnp.float32)], 1
     )
-    packed = packed.reshape(dev_count, CLS_DEV, packed.shape[1])
-    own = jnp.sum(lax.all_to_all(packed, "dev", 0, 0, tiled=True), 0)
-    own = jnp.sum(lax.all_gather(own, "grp", axis=0, tiled=False), 0)
+    packed = packed.reshape(lax.axis_size("z"), lax.axis_size("y"), CLS_DEV, packed.shape[1])
+    own = jnp.sum(lax.all_to_all(packed, "y", 1, 1, tiled=True), 1)
+    own = jnp.sum(lax.all_to_all(own, "z", 0, 0, tiled=True), 0)
+    own = jnp.sum(lax.all_gather(own, GRP, axis=0, tiled=False), 0)
     numerator = own[:, :width]
     cycle_sum = own[:, width : width + Q]
     class_mass = own[:, width + Q]
     new_references = (numerator.reshape(CLS_DEV, M, 2, Q) / cycle_sum[:, None, None, :]).reshape(
         CLS_DEV, 2 * M * Q
     )
-    particle_total = columns * lax.axis_size("grp") * lax.axis_size("dev")
+    particle_total = columns * lax.axis_size(GRP) * lax.axis_size(DEV)
     occupancy = class_mass * (classes_total / particle_total)
     return (new_references, occupancy)
 
 
 def solution(mesh):
+    grp_count, dev_count = mesh.devices.shape
+    core_count = 2
+    y_count = 4
+    split = jax.sharding.Mesh(
+        mesh.devices.reshape(
+            grp_count // core_count, core_count, dev_count // y_count, y_count
+        ),
+        GRP + DEV,
+    )
     return jax.shard_map(
         local,
-        mesh=mesh,
-        in_specs=(P("dev", None), P(None, ("grp", "dev")), P(("grp", "dev")), P(), P(), P()),
-        out_specs=(P("dev", None), P("dev")),
+        mesh=split,
+        in_specs=(P(DEV, None), P(None, GRP + DEV), P(GRP + DEV), P(), P(), P()),
+        out_specs=(P(DEV, None), P(DEV)),
         check_vma=False,
     )

time: 199 us -> 182 us (0.915)
  blocking collectives: 75.4 us -> 59.3 us
    all_to_all x1 -> x2, blocking collectives: 58.2 us -> 41.8 us  [the longest x1 22.8 us: local(): own = jnp.sum(lax.all_to_all(packed, 'y', 1, 1, tiled=True), 1)]
    concatenate x3 -> x4, local copies, waits for them, and re-layouts: 4.83 us -> 5.8 us  [local(): jnp.concatenate([numer_all, cycles_all, mass_all[:, None], jnp.zeros((cla...]
where the time goes in v5:
time: 182 us; the launch traced here: 181 us
  blocking collectives  59.3 us (33%)
  Pallas kernels  44 us (24%)
  local copies, waits for them, and re-layouts  34.1 us (19%)
  waiting for transfers between devices  17.2 us (9%)
  starting transfers between devices  12.1 us (7%)
  matrix products  7.95 us (4%)
  other arithmetic  5.48 us (3%)
    pallas_call x1, Pallas kernels, local(): pl.pallas_call(spectra_kernel, grid=(steps,), in_specs=[table_spec, cross...  23.4 us
    all_to_all x1, blocking collectives, local(): own = jnp.sum(lax.all_to_all(packed, 'y', 1, 1, tiled=True), 1)  22.8 us
    pallas_call x1, Pallas kernels, local(): pl.pallas_call(functools.partial(norm_kernel, columns), grid=(steps,), in...  20.6 us
    all_to_all x1, blocking collectives, local(): own = jnp.sum(lax.all_to_all(own, 'z', 0, 0, tiled=True), 0)  19 us
    all_gather x1, blocking collectives, local(): own = jnp.sum(lax.all_gather(own, GRP, axis=0, tiled=False), 0)  17.5 us
    all_to_all x1, waiting for transfers between devices, local(): gathered = lax.all_to_all(copies, DEV, 0, 0, tiled=True)  17.2 us
    unnamed x28, local copies, waits for them, and re-layouts  17 us
    all_to_all x1, starting transfers between devices, local(): gathered = lax.all_to_all(copies, DEV, 0, 0, tiled=True)  12.1 us
  transfers between devices with their start and end apart: 1, of which 1 were waited for; matrix products, arithmetic and copies ran while one was open for 2% of the time, Pallas kernels for 0%

profile of v5, /device:TPU:1, one launch (start us, length us, event | category | flops | bytes accessed | tf_op | source)
XLA Modules:
  0.0 181.1 jit_solution(16523471305054934082)
XLA Ops:
  0.6 0.0 copy-start
  0.6 0.0 copy-start.6
  0.7 0.9 reshape.208
  1.5 0.0 copy-start.7
  1.6 0.0 copy-start.3
  1.6 0.3 broadcast_bitcast_fusion.2
  1.9 1.9 %reshape.235 = bf16[32,2,6144]{2,1,0:T(2,128)(2,1)} reshape(bf16[32,6,32,64]{3,2,1,0:T(8,128)(2,1)S(1)} %broadcast_bitcast_fusion.2) | data formatting | bytes 1572864
  3.8 12.1 %all-to-all-start = ((bf16[32,2,6144]{2,1,0:T(2,128)(2,1)}), bf16[32,2,6144]{2,1,0:T(2,128)(2,1)}, u32[]{:S(2)}, u32[]{:S(2)}) async-start(bf16[32,2,6144]{2,1,0:T(2,128)(2,1)} %reshape.235), calls=%async_computation | async-start | bytes 1572864 | tf_op jit(solution)/shard_map/all_to_all | solution.py:102
  16.0 0.1 multiply_convert_fusion.1
  16.1 0.7 copy.31
  16.8 0.0 copy-done.6
  16.8 0.1 broadcast_bitcast_fusion.1
  16.9 0.9 copy.42
  17.8 0.1 fusion.16
  17.9 0.6 pad_maximum_fusion.4
  18.5 0.0 copy-done
  18.5 0.0 copy-done.5
  18.5 0.0 copy-done.7
  18.5 0.1 broadcast_divide_fusion
  18.7 0.0 copy-done.3
  18.7 0.3 fusion
  19.0 0.9 fusion.22
  19.9 17.2 %all-to-all-done = bf16[32,2,6144]{2,1,0:T(2,128)(2,1)} async-done(((bf16[32,2,6144]{2,1,0:T(2,128)(2,1)}), bf16[32,2,6144]{2,1,0:T(2,128)(2,1)}, u32[]{:S(2)}, u32[]{:S(2)}) %all-to-all-start) | async-done | bytes 786464 | tf_op jit(solution)/shard_map/all_to_all | solution.py:102
  37.0 3.0 %reshape.236 = bf16[32,6,32,64]{3,2,1,0:T(8,128)(2,1)S(1)} reshape(bf16[32,2,6144]{2,1,0:T(2,128)(2,1)} %all-to-all-done) | data formatting | bytes 1572864
  40.0 0.8 multiply_reduce_fusion
  40.8 2.2 %copy.32 = bf16[32,192,64]{1,2,0:T(8,128)(2,1)} copy(bf16[32,192,64]{2,0,1:T(8,128)(2,1)S(1)} %bitcast.60) | data formatting | bytes 1572864 | tf_op jit(solution)/shard_map/reshape | solution.py:103
  43.0 2.4 %convolution_convert_fusion.1 = bf16[32,256,192]{1,2,0:T(8,128)(2,1)S(1)} fusion(bf16[32,64,256]{2,1,0:T(8,128)(2,1)S(1)} %fusion, bf16[32,192,64]{1,2,0:T(8,128)(2,1)} %copy.32), kind=kOutput, calls=%fused_computation.2 | convolution fusion | flops 202899456 | bytes 4980736 | tf_op jit(solution)/shard_map/mkc,mcb->mkb/dot_general | solution.py:110
  45.3 0.0 copy-done.1
  45.3 0.0 copy-done.2
  45.4 1.0 convolution_convert_fusion
  46.4 3.4 %copy.40 = bf16[4,8,192,256]{3,1,2,0:T(8,128)(2,1)} copy(bf16[4,8,192,256]{3,2,1,0:T(8,128)(2,1)S(1)} %bitcast.63) | data formatting | bytes 6291456
  49.8 3.5 %copy.39 = bf16[4,8,192,256]{3,1,2,0:T(8,128)(2,1)} copy(bf16[4,8,192,256]{3,2,1,0:T(8,128)(2,1)S(1)} %bitcast.61) | data formatting | bytes 6291456
  53.3 0.4 fusion.1
  53.7 0.9 copy.41
  54.6 20.6 %shard_map.77 = f32[1,256]{1,0:T(1,128)} custom-call(bf16[2,128,32]{2,1,0:T(8,128)(2,1)} %bitcast.74, bf16[32,49152]{1,0:T(8,128)(2,1)} %bitcast.58, bf16[32,49152]{1,0:T(8,128)(2,1)} %bitcast.56, f32[1,49152]{1,0:T(1,128)} %bitcast.69, f32[1,49152]{1,0:T(1,128)} %bitcast.67), custom_call_target="tpu_custom_call" | custom-call | tf_op jit(solution)/shard_map/pallas_call | solution.py:127
  75.2 0.6 broadcast_bitcast_fusion
  75.8 0.9 copy.43
  76.7 23.4 %shard_map.78 = (bf16[64,49152]{1,0:T(8,128)(2,1)}, f32[1,49152]{1,0:T(1,128)}) custom-call(bf16[2,128,32]{2,1,0:T(8,128)(2,1)} %bitcast.75, bf16[32,49152]{1,0:T(8,128)(2,1)} %bitcast.59, bf16[32,49152]{1,0:T(8,128)(2,1)} %bitcast.57, f32[1,49152]{1,0:T(1,128)} %bitcast.70, f32[1,49152]{1,0:T(1,128)} %bitcast.68, f32[1,49152]{1,0:T(1,128)} %bitcast.73, ...), custom_call_target="tpu_custom_call" | custom-call | tf_op jit(solution)/shard_map/pallas_call | solution.py:137
  100.1 3.3 %fusion.21 = (bf16[32,49152]{1,0:T(8,128)(2,1)S(1)}, bf16[32,49152]{1,0:T(8,128)(2,1)S(1)}) fusion(bf16[64,49152]{1,0:T(8,128)(2,1)} %get-tuple-element.4), kind=kLoop, calls=%fused_computation.45 | loop fusion | bytes 12582912 | tf_op jit(solution)/shard_map/slice | solution.py:160
  103.4 0.7 copy.44
  104.2 1.1 fusion.23
  105.3 0.7 copy.45
  106.0 2.5 %add_bitcast_fusion = f32[192,32,64]{0,2,1:T(8,128)} fusion(f32[32,64,192]{2,1,0:T(8,128)S(1)} %fusion.23, bf16[32,192,256]{2,1,0:T(8,128)(2,1)S(1)} %bitcast.65, bf16[32,32,256]{2,1,0:T(8,128)(2,1)S(1)} %copy-done.2, bf16[32,32,256]{2,1,0:T(8,128)(2,1)S(1)} %get-tuple-element.8), kind=kOutput, calls=%fused_computation.5 | convolution fusion | flops 203816960 | bytes 7340032 | tf_op jit(solution)/shard_map/mkb,mcb->kmc/dot_general | solution.py:160
  108.5 3.2 %copy.34 = f32[192,32,64]{2,1,0:T(8,128)S(1)} copy(f32[192,32,64]{0,2,1:T(8,128)} %add_bitcast_fusion) | data formatting | bytes 3145728 | tf_op jit(solution)/shard_map/add | solution.py:158
  111.7 2.1 %concatenate.12 = f32[8,4,6,2048]{3,2,1,0:T(8,128)} reshape(f32[192,32,64]{2,1,0:T(8,128)S(1)} %copy.34) | data formatting | bytes 3145728 | tf_op jit(solution)/shard_map/concatenate | solution.py:167
  113.8 0.5 broadcast.236
  114.3 0.0 copy-done.4
  114.3 1.1 reduce.9
  115.4 0.1 dot_general.32
  115.5 0.4 fusion.3
  115.9 0.1 reshape.214
  116.0 0.1 reduce_sum.49
  116.1 0.2 concatenate.15
  116.3 2.5 %concatenate.14 = f32[8,4,6,2176]{3,2,1,0:T(8,128)S(1)} concatenate(f32[8,4,6,2048]{3,2,1,0:T(8,128)} %concatenate.12, f32[8,4,6,32]{3,2,1,0:T(8,128)S(1)} %fusion.3, f32[8,4,6,1]{3,2,1,0:T(8,128)S(1)} %concatenate.15, f32[8,4,6,95]{3,2,1,0:T(8,128)S(1)} %broadcast_in_dim.20), dimensions={3} | concatenate | bytes 3342336 | tf_op jit(solution)/shard_map/concatenate | solution.py:167
  118.9 1.0 copy.36
  119.8 22.8 %all_to_all.15 = f32[8,4,6,2176]{3,0,2,1:T(8,128)S(1)} all-to-all(f32[8,4,6,2176]{3,0,2,1:T(8,128)S(1)} %copy.36), channel_id=1, replica_groups=mesh['x'=4,'core'=2,'z'=8,'y'=4] {'y'}, dimensions={1} | all-to-all | bytes 3342336 | tf_op jit(solution)/shard_map/all_to_all | solution.py:171
  142.6 0.1 reduce_sum.50
  142.7 0.1 copy.37
  142.9 19.0 %all_to_all.16 = f32[8,6,2176]{2,1,0:T(8,128)S(1)} all-to-all(f32[8,6,2176]{2,1,0:T(8,128)S(1)} %copy.37), channel_id=1, replica_groups=mesh['x'=4,'core'=2,'z'=8,'y'=4] {'z'}, dimensions={0} | all-to-all | bytes 835584 | tf_op jit(solution)/shard_map/all_to_all | solution.py:172
  161.9 17.5 %all-gather.1 = f32[8,6,2176]{2,1,0:T(8,128)S(1)} all-gather(f32[1,6,2176]{2,1,0:T(8,128)S(1)} %bitcast.76), channel_id=2, replica_groups=mesh['x'=4,'core'=2,'z'=8,'y'=4] {'x','core'}, dimensions={0}, use_global_device_ids=true | all-gather | bytes 470016 | tf_op jit(solution)/shard_map/all_gather | solution.py:173
  179.4 0.7 fusion.18
  180.1 0.1 div.21
  180.2 0.2 div.22
  180.4 0.6 slice_divide_fusion
  (12 shorter events, 0.1 us)
Async XLA Ops:
  0.6 17.9 %copy-start = (f32[64,32]{0,1:T(8,128)S(1)}, f32[64,32]{0,1:T(8,128)}, u32[]{:S(2)}) copy-start(f32[64,32]{0,1:T(8,128)} %param.9) | copy-start | bytes 24580
  0.6 16.2 %copy-start.6 = (f32[192]{0:T(256)S(1)}, f32[192]{0:T(256)}, u32[]{:S(2)}) copy-start(f32[192]{0:T(256)} %param.11) | copy-start | bytes 2308
  1.5 17.0 %copy-start.5 = (f32[32]{0:T(128)S(1)}, f32[32]{0:T(128)}, u32[]{:S(2)}) copy-start(f32[32]{0:T(128)} %param.10) | copy-start | bytes 388
  1.5 17.0 %copy-start.7 = (s32[256]{0:T(256)S(1)}, s32[256]{0:T(256)}, u32[]{:S(2)}) copy-start(s32[256]{0:T(256)} %param.8) | copy-start | bytes 3076
  1.6 17.1 %copy-start.3 = (bf16[2048,256]{1,0:T(8,128)(2,1)S(1)}, bf16[2048,256]{1,0:T(8,128)(2,1)}, u32[]{:S(2)}) copy-start(bf16[2048,256]{1,0:T(8,128)(2,1)} %param.7) | copy-start | bytes 3145732
  3.8 33.2 %all-to-all-start = ((bf16[32,2,6144]{2,1,0:T(2,128)(2,1)}), bf16[32,2,6144]{2,1,0:T(2,128)(2,1)}, u32[]{:S(2)}, u32[]{:S(2)}) async-start(bf16[32,2,6144]{2,1,0:T(2,128)(2,1)} %reshape.235), calls=%async_computation | async-start | bytes 1572864 | tf_op jit(solution)/shard_map/all_to_all | solution.py:102
  43.0 2.4 %copy-start.1 = (bf16[32,192,64]{1,2,0:T(8,128)(2,1)S(1)}, bf16[32,192,64]{1,2,0:T(8,128)(2,1)}, u32[]{:S(2)}) copy-start(bf16[32,192,64]{1,2,0:T(8,128)(2,1)} %copy.32) | copy-start | bytes 2359300
  43.0 2.4 %copy-start.2 = (bf16[32,32,256]{2,1,0:T(8,128)(2,1)S(1)}, bf16[32,32,256]{2,1,0:T(8,128)(2,1)}, u32[]{:S(2)}) copy-start(bf16[32,32,256]{2,1,0:T(8,128)(2,1)} %get-tuple-element.9) | copy-start | bytes 1572868
  111.7 2.6 %copy-start.4 = (f32[1,49152]{1,0:T(1,128)S(1)}, f32[1,49152]{1,0:T(1,128)}, u32[]{:S(2)}) copy-start(f32[1,49152]{1,0:T(1,128)} %get-tuple-element.5) | copy-start | bytes 589828

commit v6 on v5

--- a/solution.py
+++ b/solution.py
@@ -12,7 +12,7 @@
 M = 32
 R = 128
 CLS_DEV = 6
-CLS_STEP = 8
+CLS_STEP = 24
 GRP = ("x", "core")
 DEV = ("z", "y")
 
@@ -47,15 +47,13 @@
     return (weighted.reshape(freq_count, 2 * cycle_count, columns), power_term)
 
 
-def block_scores(table_ref, real_ref, imag_ref, half_ref, prior_ref):
-    raw = jnp.dot(table_ref[0], real_ref[...], preferred_element_type=jnp.float32)
-    raw = raw + jnp.dot(table_ref[1], imag_ref[...], preferred_element_type=jnp.float32)
-    return raw - half_ref[...] + prior_ref[...]
+def block_scores(table_ref, real_ref, imag_ref, shift_ref):
+    crossed = jnp.concatenate([real_ref[...], imag_ref[...]], 0)
+    raw = jnp.dot(table_ref[...], crossed, preferred_element_type=jnp.float32)
+    return raw + shift_ref[...]
 
 
-def norm_kernel(
-    cols, table_ref, real_ref, imag_ref, half_ref, prior_ref, out_ref, top_ref, total_ref
-):
+def norm_kernel(cols, table_ref, real_ref, imag_ref, bias_ref, out_ref, top_ref, total_ref):
     step = pl.program_id(0)
 
     @pl.when(step == 0)
@@ -63,7 +61,7 @@
         top_ref[...] = jnp.full(top_ref.shape, -1e30, jnp.float32)
         total_ref[...] = jnp.zeros(total_ref.shape, jnp.float32)
 
-    scores = block_scores(table_ref, real_ref, imag_ref, half_ref, prior_ref)
+    scores = block_scores(table_ref, real_ref, imag_ref, bias_ref)
     parts = [scores[:, j * cols : (j + 1) * cols] for j in range(scores.shape[1] // cols)]
     block_top = functools.reduce(jnp.maximum, [jnp.max(s, axis=0, keepdims=True) for s in parts])
     old_top = top_ref[...]
@@ -79,15 +77,14 @@
         out_ref[...] = top_ref[...] + jnp.log(total_ref[...])
 
 
-def spectra_kernel(
-    table_ref, real_ref, imag_ref, half_ref, prior_ref, norm_ref, turn_ref, spectra_ref, weight_ref
-):
-    scores = block_scores(table_ref, real_ref, imag_ref, half_ref, prior_ref)
-    responsibility = jnp.exp(scores - norm_ref[...]).astype(jnp.bfloat16)
-    spectra_ref[...] = jnp.dot(
-        turn_ref[...], responsibility, preferred_element_type=jnp.float32
-    ).astype(jnp.bfloat16)
-    weight_ref[...] = jnp.sum(responsibility.astype(jnp.float32), axis=0, keepdims=True)
+def spectra_kernel(table_ref, real_ref, imag_ref, shift_ref, turn_ref, spectra_ref, weight_ref):
+    responsibility = jnp.exp(block_scores(table_ref, real_ref, imag_ref, shift_ref))
+    full = jnp.dot(
+        turn_ref[...], responsibility.astype(jnp.bfloat16), preferred_element_type=jnp.float32
+    )
+    rows = spectra_ref.shape[0]
+    spectra_ref[...] = full[:rows].astype(jnp.bfloat16)
+    weight_ref[...] = full[rows : rows + 1]
 
 
 def local(references, particles, defocus_bin, contrast_table, noise_power, class_prior):
@@ -114,26 +111,27 @@
         "mkc,mcb->mkb", grid_rows, swapped, preferred_element_type=jnp.float32
     ).astype(jnp.bfloat16).reshape(rows, width)
     penalty = jnp.dot(cycle_power, power_term, precision=lax.Precision.HIGHEST)
-    half = (0.5 * penalty).reshape(1, width)
-    prior = jnp.broadcast_to(class_prior[:, None], (classes_total, columns)).reshape(1, width)
-    table = jnp.transpose(score_table, (0, 2, 1))
-    turn = turn_table.reshape(2 * M, R)
+    bias = (class_prior[:, None] - 0.5 * penalty).reshape(1, width)
+    table = jnp.transpose(score_table, (2, 0, 1)).reshape(R, 2 * M)
+    turn = jnp.concatenate(
+        [turn_table.reshape(2 * M, R), jnp.ones((1, R), jnp.bfloat16), jnp.zeros((15, R), jnp.bfloat16)], 0
+    )
 
     block = CLS_STEP * columns
     steps = width // block
-    table_spec = pl.BlockSpec((2, R, rows), lambda i: (0, 0, 0))
+    table_spec = pl.BlockSpec((R, 2 * rows), lambda i: (0, 0))
     crossed_spec = pl.BlockSpec((rows, block), lambda i: (0, i))
     row_spec = pl.BlockSpec((1, block), lambda i: (0, i))
     log_norm = pl.pallas_call(
         functools.partial(norm_kernel, columns),
         grid=(steps,),
-        in_specs=[table_spec, crossed_spec, crossed_spec, row_spec, row_spec],
+        in_specs=[table_spec, crossed_spec, crossed_spec, row_spec],
         out_specs=pl.BlockSpec((1, columns), lambda i: (0, 0)),
         out_shape=jax.ShapeDtypeStruct((1, columns), jnp.float32),
         scratch_shapes=[pltpu.VMEM((1, columns), jnp.float32)] * 2,
         compiler_params=pltpu.CompilerParams(dimension_semantics=("arbitrary",)),
-    )(table, crossed_real, crossed_imag, half, prior)
-    norm_row = jnp.tile(log_norm, (1, classes_total))
+    )(table, crossed_real, crossed_imag, bias)
+    shift = bias - jnp.tile(log_norm, (1, classes_total))
     spectra, class_weight = pl.pallas_call(
         spectra_kernel,
         grid=(steps,),
@@ -142,9 +140,7 @@
             crossed_spec,
             crossed_spec,
             row_spec,
-            row_spec,
-            row_spec,
-            pl.BlockSpec((2 * rows, R), lambda i: (0, 0)),
+            pl.BlockSpec(turn.shape, lambda i: (0, 0)),
         ],
         out_specs=[pl.BlockSpec((2 * rows, block), lambda i: (0, i)), row_spec],
         out_shape=[
@@ -152,7 +148,7 @@
             jax.ShapeDtypeStruct((1, width), jnp.float32),
         ],
         compiler_params=pltpu.CompilerParams(dimension_semantics=("arbitrary",)),
-    )(table, crossed_real, crossed_imag, half, prior, norm_row, turn)
+    )(table, crossed_real, crossed_imag, shift, turn)
 
     spectra = spectra.reshape(2, M, classes_total, columns)
     numer_all = jnp.einsum(

time: 182 us -> 160 us (0.88)
  Pallas kernels: 44 us -> 21.4 us
    pallas_call x1, Pallas kernels: 23.4 us -> 10.6 us  [local(): pl.pallas_call(spectra_kernel, grid=(steps,), in_specs=[table_spec, cross...]
    pallas_call x1, Pallas kernels: 20.6 us -> 10.8 us  [local(): pl.pallas_call(functools.partial(norm_kernel, columns), grid=(steps,), in...]
where the time goes in v6:
time: 160 us; the launch traced here: 159 us
  blocking collectives  59.3 us (37%)
  local copies, waits for them, and re-layouts  32.7 us (20%)
  Pallas kernels  21.4 us (13%)
  waiting for transfers between devices  17.9 us (11%)
  starting transfers between devices  12.1 us (8%)
  matrix products  7.95 us (5%)
  other arithmetic  6.45 us (4%)
    all_to_all x1, blocking collectives, local(): own = jnp.sum(lax.all_to_all(packed, 'y', 1, 1, tiled=True), 1)  22.8 us
    all_to_all x1, blocking collectives, local(): own = jnp.sum(lax.all_to_all(own, 'z', 0, 0, tiled=True), 0)  19 us
    all_to_all x1, waiting for transfers between devices, local(): gathered = lax.all_to_all(copies, DEV, 0, 0, tiled=True)  17.9 us
    all_gather x1, blocking collectives, local(): own = jnp.sum(lax.all_gather(own, GRP, axis=0, tiled=False), 0)  17.5 us
    unnamed x28, local copies, waits for them, and re-layouts  15.4 us
    all_to_all x1, starting transfers between devices, local(): gathered = lax.all_to_all(copies, DEV, 0, 0, tiled=True)  12.1 us
    pallas_call x1, Pallas kernels, local(): pl.pallas_call(functools.partial(norm_kernel, columns), grid=(steps,), in...  10.8 us
    pallas_call x1, Pallas kernels, local(): pl.pallas_call(spectra_kernel, grid=(steps,), in_specs=[table_spec, cross...  10.6 us
  transfers between devices with their start and end apart: 1, of which 1 were waited for; matrix products, arithmetic and copies ran while one was open for 2% of the time, Pallas kernels for 0%

profile of v6, /device:TPU:1, one launch (start us, length us, event | category | flops | bytes accessed | tf_op | source)
XLA Modules:
  0.0 158.8 jit_solution(7831476175989734366)
XLA Ops:
  0.6 0.0 copy-start
  0.6 0.0 copy-start.6
  0.7 0.0 copy-start.8
  0.7 0.0 copy-start.4
  0.7 1.0 reshape.229
  1.6 0.3 broadcast_bitcast_fusion.1
  2.0 1.9 %reshape.256 = bf16[32,2,6144]{2,1,0:T(2,128)(2,1)} reshape(bf16[32,6,32,64]{3,2,1,0:T(8,128)(2,1)S(1)} %broadcast_bitcast_fusion.1) | data formatting | bytes 1572864
  3.9 12.1 %all-to-all-start = ((bf16[32,2,6144]{2,1,0:T(2,128)(2,1)}), bf16[32,2,6144]{2,1,0:T(2,128)(2,1)}, u32[]{:S(2)}, u32[]{:S(2)}) async-start(bf16[32,2,6144]{2,1,0:T(2,128)(2,1)} %reshape.256), calls=%async_computation | async-start | bytes 1572864 | tf_op jit(solution)/shard_map/all_to_all | solution.py:99
  16.0 0.1 multiply_convert_fusion.1
  16.1 0.7 copy.37.table_ref
  16.9 0.1 pad.2.clone
  17.0 0.1 pad.1.clone
  17.0 0.1 fusion.17
  17.1 0.7 maximum_maximum_fusion.turn_ref
  17.8 0.0 copy-done
  17.8 0.0 copy-done.6
  17.8 0.0 copy-done.8
  17.8 0.1 broadcast_divide_fusion
  18.0 0.0 copy-done.4
  18.0 0.3 fusion
  18.3 0.9 fusion.23
  19.2 17.9 %all-to-all-done = bf16[32,2,6144]{2,1,0:T(2,128)(2,1)} async-done(((bf16[32,2,6144]{2,1,0:T(2,128)(2,1)}), bf16[32,2,6144]{2,1,0:T(2,128)(2,1)}, u32[]{:S(2)}, u32[]{:S(2)}) %all-to-all-start) | async-done | bytes 786464 | tf_op jit(solution)/shard_map/all_to_all | solution.py:99
  37.1 3.0 %reshape.257 = bf16[32,6,32,64]{3,2,1,0:T(8,128)(2,1)S(1)} reshape(bf16[32,2,6144]{2,1,0:T(2,128)(2,1)} %all-to-all-done) | data formatting | bytes 1572864
  40.1 0.8 multiply_reduce_fusion
  40.9 2.2 %copy.34 = bf16[32,192,64]{1,2,0:T(8,128)(2,1)} copy(bf16[32,192,64]{2,0,1:T(8,128)(2,1)S(1)} %bitcast.59) | data formatting | bytes 1572864 | tf_op jit(solution)/shard_map/reshape | solution.py:100
  43.0 2.4 %convolution_convert_fusion.1 = bf16[32,256,192]{1,2,0:T(8,128)(2,1)S(1)} fusion(bf16[32,64,256]{2,1,0:T(8,128)(2,1)S(1)} %fusion, bf16[32,192,64]{1,2,0:T(8,128)(2,1)} %copy.34), kind=kOutput, calls=%fused_computation.2 | convolution fusion | flops 202899456 | bytes 4980736 | tf_op jit(solution)/shard_map/mkc,mcb->mkb/dot_general | solution.py:107
  45.4 0.0 copy-done.1
  45.4 1.0 convolution_convert_fusion
  46.4 3.4 %copy.44 = bf16[4,8,192,256]{3,1,2,0:T(8,128)(2,1)} copy(bf16[4,8,192,256]{3,2,1,0:T(8,128)(2,1)S(1)} %bitcast.62) | data formatting | bytes 6291456
  49.9 3.5 %copy.43 = bf16[4,8,192,256]{3,1,2,0:T(8,128)(2,1)} copy(bf16[4,8,192,256]{3,2,1,0:T(8,128)(2,1)S(1)} %bitcast.60) | data formatting | bytes 6291456
  53.4 0.4 fusion.2
  53.8 0.9 copy.45
  54.6 10.8 %shard_map.77 = f32[1,256]{1,0:T(1,128)} custom-call(bf16[128,64]{1,0:T(8,128)(2,1)} %copy.37.table_ref, bf16[32,49152]{1,0:T(8,128)(2,1)} %bitcast.57, bf16[32,49152]{1,0:T(8,128)(2,1)} %bitcast.55, f32[1,49152]{1,0:T(1,128)} %bitcast.66), custom_call_target="tpu_custom_call" | custom-call | tf_op jit(solution)/shard_map/pallas_call | solution.py:125
  65.5 0.7 broadcast_bitcast_fusion
  66.1 0.2 copy.46
  66.3 0.0 copy-done.3
  66.4 0.9 sub.13.shift_ref
  67.2 10.6 %shard_map.78 = (bf16[64,49152]{1,0:T(8,128)(2,1)}, f32[1,49152]{1,0:T(1,128)}) custom-call(bf16[128,64]{1,0:T(8,128)(2,1)} %copy.37.table_ref, bf16[32,49152]{1,0:T(8,128)(2,1)} %bitcast.58, bf16[32,49152]{1,0:T(8,128)(2,1)} %bitcast.56, f32[1,49152]{1,0:T(1,128)} %sub.13.shift_ref, bf16[80,128]{1,0:T(8,128)(2,1)} %maximum_maximum_fusion.turn_ref), custom_call_target="tpu_custom_call" | custom-call | tf_op jit(solution)/shard_map/pallas_call | solution.py:135
  77.8 3.3 %fusion.22 = (bf16[32,49152]{1,0:T(8,128)(2,1)S(1)}, bf16[32,49152]{1,0:T(8,128)(2,1)S(1)}) fusion(bf16[64,49152]{1,0:T(8,128)(2,1)} %get-tuple-element.4), kind=kLoop, calls=%fused_computation.46 | loop fusion | bytes 12582912 | tf_op jit(solution)/shard_map/slice | solution.py:156
  81.1 0.7 copy.47
  81.8 1.1 fusion.24
  83.0 0.7 copy.48
  83.7 2.5 %add_bitcast_fusion = f32[192,32,64]{0,2,1:T(8,128)} fusion(f32[32,64,192]{2,1,0:T(8,128)S(1)} %fusion.24, bf16[32,192,256]{2,1,0:T(8,128)(2,1)S(1)} %bitcast.64, bf16[32,32,256]{2,1,0:T(8,128)(2,1)S(1)} %copy-done.2, bf16[32,32,256]{2,1,0:T(8,128)(2,1)S(1)} %get-tuple-element.8), kind=kOutput, calls=%fused_computation.5 | convolution fusion | flops 203816960 | bytes 7340032 | tf_op jit(solution)/shard_map/mkb,mcb->kmc/dot_general | solution.py:156
  86.2 3.2 %copy.38 = f32[192,32,64]{2,1,0:T(8,128)S(1)} copy(f32[192,32,64]{0,2,1:T(8,128)} %add_bitcast_fusion) | data formatting | bytes 3145728 | tf_op jit(solution)/shard_map/add | solution.py:154
  89.4 0.0 copy-start.5
  89.4 2.1 %concatenate.16 = f32[8,4,6,2048]{3,2,1,0:T(8,128)} reshape(f32[192,32,64]{2,1,0:T(8,128)S(1)} %copy.38) | data formatting | bytes 3145728 | tf_op jit(solution)/shard_map/concatenate | solution.py:163
  91.5 0.5 broadcast.240
  92.0 1.1 reduce.9
  93.1 0.1 dot_general.32
  93.2 0.4 fusion.4
  93.6 0.1 reshape.234
  93.7 0.1 reduce_sum.49
  93.8 0.2 concatenate.19
  94.0 2.5 %concatenate.18 = f32[8,4,6,2176]{3,2,1,0:T(8,128)S(1)} concatenate(f32[8,4,6,2048]{3,2,1,0:T(8,128)} %concatenate.16, f32[8,4,6,32]{3,2,1,0:T(8,128)S(1)} %fusion.4, f32[8,4,6,1]{3,2,1,0:T(8,128)S(1)} %concatenate.19, f32[8,4,6,95]{3,2,1,0:T(8,128)S(1)} %broadcast_in_dim.41), dimensions={3} | concatenate | bytes 3342336 | tf_op jit(solution)/shard_map/concatenate | solution.py:163
  96.5 1.0 copy.40
  97.5 22.8 %all_to_all.15 = f32[8,4,6,2176]{3,0,2,1:T(8,128)S(1)} all-to-all(f32[8,4,6,2176]{3,0,2,1:T(8,128)S(1)} %copy.40), channel_id=1, replica_groups=mesh['x'=4,'core'=2,'z'=8,'y'=4] {'y'}, dimensions={1} | all-to-all | bytes 3342336 | tf_op jit(solution)/shard_map/all_to_all | solution.py:167
  120.3 0.1 reduce_sum.50
  120.4 0.1 copy.41
  120.5 19.0 %all_to_all.16 = f32[8,6,2176]{2,1,0:T(8,128)S(1)} all-to-all(f32[8,6,2176]{2,1,0:T(8,128)S(1)} %copy.41), channel_id=1, replica_groups=mesh['x'=4,'core'=2,'z'=8,'y'=4] {'z'}, dimensions={0} | all-to-all | bytes 835584 | tf_op jit(solution)/shard_map/all_to_all | solution.py:168
  139.6 17.5 %all-gather.1 = f32[8,6,2176]{2,1,0:T(8,128)S(1)} all-gather(f32[1,6,2176]{2,1,0:T(8,128)S(1)} %bitcast.71), channel_id=2, replica_groups=mesh['x'=4,'core'=2,'z'=8,'y'=4] {'x','core'}, dimensions={0}, use_global_device_ids=true | all-gather | bytes 470016 | tf_op jit(solution)/shard_map/all_gather | solution.py:169
  157.1 0.7 fusion.19
  157.8 0.1 div.21
  157.9 0.2 div.22
  158.1 0.6 slice_divide_fusion
  (17 shorter events, 0.2 us)
Async XLA Ops:
  0.6 17.2 %copy-start = (f32[64,32]{0,1:T(8,128)S(1)}, f32[64,32]{0,1:T(8,128)}, u32[]{:S(2)}) copy-start(f32[64,32]{0,1:T(8,128)} %param.9) | copy-start | bytes 24580
  0.6 17.2 %copy-start.6 = (f32[32]{0:T(128)S(1)}, f32[32]{0:T(128)}, u32[]{:S(2)}) copy-start(f32[32]{0:T(128)} %param.10) | copy-start | bytes 388
  0.7 17.2 %copy-start.8 = (s32[256]{0:T(256)S(1)}, s32[256]{0:T(256)}, u32[]{:S(2)}) copy-start(s32[256]{0:T(256)} %param.8) | copy-start | bytes 3076
  0.7 17.3 %copy-start.4 = (bf16[2048,256]{1,0:T(8,128)(2,1)S(1)}, bf16[2048,256]{1,0:T(8,128)(2,1)}, u32[]{:S(2)}) copy-start(bf16[2048,256]{1,0:T(8,128)(2,1)} %param.7) | copy-start | bytes 3145732
  3.9 33.2 %all-to-all-start = ((bf16[32,2,6144]{2,1,0:T(2,128)(2,1)}), bf16[32,2,6144]{2,1,0:T(2,128)(2,1)}, u32[]{:S(2)}, u32[]{:S(2)}) async-start(bf16[32,2,6144]{2,1,0:T(2,128)(2,1)} %reshape.256), calls=%async_computation | async-start | bytes 1572864 | tf_op jit(solution)/shard_map/all_to_all | solution.py:99
  43.0 2.4 %copy-start.1 = (bf16[32,192,64]{1,2,0:T(8,128)(2,1)S(1)}, bf16[32,192,64]{1,2,0:T(8,128)(2,1)}, u32[]{:S(2)}) copy-start(bf16[32,192,64]{1,2,0:T(8,128)(2,1)} %copy.34) | copy-start | bytes 2359300
  43.0 2.4 %copy-start.2 = (bf16[32,32,256]{2,1,0:T(8,128)(2,1)S(1)}, bf16[32,32,256]{2,1,0:T(8,128)(2,1)}, u32[]{:S(2)}) copy-start(bf16[32,32,256]{2,1,0:T(8,128)(2,1)} %get-tuple-element.9) | copy-start | bytes 1572868
  49.9 3.5 %copy-start.7 = (f32[192]{0:T(256)S(1)}, f32[192]{0:T(256)}, u32[]{:S(2)}) copy-start(f32[192]{0:T(256)} %param.11) | copy-start | bytes 2308
  54.6 11.7 %copy-start.3 = (f32[1,1,192,256]{3,1,2,0:T(1,128)S(1)}, f32[1,1,192,256]{3,1,2,0:T(1,128)}, u32[]{:S(2)}) copy-start(f32[1,1,192,256]{3,1,2,0:T(1,128)} %copy.45) | copy-start | bytes 589828
  89.4 2.6 %copy-start.5 = (f32[1,49152]{1,0:T(1,128)S(1)}, f32[1,49152]{1,0:T(1,128)}, u32[]{:S(2)}) copy-start(f32[1,49152]{1,0:T(1,128)} %get-tuple-element.5) | copy-start | bytes 589828

commit v7 on v6

--- a/solution.py
+++ b/solution.py
@@ -77,14 +77,17 @@
         out_ref[...] = top_ref[...] + jnp.log(total_ref[...])
 
 
-def spectra_kernel(table_ref, real_ref, imag_ref, shift_ref, turn_ref, spectra_ref, weight_ref):
+def spectra_kernel(
+    table_ref, real_ref, imag_ref, shift_ref, turn_ref, cos_ref, sin_ref, weight_ref
+):
     responsibility = jnp.exp(block_scores(table_ref, real_ref, imag_ref, shift_ref))
     full = jnp.dot(
         turn_ref[...], responsibility.astype(jnp.bfloat16), preferred_element_type=jnp.float32
     )
-    rows = spectra_ref.shape[0]
-    spectra_ref[...] = full[:rows].astype(jnp.bfloat16)
-    weight_ref[...] = full[rows : rows + 1]
+    rows = cos_ref.shape[0]
+    cos_ref[...] = full[:rows].astype(jnp.bfloat16)
+    sin_ref[...] = full[rows : 2 * rows].astype(jnp.bfloat16)
+    weight_ref[...] = full[2 * rows : 2 * rows + 1]
 
 
 def local(references, particles, defocus_bin, contrast_table, noise_power, class_prior):
@@ -132,7 +135,7 @@
         compiler_params=pltpu.CompilerParams(dimension_semantics=("arbitrary",)),
     )(table, crossed_real, crossed_imag, bias)
     shift = bias - jnp.tile(log_norm, (1, classes_total))
-    spectra, class_weight = pl.pallas_call(
+    spectra_cos, spectra_sin, class_weight = pl.pallas_call(
         spectra_kernel,
         grid=(steps,),
         in_specs=[
@@ -142,18 +145,20 @@
             row_spec,
             pl.BlockSpec(turn.shape, lambda i: (0, 0)),
         ],
-        out_specs=[pl.BlockSpec((2 * rows, block), lambda i: (0, i)), row_spec],
+        out_specs=[crossed_spec, crossed_spec, row_spec],
         out_shape=[
-            jax.ShapeDtypeStruct((2 * rows, width), jnp.bfloat16),
+            jax.ShapeDtypeStruct((rows, width), jnp.bfloat16),
+            jax.ShapeDtypeStruct((rows, width), jnp.bfloat16),
             jax.ShapeDtypeStruct((1, width), jnp.float32),
         ],
         compiler_params=pltpu.CompilerParams(dimension_semantics=("arbitrary",)),
     )(table, crossed_real, crossed_imag, shift, turn)
 
-    spectra = spectra.reshape(2, M, classes_total, columns)
+    spectra_cos = spectra_cos.reshape(M, classes_total, columns)
+    spectra_sin = spectra_sin.reshape(M, classes_total, columns)
     numer_all = jnp.einsum(
-        "mkb,mcb->kmc", spectra[0], weighted, preferred_element_type=jnp.float32
-    ) + jnp.einsum("mkb,mcb->kmc", spectra[1], swapped, preferred_element_type=jnp.float32)
+        "mkb,mcb->kmc", spectra_cos, weighted, preferred_element_type=jnp.float32
+    ) + jnp.einsum("mkb,mcb->kmc", spectra_sin, swapped, preferred_element_type=jnp.float32)
     numer_all = numer_all.reshape(classes_total, 2 * M * Q)
     class_weight = class_weight.reshape(classes_total, columns)
     cycles_all = jnp.dot(class_weight, power_term.T, precision=lax.Precision.HIGHEST)

time: 160 us -> 159 us (level)
    slice x1 -> x0, local copies, waits for them, and re-layouts: 3.25 us -> none  [local(): spectra[1]]
    unnamed x28 -> x30, local copies, waits for them, and re-layouts: 15.4 us -> 18.1 us
where the time goes in v7:
time: 159 us; the launch traced here: 158 us
  blocking collectives  59.3 us (37%)
  local copies, waits for them, and re-layouts  32.1 us (20%)
  Pallas kernels  21.3 us (13%)
  waiting for transfers between devices  17.9 us (11%)
  starting transfers between devices  12.1 us (8%)
  matrix products  7.95 us (5%)
  other arithmetic  6.45 us (4%)
    all_to_all x1, blocking collectives, local(): own = jnp.sum(lax.all_to_all(packed, 'y', 1, 1, tiled=True), 1)  22.8 us
    all_to_all x1, blocking collectives, local(): own = jnp.sum(lax.all_to_all(own, 'z', 0, 0, tiled=True), 0)  19 us
    unnamed x30, local copies, waits for them, and re-layouts  18.1 us
    all_to_all x1, waiting for transfers between devices, local(): gathered = lax.all_to_all(copies, DEV, 0, 0, tiled=True)  17.9 us
    all_gather x1, blocking collectives, local(): own = jnp.sum(lax.all_gather(own, GRP, axis=0, tiled=False), 0)  17.5 us
    all_to_all x1, starting transfers between devices, local(): gathered = lax.all_to_all(copies, DEV, 0, 0, tiled=True)  12.1 us
    pallas_call x1, Pallas kernels, local(): pl.pallas_call(functools.partial(norm_kernel, columns), grid=(steps,), in...  10.7 us
    pallas_call x1, Pallas kernels, local(): pl.pallas_call(spectra_kernel, grid=(steps,), in_specs=[table_spec, cross...  10.6 us
  transfers between devices with their start and end apart: 1, of which 1 were waited for; matrix products, arithmetic and copies ran while one was open for 2% of the time, Pallas kernels for 0%

profile of v7, /device:TPU:1, one launch (start us, length us, event | category | flops | bytes accessed | tf_op | source)
XLA Modules:
  0.0 158.2 jit_solution(8985738627676478417)
XLA Ops:
  0.6 0.0 copy-start
  0.6 0.0 copy-start.7
  0.7 0.0 copy-start.9
  0.7 0.0 copy-start.5
  0.7 1.0 reshape.230
  1.6 0.3 broadcast_bitcast_fusion.1
  2.0 1.9 %reshape.259 = bf16[32,2,6144]{2,1,0:T(2,128)(2,1)} reshape(bf16[32,6,32,64]{3,2,1,0:T(8,128)(2,1)S(1)} %broadcast_bitcast_fusion.1) | data formatting | bytes 1572864
  3.9 12.1 %all-to-all-start = ((bf16[32,2,6144]{2,1,0:T(2,128)(2,1)}), bf16[32,2,6144]{2,1,0:T(2,128)(2,1)}, u32[]{:S(2)}, u32[]{:S(2)}) async-start(bf16[32,2,6144]{2,1,0:T(2,128)(2,1)} %reshape.259), calls=%async_computation | async-start | bytes 1572864 | tf_op jit(solution)/shard_map/all_to_all | solution.py:102
  16.0 0.1 multiply_convert_fusion.1
  16.1 0.7 copy.37.table_ref
  16.9 0.1 pad.2.clone
  17.0 0.1 pad.1.clone
  17.0 0.1 fusion.17
  17.1 0.7 maximum_maximum_fusion.turn_ref
  17.8 0.0 copy-done
  17.8 0.0 copy-done.7
  17.8 0.0 copy-done.9
  17.8 0.1 broadcast_divide_fusion
  18.0 0.0 copy-done.5
  18.0 0.3 fusion
  18.3 0.9 fusion.22
  19.2 17.9 %all-to-all-done = bf16[32,2,6144]{2,1,0:T(2,128)(2,1)} async-done(((bf16[32,2,6144]{2,1,0:T(2,128)(2,1)}), bf16[32,2,6144]{2,1,0:T(2,128)(2,1)}, u32[]{:S(2)}, u32[]{:S(2)}) %all-to-all-start) | async-done | bytes 786464 | tf_op jit(solution)/shard_map/all_to_all | solution.py:102
  37.1 3.0 %reshape.260 = bf16[32,6,32,64]{3,2,1,0:T(8,128)(2,1)S(1)} reshape(bf16[32,2,6144]{2,1,0:T(2,128)(2,1)} %all-to-all-done) | data formatting | bytes 1572864
  40.1 0.8 multiply_reduce_fusion
  40.9 2.2 %copy.34 = bf16[32,192,64]{1,2,0:T(8,128)(2,1)} copy(bf16[32,192,64]{2,0,1:T(8,128)(2,1)S(1)} %bitcast.59) | data formatting | bytes 1572864 | tf_op jit(solution)/shard_map/reshape | solution.py:103
  43.0 2.4 %convolution_convert_fusion.1 = bf16[32,256,192]{1,2,0:T(8,128)(2,1)S(1)} fusion(bf16[32,64,256]{2,1,0:T(8,128)(2,1)S(1)} %fusion, bf16[32,192,64]{1,2,0:T(8,128)(2,1)} %copy.34), kind=kOutput, calls=%fused_computation.2 | convolution fusion | flops 202899456 | bytes 4980736 | tf_op jit(solution)/shard_map/mkc,mcb->mkb/dot_general | solution.py:110
  45.4 0.0 copy-done.1
  45.4 0.0 copy-done.2
  45.4 1.0 convolution_convert_fusion
  46.4 3.5 %copy.44 = bf16[4,8,192,256]{3,1,2,0:T(8,128)(2,1)} copy(bf16[4,8,192,256]{3,2,1,0:T(8,128)(2,1)S(1)} %bitcast.62) | data formatting | bytes 6291456
  49.9 3.5 %copy.43 = bf16[4,8,192,256]{3,1,2,0:T(8,128)(2,1)} copy(bf16[4,8,192,256]{3,2,1,0:T(8,128)(2,1)S(1)} %bitcast.60) | data formatting | bytes 6291456
  53.4 0.4 fusion.2
  53.8 0.9 copy.45
  54.7 10.7 %shard_map.77 = f32[1,256]{1,0:T(1,128)} custom-call(bf16[128,64]{1,0:T(8,128)(2,1)} %copy.37.table_ref, bf16[32,49152]{1,0:T(8,128)(2,1)} %bitcast.57, bf16[32,49152]{1,0:T(8,128)(2,1)} %bitcast.55, f32[1,49152]{1,0:T(1,128)} %bitcast.66), custom_call_target="tpu_custom_call" | custom-call | tf_op jit(solution)/shard_map/pallas_call | solution.py:128
  65.4 0.7 broadcast_bitcast_fusion
  66.1 0.2 copy.46
  66.3 0.9 sub.13.shift_ref
  67.2 10.6 %shard_map.78 = (bf16[32,49152]{1,0:T(8,128)(2,1)}, bf16[32,49152]{1,0:T(8,128)(2,1)}, f32[1,49152]{1,0:T(1,128)}) custom-call(bf16[128,64]{1,0:T(8,128)(2,1)} %copy.37.table_ref, bf16[32,49152]{1,0:T(8,128)(2,1)} %bitcast.58, bf16[32,49152]{1,0:T(8,128)(2,1)} %bitcast.56, f32[1,49152]{1,0:T(1,128)} %sub.13.shift_ref, ...), custom_call_target="tpu_custom_call" | custom-call | tf_op jit(solution)/shard_map/pallas_call | solution.py:138
  77.8 2.6 %copy.47 = bf16[4,8,192,256]{3,2,1,0:T(8,128)(2,1)S(1)} copy(bf16[4,8,192,256]{3,1,2,0:T(8,128)(2,1)} %bitcast.65) | data formatting | bytes 6291456
  80.4 1.1 fusion.23
  81.6 0.8 copy-done.3
  82.3 0.7 copy.48
  83.1 2.5 %add_bitcast_fusion = f32[192,32,64]{0,2,1:T(8,128)} fusion(f32[32,64,192]{2,1,0:T(8,128)S(1)} %fusion.23, bf16[32,192,256]{2,1,0:T(8,128)(2,1)S(1)} %bitcast.63, bf16[32,32,256]{2,1,0:T(8,128)(2,1)S(1)} %copy-done.2, bf16[32,32,256]{2,1,0:T(8,128)(2,1)S(1)} %get-tuple-element.8), kind=kOutput, calls=%fused_computation.5 | convolution fusion | flops 203816960 | bytes 7340032 | tf_op jit(solution)/shard_map/mkb,mcb->kmc/dot_general | solution.py:161
  85.6 3.2 %copy.38 = f32[192,32,64]{2,1,0:T(8,128)S(1)} copy(f32[192,32,64]{0,2,1:T(8,128)} %add_bitcast_fusion) | data formatting | bytes 3145728 | tf_op jit(solution)/shard_map/add | solution.py:159
  88.8 2.1 %concatenate.16 = f32[8,4,6,2048]{3,2,1,0:T(8,128)} reshape(f32[192,32,64]{2,1,0:T(8,128)S(1)} %copy.38) | data formatting | bytes 3145728 | tf_op jit(solution)/shard_map/concatenate | solution.py:168
  90.8 0.5 broadcast.240
  91.4 0.0 copy-done.6
  91.4 1.1 reduce.9
  92.5 0.1 dot_general.32
  92.5 0.4 fusion.4
  93.0 0.1 reshape.237
  93.0 0.1 reduce_sum.49
  93.2 0.2 concatenate.19
  93.4 2.5 %concatenate.18 = f32[8,4,6,2176]{3,2,1,0:T(8,128)S(1)} concatenate(f32[8,4,6,2048]{3,2,1,0:T(8,128)} %concatenate.16, f32[8,4,6,32]{3,2,1,0:T(8,128)S(1)} %fusion.4, f32[8,4,6,1]{3,2,1,0:T(8,128)S(1)} %concatenate.19, f32[8,4,6,95]{3,2,1,0:T(8,128)S(1)} %broadcast_in_dim.41), dimensions={3} | concatenate | bytes 3342336 | tf_op jit(solution)/shard_map/concatenate | solution.py:168
  95.9 1.0 copy.40
  96.9 22.8 %all_to_all.15 = f32[8,4,6,2176]{3,0,2,1:T(8,128)S(1)} all-to-all(f32[8,4,6,2176]{3,0,2,1:T(8,128)S(1)} %copy.40), channel_id=1, replica_groups=mesh['x'=4,'core'=2,'z'=8,'y'=4] {'y'}, dimensions={1} | all-to-all | bytes 3342336 | tf_op jit(solution)/shard_map/all_to_all | solution.py:172
  119.7 0.1 reduce_sum.50
  119.8 0.1 copy.41
  119.9 19.0 %all_to_all.16 = f32[8,6,2176]{2,1,0:T(8,128)S(1)} all-to-all(f32[8,6,2176]{2,1,0:T(8,128)S(1)} %copy.41), channel_id=1, replica_groups=mesh['x'=4,'core'=2,'z'=8,'y'=4] {'z'}, dimensions={0} | all-to-all | bytes 835584 | tf_op jit(solution)/shard_map/all_to_all | solution.py:173
  139.0 17.5 %all-gather.1 = f32[8,6,2176]{2,1,0:T(8,128)S(1)} all-gather(f32[1,6,2176]{2,1,0:T(8,128)S(1)} %bitcast.71), channel_id=2, replica_groups=mesh['x'=4,'core'=2,'z'=8,'y'=4] {'x','core'}, dimensions={0}, use_global_device_ids=true | all-gather | bytes 470016 | tf_op jit(solution)/shard_map/all_gather | solution.py:174
  156.5 0.7 fusion.19
  157.2 0.1 div.21
  157.3 0.2 div.22
  157.5 0.6 slice_divide_fusion
  (18 shorter events, 0.2 us)
Async XLA Ops:
  0.6 17.2 %copy-start = (f32[64,32]{0,1:T(8,128)S(1)}, f32[64,32]{0,1:T(8,128)}, u32[]{:S(2)}) copy-start(f32[64,32]{0,1:T(8,128)} %param.9) | copy-start | bytes 24580
  0.6 17.2 %copy-start.7 = (f32[32]{0:T(128)S(1)}, f32[32]{0:T(128)}, u32[]{:S(2)}) copy-start(f32[32]{0:T(128)} %param.10) | copy-start | bytes 388
  0.7 17.2 %copy-start.9 = (s32[256]{0:T(256)S(1)}, s32[256]{0:T(256)}, u32[]{:S(2)}) copy-start(s32[256]{0:T(256)} %param.8) | copy-start | bytes 3076
  0.7 17.3 %copy-start.5 = (bf16[2048,256]{1,0:T(8,128)(2,1)S(1)}, bf16[2048,256]{1,0:T(8,128)(2,1)}, u32[]{:S(2)}) copy-start(bf16[2048,256]{1,0:T(8,128)(2,1)} %param.7) | copy-start | bytes 3145732
  3.9 33.2 %all-to-all-start = ((bf16[32,2,6144]{2,1,0:T(2,128)(2,1)}), bf16[32,2,6144]{2,1,0:T(2,128)(2,1)}, u32[]{:S(2)}, u32[]{:S(2)}) async-start(bf16[32,2,6144]{2,1,0:T(2,128)(2,1)} %reshape.259), calls=%async_computation | async-start | bytes 1572864 | tf_op jit(solution)/shard_map/all_to_all | solution.py:102
  43.0 2.4 %copy-start.1 = (bf16[32,192,64]{1,2,0:T(8,128)(2,1)S(1)}, bf16[32,192,64]{1,2,0:T(8,128)(2,1)}, u32[]{:S(2)}) copy-start(bf16[32,192,64]{1,2,0:T(8,128)(2,1)} %copy.34) | copy-start | bytes 2359300
  43.0 2.4 %copy-start.2 = (bf16[32,32,256]{2,1,0:T(8,128)(2,1)S(1)}, bf16[32,32,256]{2,1,0:T(8,128)(2,1)}, u32[]{:S(2)}) copy-start(bf16[32,32,256]{2,1,0:T(8,128)(2,1)} %get-tuple-element.9) | copy-start | bytes 1572868
  49.9 3.5 %copy-start.8 = (f32[192]{0:T(256)S(1)}, f32[192]{0:T(256)}, u32[]{:S(2)}) copy-start(f32[192]{0:T(256)} %param.11) | copy-start | bytes 2308
  54.7 11.6 %copy-start.4 = (f32[1,1,192,256]{3,1,2,0:T(1,128)S(1)}, f32[1,1,192,256]{3,1,2,0:T(1,128)}, u32[]{:S(2)}) copy-start(f32[1,1,192,256]{3,1,2,0:T(1,128)} %copy.45) | copy-start | bytes 589828
  80.4 1.9 %copy-start.3 = (bf16[32,49152]{1,0:T(8,128)(2,1)S(1)}, bf16[32,49152]{1,0:T(8,128)(2,1)}, u32[]{:S(2)}) copy-start(bf16[32,49152]{1,0:T(8,128)(2,1)} %get-tuple-element.6) | copy-start | bytes 9437188
  88.8 2.6 %copy-start.6 = (f32[1,49152]{1,0:T(1,128)S(1)}, f32[1,49152]{1,0:T(1,128)}, u32[]{:S(2)}) copy-start(f32[1,49152]{1,0:T(1,128)} %get-tuple-element.7) | copy-start | bytes 589828

commit v8 on v7

--- a/solution.py
+++ b/solution.py
@@ -47,13 +47,13 @@
     return (weighted.reshape(freq_count, 2 * cycle_count, columns), power_term)
 
 
-def block_scores(table_ref, real_ref, imag_ref, shift_ref):
-    crossed = jnp.concatenate([real_ref[...], imag_ref[...]], 0)
+def class_scores(table_ref, real_ref, imag_ref, shift_ref, j):
+    crossed = jnp.concatenate([real_ref[j], imag_ref[j]], 0)
     raw = jnp.dot(table_ref[...], crossed, preferred_element_type=jnp.float32)
-    return raw + shift_ref[...]
+    return raw + shift_ref[pl.ds(j, 1), :]
 
 
-def norm_kernel(cols, table_ref, real_ref, imag_ref, bias_ref, out_ref, top_ref, total_ref):
+def norm_kernel(table_ref, real_ref, imag_ref, bias_ref, out_ref, top_ref, total_ref):
     step = pl.program_id(0)
 
     @pl.when(step == 0)
@@ -61,8 +61,7 @@
         top_ref[...] = jnp.full(top_ref.shape, -1e30, jnp.float32)
         total_ref[...] = jnp.zeros(total_ref.shape, jnp.float32)
 
-    scores = block_scores(table_ref, real_ref, imag_ref, bias_ref)
-    parts = [scores[:, j * cols : (j + 1) * cols] for j in range(scores.shape[1] // cols)]
+    parts = [class_scores(table_ref, real_ref, imag_ref, bias_ref, j) for j in range(real_ref.shape[0])]
     block_top = functools.reduce(jnp.maximum, [jnp.max(s, axis=0, keepdims=True) for s in parts])
     old_top = top_ref[...]
     new_top = jnp.maximum(old_top, block_top)
@@ -80,14 +79,15 @@
 def spectra_kernel(
     table_ref, real_ref, imag_ref, shift_ref, turn_ref, cos_ref, sin_ref, weight_ref
 ):
-    responsibility = jnp.exp(block_scores(table_ref, real_ref, imag_ref, shift_ref))
-    full = jnp.dot(
-        turn_ref[...], responsibility.astype(jnp.bfloat16), preferred_element_type=jnp.float32
-    )
-    rows = cos_ref.shape[0]
-    cos_ref[...] = full[:rows].astype(jnp.bfloat16)
-    sin_ref[...] = full[rows : 2 * rows].astype(jnp.bfloat16)
-    weight_ref[...] = full[2 * rows : 2 * rows + 1]
+    rows = cos_ref.shape[1]
+    for j in range(real_ref.shape[0]):
+        responsibility = jnp.exp(class_scores(table_ref, real_ref, imag_ref, shift_ref, j))
+        full = jnp.dot(
+            turn_ref[...], responsibility.astype(jnp.bfloat16), preferred_element_type=jnp.float32
+        )
+        cos_ref[j] = full[:rows].astype(jnp.bfloat16)
+        sin_ref[j] = full[rows : 2 * rows].astype(jnp.bfloat16)
+        weight_ref[pl.ds(j, 1), :] = full[2 * rows : 2 * rows + 1]
 
 
 def local(references, particles, defocus_bin, contrast_table, noise_power, class_prior):
@@ -97,36 +97,33 @@
     dev_count = lax.axis_size(DEV)
     classes_total = CLS_DEV * dev_count
 
-    own_rows = jnp.transpose(references.reshape(CLS_DEV, M, 2 * Q), (1, 0, 2))
-    copies = jnp.broadcast_to(own_rows[None], (dev_count,) + own_rows.shape)
+    copies = jnp.broadcast_to(references[None], (dev_count,) + references.shape)
     gathered = lax.all_to_all(copies, DEV, 0, 0, tiled=True)
-    grid_rows = jnp.transpose(gathered, (1, 0, 2, 3)).reshape(M, classes_total, 2 * Q)
+    class_grid = gathered.reshape(classes_total, M, 2 * Q)
     factor = jnp.where(jnp.arange(M) == 0, 1.0, 2.0).astype(jnp.float32)
-    squares = jnp.sum(grid_rows.astype(jnp.float32) ** 2 * factor[:, None, None], axis=0)
+    squares = jnp.sum(class_grid.astype(jnp.float32) ** 2 * factor[None, :, None], axis=1)
     cycle_power = squares[:, :Q] + squares[:, Q:]
     swapped = jnp.concatenate([weighted[:, Q:], -weighted[:, :Q]], 1)
     rows = M
-    width = classes_total * columns
     crossed_real = jnp.einsum(
-        "mkc,mcb->mkb", grid_rows, weighted, preferred_element_type=jnp.float32
-    ).astype(jnp.bfloat16).reshape(rows, width)
+        "kmc,mcb->kmb", class_grid, weighted, preferred_element_type=jnp.float32
+    ).astype(jnp.bfloat16)
     crossed_imag = jnp.einsum(
-        "mkc,mcb->mkb", grid_rows, swapped, preferred_element_type=jnp.float32
-    ).astype(jnp.bfloat16).reshape(rows, width)
+        "kmc,mcb->kmb", class_grid, swapped, preferred_element_type=jnp.float32
+    ).astype(jnp.bfloat16)
     penalty = jnp.dot(cycle_power, power_term, precision=lax.Precision.HIGHEST)
-    bias = (class_prior[:, None] - 0.5 * penalty).reshape(1, width)
+    bias = class_prior[:, None] - 0.5 * penalty
     table = jnp.transpose(score_table, (2, 0, 1)).reshape(R, 2 * M)
     turn = jnp.concatenate(
         [turn_table.reshape(2 * M, R), jnp.ones((1, R), jnp.bfloat16), jnp.zeros((15, R), jnp.bfloat16)], 0
     )
 
-    block = CLS_STEP * columns
-    steps = width // block
+    steps = classes_total // CLS_STEP
     table_spec = pl.BlockSpec((R, 2 * rows), lambda i: (0, 0))
-    crossed_spec = pl.BlockSpec((rows, block), lambda i: (0, i))
-    row_spec = pl.BlockSpec((1, block), lambda i: (0, i))
+    crossed_spec = pl.BlockSpec((CLS_STEP, rows, columns), lambda i: (i, 0, 0))
+    row_spec = pl.BlockSpec((CLS_STEP, columns), lambda i: (i, 0))
     log_norm = pl.pallas_call(
-        functools.partial(norm_kernel, columns),
+        norm_kernel,
         grid=(steps,),
         in_specs=[table_spec, crossed_spec, crossed_spec, row_spec],
         out_specs=pl.BlockSpec((1, columns), lambda i: (0, 0)),
@@ -134,7 +131,7 @@
         scratch_shapes=[pltpu.VMEM((1, columns), jnp.float32)] * 2,
         compiler_params=pltpu.CompilerParams(dimension_semantics=("arbitrary",)),
     )(table, crossed_real, crossed_imag, bias)
-    shift = bias - jnp.tile(log_norm, (1, classes_total))
+    shift = bias - log_norm
     spectra_cos, spectra_sin, class_weight = pl.pallas_call(
         spectra_kernel,
         grid=(steps,),
@@ -147,18 +144,16 @@
         ],
         out_specs=[crossed_spec, crossed_spec, row_spec],
         out_shape=[
-            jax.ShapeDtypeStruct((rows, width), jnp.bfloat16),
-            jax.ShapeDtypeStruct((rows, width), jnp.bfloat16),
-            jax.ShapeDtypeStruct((1, width), jnp.float32),
+            jax.ShapeDtypeStruct((classes_total, rows, columns), jnp.bfloat16),
+            jax.ShapeDtypeStruct((classes_total, rows, columns), jnp.bfloat16),
+            jax.ShapeDtypeStruct((classes_total, columns), jnp.float32),
         ],
         compiler_params=pltpu.CompilerParams(dimension_semantics=("arbitrary",)),
     )(table, crossed_real, crossed_imag, shift, turn)
 
-    spectra_cos = spectra_cos.reshape(M, classes_total, columns)
-    spectra_sin = spectra_sin.reshape(M, classes_total, columns)
     numer_all = jnp.einsum(
-        "mkb,mcb->kmc", spectra_cos, weighted, preferred_element_type=jnp.float32
-    ) + jnp.einsum("mkb,mcb->kmc", spectra_sin, swapped, preferred_element_type=jnp.float32)
+        "kmb,mcb->kmc", spectra_cos, weighted, preferred_element_type=jnp.float32
+    ) + jnp.einsum("kmb,mcb->kmc", spectra_sin, swapped, preferred_element_type=jnp.float32)
     numer_all = numer_all.reshape(classes_total, 2 * M * Q)
     class_weight = class_weight.reshape(classes_total, columns)
     cycles_all = jnp.dot(class_weight, power_term.T, precision=lax.Precision.HIGHEST)

time: 159 us -> 188 us (1.18)
  Pallas kernels: 21.3 us -> 48.1 us
  local copies, waits for them, and re-layouts: 32.1 us -> 23.6 us
  matrix products: 7.95 us -> 13.3 us
  waiting for transfers between devices: 17.9 us -> 23.1 us
    pallas_call x1, Pallas kernels: 10.6 us -> 37.2 us  [local(): pl.pallas_call(spectra_kernel, grid=(steps,), in_specs=[table_spec, cross...]
    unnamed x30 -> x18, local copies, waits for them, and re-layouts: 18.1 us -> 0.04 us
    convert_element_type x0 -> x1, local copies, waits for them, and re-layouts: none -> 6.24 us  [local(): crossed_real = jnp.einsum('kmc,mcb->kmb', class_grid, weighted, preferred...]
    all_to_all x1, waiting for transfers between devices: 17.9 us -> 23.1 us  [local(): gathered = lax.all_to_all(copies, DEV, 0, 0, tiled=True)]
    dot_general x4, matrix products: 6.99 us -> 10.8 us  [the longest x1 4 us: local(): jnp.einsum('kmb,mcb->kmc', spectra_sin, swapped, preferred_element_type=j...]
    broadcast_in_dim x0 -> x1, local copies, waits for them, and re-layouts: none -> 2 us  [local(): copies = jnp.broadcast_to(references[None], (dev_count,) + references.shape)]
    reshape x3 -> x2, local copies, waits for them, and re-layouts: 3.17 us -> 5.02 us  [local(): class_grid = gathered.reshape(classes_total, M, 2 * Q)]
    concatenate x4 -> x5, local copies, waits for them, and re-layouts: 5.8 us -> 5.81 us  [local(): jnp.concatenate([numer_all, cycles_all, mass_all[:, None], jnp.zeros((cla...]
where the time goes in v8:
time: 188 us; the launch traced here: 187 us
  blocking collectives  59.5 us (32%)
  Pallas kernels  48.1 us (26%)
  local copies, waits for them, and re-layouts  23.6 us (13%)
  waiting for transfers between devices  23.1 us (12%)
  matrix products  13.3 us (7%)
  starting transfers between devices  12.2 us (6%)
  other arithmetic  6.79 us (4%)
    pallas_call x1, Pallas kernels, local(): pl.pallas_call(spectra_kernel, grid=(steps,), in_specs=[table_spec, cross...  37.2 us
    all_to_all x1, blocking collectives, local(): own = jnp.sum(lax.all_to_all(packed, 'y', 1, 1, tiled=True), 1)  23.4 us
    all_to_all x1, waiting for transfers between devices, local(): gathered = lax.all_to_all(copies, DEV, 0, 0, tiled=True)  23.1 us
    all_gather x1, blocking collectives, local(): own = jnp.sum(lax.all_gather(own, GRP, axis=0, tiled=False), 0)  18.5 us
    all_to_all x1, blocking collectives, local(): own = jnp.sum(lax.all_to_all(own, 'z', 0, 0, tiled=True), 0)  17.6 us
    all_to_all x1, starting transfers between devices, local(): gathered = lax.all_to_all(copies, DEV, 0, 0, tiled=True)  12.2 us
    pallas_call x1, Pallas kernels, local(): pl.pallas_call(norm_kernel, grid=(steps,), in_specs=[table_spec, crossed_...  10.9 us
    convert_element_type x1, local copies, waits for them, and re-layouts, local(): crossed_real = jnp.einsum('kmc,mcb->kmb', class_grid, weighted, preferred...  6.24 us
  transfers between devices with their start and end apart: 1, of which 1 were waited for; matrix products, arithmetic and copies ran while one was open for 2% of the time, Pallas kernels for 0%

profile of v8, /device:TPU:1, one launch (start us, length us, event | category | flops | bytes accessed | tf_op | source)
XLA Modules:
  0.0 187.4 jit_solution(3096752066800029495)
XLA Ops:
  0.6 0.0 copy-start
  0.6 0.0 copy-start.6
  0.7 0.0 copy-start.8
  0.7 0.0 copy-start.5
  0.7 2.0 %broadcast_in_dim.20 = bf16[32,6,2048]{2,1,0:T(8,128)(2,1)} broadcast(bf16[6,2048]{1,0:T(8,128)(2,1)} %param.6), dimensions={1,2} | broadcast | bytes 811008 | tf_op jit(solution)/shard_map/broadcast_in_dim | solution.py:100
  2.7 12.2 %all-to-all-start = ((bf16[32,6,2048]{2,1,0:T(8,128)(2,1)}), bf16[32,6,2048]{2,1,0:T(8,128)(2,1)}, u32[]{:S(2)}, u32[]{:S(2)}) async-start(bf16[32,6,2048]{2,1,0:T(8,128)(2,1)} %broadcast_in_dim.20), calls=%async_computation | async-start | bytes 2097152 | tf_op jit(solution)/shard_map/all_to_all | solution.py:101
  14.9 0.1 pad.1.clone
  14.9 0.1 pad.2.clone
  15.0 0.1 multiply_convert_fusion.1
  15.1 0.7 copy.54.table_ref
  15.8 0.1 fusion.21
  15.9 0.7 maximum_maximum_fusion.turn_ref
  16.6 0.0 copy-done
  16.6 0.0 copy-done.6
  16.6 0.0 copy-done.8
  16.6 0.1 broadcast_divide_fusion
  16.8 0.0 copy-done.5
  16.8 0.3 fusion.6
  17.1 0.9 fusion.30
  18.0 23.1 %all-to-all-done = bf16[32,6,2048]{2,1,0:T(8,128)(2,1)} async-done(((bf16[32,6,2048]{2,1,0:T(8,128)(2,1)}), bf16[32,6,2048]{2,1,0:T(8,128)(2,1)}, u32[]{:S(2)}, u32[]{:S(2)}) %all-to-all-start) | async-done | bytes 786464 | tf_op jit(solution)/shard_map/all_to_all | solution.py:101
  41.0 2.9 %reshape.180 = bf16[192,32,64]{2,1,0:T(8,128)(2,1)S(1)} reshape(bf16[32,6,2048]{2,1,0:T(8,128)(2,1)} %all-to-all-done) | data formatting | bytes 1572864 | tf_op jit(solution)/shard_map/reshape | solution.py:102
  43.9 0.9 multiply_reduce_fusion
  44.8 2.2 %copy.49 = bf16[192,32,64]{0,2,1:T(8,128)(2,1)} copy(bf16[192,32,64]{2,1,0:T(8,128)(2,1)S(1)} %reshape.180) | data formatting | bytes 1572864 | tf_op jit(solution)/shard_map/reshape | solution.py:102
  46.9 0.0 copy-start.1
  46.9 0.0 copy-start.2
  46.9 2.4 %fusion.31 = bf16[32,256,192]{1,2,0:T(8,128)(2,1)S(1)} fusion(bf16[32,64,256]{2,1,0:T(8,128)(2,1)S(1)} %fusion.6, bf16[192,32,64]{0,2,1:T(8,128)(2,1)} %copy.49), kind=kOutput, calls=%fused_computation.51 | convolution fusion | flops 201326592 | bytes 4980736 | tf_op jit(solution)/shard_map/kmc,mcb->kmb/dot_general | solution.py:108
  49.3 0.0 copy-done.1
  49.3 0.0 copy-done.2
  49.3 1.0 fusion.10
  50.4 0.0 copy-start.7
  50.4 6.2 %fusion = (bf16[192,32,256]{2,1,0:T(8,128)(2,1)}, bf16[192,32,256]{2,1,0:T(8,128)(2,1)}) fusion(bf16[32,256,192]{1,2,0:T(8,128)(2,1)S(1)} %fusion.31, bf16[32,256,192]{1,2,0:T(8,128)(2,1)S(1)} %fusion.10), kind=kLoop, calls=%fused_computation.2 | loop fusion | bytes 12582912 | tf_op jit(solution)/shard_map/convert_element_type | solution.py:110
  56.6 0.0 copy-done.7
  56.6 1.1 fusion.9.bias_ref
  57.7 0.0 copy-start.4
  57.7 10.9 %shard_map.77 = f32[1,256]{1,0:T(1,128)} custom-call(bf16[128,64]{1,0:T(8,128)(2,1)} %copy.54.table_ref, bf16[192,32,256]{2,1,0:T(8,128)(2,1)} %get-tuple-element.14.real_ref, bf16[192,32,256]{2,1,0:T(8,128)(2,1)} %get-tuple-element.15.imag_ref, f32[192,256]{1,0:T(8,128)} %fusion.9.bias_ref), custom_call_target="tpu_custom_call" | custom-call | tf_op jit(solution)/shard_map/pallas_call | solution.py:125
  68.6 0.0 copy-done.4
  68.6 1.3 broadcast_subtract_fusion.shift_ref
  69.9 37.2 %shard_map.78 = (bf16[192,32,256]{2,1,0:T(8,128)(2,1)}, bf16[192,32,256]{2,1,0:T(8,128)(2,1)}, f32[192,256]{1,0:T(8,128)}) custom-call(bf16[128,64]{1,0:T(8,128)(2,1)} %copy.54.table_ref, bf16[192,32,256]{2,1,0:T(8,128)(2,1)} %get-tuple-element.14.real_ref, bf16[192,32,256]{2,1,0:T(8,128)(2,1)} %get-tuple-element.15.imag_ref, ...), custom_call_target="tpu_custom_call" | custom-call | tf_op jit(solution)/shard_map/pallas_call | solution.py:135
  107.1 1.3 fusion.27
  108.4 1.0 reduce_sum.46
  109.5 0.2 concatenate.22
  109.7 0.0 copy-start.3
  109.7 4.0 %fusion.2 = f32[32,64,192]{2,1,0:T(8,128)S(1)} fusion(bf16[192,32,256]{2,1,0:T(8,128)(2,1)} %get-tuple-element.6, bf16[32,32,256]{2,1,0:T(8,128)(2,1)S(1)} %copy-done.2, bf16[32,32,256]{2,1,0:T(8,128)(2,1)S(1)} %get-tuple-element.8), kind=kOutput, calls=%fused_computation.4 | convolution fusion | flops 203423744 | bytes 5767168 | tf_op jit(solution)/shard_map/kmb,mcb->kmc/dot_general | solution.py:156
  113.7 0.0 copy-done.3
  113.7 3.4 %add_bitcast_fusion = f32[192,32,64]{0,2,1:T(8,128)} fusion(f32[32,64,192]{2,1,0:T(8,128)S(1)} %fusion.2, bf16[32,64,256]{2,1,0:T(8,128)(2,1)S(1)} %fusion.6, bf16[192,32,256]{2,1,0:T(8,128)(2,1)S(1)} %copy-done.3), kind=kOutput, calls=%fused_computation.11 | convolution fusion | flops 201719808 | bytes 7340032 | tf_op jit(solution)/shard_map/kmb,mcb->kmc/dot_general | solution.py:154
  117.1 3.2 %copy.57 = f32[192,32,64]{2,1,0:T(8,128)S(1)} copy(f32[192,32,64]{0,2,1:T(8,128)} %add_bitcast_fusion) | data formatting | bytes 3145728 | tf_op jit(solution)/shard_map/add | solution.py:154
  120.3 2.1 %concatenate.18 = f32[8,4,6,2048]{3,2,1,0:T(8,128)} reshape(f32[192,32,64]{2,1,0:T(8,128)S(1)} %copy.57) | data formatting | bytes 3145728 | tf_op jit(solution)/shard_map/concatenate | solution.py:163
  122.4 2.5 %concatenate.21 = f32[8,4,6,2176]{3,2,1,0:T(8,128)S(1)} concatenate(f32[8,4,6,2048]{3,2,1,0:T(8,128)} %concatenate.18, f32[8,4,6,32]{3,2,1,0:T(8,128)S(1)} %concatenate.19, f32[8,4,6,1]{3,2,1,0:T(8,128)S(1)} %concatenate.22, f32[8,4,6,95]{3,2,1,0:T(8,128)S(1)} %broadcast_in_dim.41), dimensions={3} | concatenate | bytes 3342336 | tf_op jit(solution)/shard_map/concatenate | solution.py:163
  124.9 1.0 copy.60
  125.9 23.4 %all_to_all.15 = f32[8,4,6,2176]{3,0,2,1:T(8,128)S(1)} all-to-all(f32[8,4,6,2176]{3,0,2,1:T(8,128)S(1)} %copy.60), channel_id=1, replica_groups=mesh['x'=4,'core'=2,'z'=8,'y'=4] {'y'}, dimensions={1} | all-to-all | bytes 3342336 | tf_op jit(solution)/shard_map/all_to_all | solution.py:167
  149.3 0.1 reduce_sum.47
  149.4 0.1 copy.61
  149.6 17.6 %all_to_all.16 = f32[8,6,2176]{2,1,0:T(8,128)S(1)} all-to-all(f32[8,6,2176]{2,1,0:T(8,128)S(1)} %copy.61), channel_id=1, replica_groups=mesh['x'=4,'core'=2,'z'=8,'y'=4] {'z'}, dimensions={0} | all-to-all | bytes 835584 | tf_op jit(solution)/shard_map/all_to_all | solution.py:168
  167.2 18.5 %all-gather.1 = f32[8,6,2176]{2,1,0:T(8,128)S(1)} all-gather(f32[1,6,2176]{2,1,0:T(8,128)S(1)} %bitcast.25), channel_id=2, replica_groups=mesh['x'=4,'core'=2,'z'=8,'y'=4] {'x','core'}, dimensions={0}, use_global_device_ids=true | all-gather | bytes 470016 | tf_op jit(solution)/shard_map/all_gather | solution.py:169
  185.8 0.7 fusion.23
  186.5 0.1 div.21
  186.5 0.2 div.22
  186.7 0.6 slice_divide_fusion
  (10 shorter events, 0.1 us)
Async XLA Ops:
  0.6 16.0 %copy-start = (f32[64,32]{0,1:T(8,128)S(1)}, f32[64,32]{0,1:T(8,128)}, u32[]{:S(2)}) copy-start(f32[64,32]{0,1:T(8,128)} %param.9) | copy-start | bytes 24580
  0.6 16.0 %copy-start.6 = (f32[32]{0:T(128)S(1)}, f32[32]{0:T(128)}, u32[]{:S(2)}) copy-start(f32[32]{0:T(128)} %param.10) | copy-start | bytes 388
  0.7 16.0 %copy-start.8 = (s32[256]{0:T(256)S(1)}, s32[256]{0:T(256)}, u32[]{:S(2)}) copy-start(s32[256]{0:T(256)} %param.8) | copy-start | bytes 3076
  0.7 16.1 %copy-start.5 = (bf16[2048,256]{1,0:T(8,128)(2,1)S(1)}, bf16[2048,256]{1,0:T(8,128)(2,1)}, u32[]{:S(2)}) copy-start(bf16[2048,256]{1,0:T(8,128)(2,1)} %param.7) | copy-start | bytes 3145732
  2.7 38.4 %all-to-all-start = ((bf16[32,6,2048]{2,1,0:T(8,128)(2,1)}), bf16[32,6,2048]{2,1,0:T(8,128)(2,1)}, u32[]{:S(2)}, u32[]{:S(2)}) async-start(bf16[32,6,2048]{2,1,0:T(8,128)(2,1)} %broadcast_in_dim.20), calls=%async_computation | async-start | bytes 2097152 | tf_op jit(solution)/shard_map/all_to_all | solution.py:101
  46.9 2.4 %copy-start.1 = (bf16[192,32,64]{0,2,1:T(8,128)(2,1)S(1)}, bf16[192,32,64]{0,2,1:T(8,128)(2,1)}, u32[]{:S(2)}) copy-start(bf16[192,32,64]{0,2,1:T(8,128)(2,1)} %copy.49) | copy-start | bytes 2359300
  46.9 2.4 %copy-start.2 = (bf16[32,32,256]{2,1,0:T(8,128)(2,1)S(1)}, bf16[32,32,256]{2,1,0:T(8,128)(2,1)}, u32[]{:S(2)}) copy-start(bf16[32,32,256]{2,1,0:T(8,128)(2,1)} %get-tuple-element.9) | copy-start | bytes 1572868
  50.4 6.3 %copy-start.7 = (f32[192]{0:T(256)S(1)}, f32[192]{0:T(256)}, u32[]{:S(2)}) copy-start(f32[192]{0:T(256)} %param.11) | copy-start | bytes 2308
  57.7 10.9 %copy-start.4 = (f32[192,256]{1,0:T(8,128)S(1)}, f32[192,256]{1,0:T(8,128)}, u32[]{:S(2)}) copy-start(f32[192,256]{1,0:T(8,128)} %fusion.9.bias_ref) | copy-start | bytes 589828
  109.7 4.0 %copy-start.3 = (bf16[192,32,256]{2,1,0:T(8,128)(2,1)S(1)}, bf16[192,32,256]{2,1,0:T(8,128)(2,1)}, u32[]{:S(2)}) copy-start(bf16[192,32,256]{2,1,0:T(8,128)(2,1)} %get-tuple-element.5) | copy-start | bytes 9437188

commit v9 on v8

--- a/solution.py
+++ b/solution.py
@@ -47,13 +47,17 @@
     return (weighted.reshape(freq_count, 2 * cycle_count, columns), power_term)
 
 
-def class_scores(table_ref, real_ref, imag_ref, shift_ref, j):
-    crossed = jnp.concatenate([real_ref[j], imag_ref[j]], 0)
+def block_scores(table_ref, real_ref, imag_ref, shift_ref):
+    classes = real_ref.shape[0]
+    crossed = jnp.concatenate(
+        [jnp.concatenate([real_ref[j], imag_ref[j]], 0) for j in range(classes)], 1
+    )
     raw = jnp.dot(table_ref[...], crossed, preferred_element_type=jnp.float32)
-    return raw + shift_ref[pl.ds(j, 1), :]
-
-
-def norm_kernel(table_ref, real_ref, imag_ref, bias_ref, out_ref, top_ref, total_ref):
+    shift = jnp.concatenate([shift_ref[pl.ds(j, 1), :] for j in range(classes)], 1)
+    return raw + shift
+
+
+def norm_kernel(cols, table_ref, real_ref, imag_ref, bias_ref, out_ref, top_ref, total_ref):
     step = pl.program_id(0)
 
     @pl.when(step == 0)
@@ -61,7 +65,8 @@
         top_ref[...] = jnp.full(top_ref.shape, -1e30, jnp.float32)
         total_ref[...] = jnp.zeros(total_ref.shape, jnp.float32)
 
-    parts = [class_scores(table_ref, real_ref, imag_ref, bias_ref, j) for j in range(real_ref.shape[0])]
+    scores = block_scores(table_ref, real_ref, imag_ref, bias_ref)
+    parts = [scores[:, j * cols : (j + 1) * cols] for j in range(scores.shape[1] // cols)]
     block_top = functools.reduce(jnp.maximum, [jnp.max(s, axis=0, keepdims=True) for s in parts])
     old_top = top_ref[...]
     new_top = jnp.maximum(old_top, block_top)
@@ -77,17 +82,18 @@
 
 
 def spectra_kernel(
-    table_ref, real_ref, imag_ref, shift_ref, turn_ref, cos_ref, sin_ref, weight_ref
+    cols, table_ref, real_ref, imag_ref, shift_ref, turn_ref, cos_ref, sin_ref, weight_ref
 ):
+    responsibility = jnp.exp(block_scores(table_ref, real_ref, imag_ref, shift_ref))
+    full = jnp.dot(
+        turn_ref[...], responsibility.astype(jnp.bfloat16), preferred_element_type=jnp.float32
+    )
     rows = cos_ref.shape[1]
-    for j in range(real_ref.shape[0]):
-        responsibility = jnp.exp(class_scores(table_ref, real_ref, imag_ref, shift_ref, j))
-        full = jnp.dot(
-            turn_ref[...], responsibility.astype(jnp.bfloat16), preferred_element_type=jnp.float32
-        )
-        cos_ref[j] = full[:rows].astype(jnp.bfloat16)
-        sin_ref[j] = full[rows : 2 * rows].astype(jnp.bfloat16)
-        weight_ref[pl.ds(j, 1), :] = full[2 * rows : 2 * rows + 1]
+    for j in range(cos_ref.shape[0]):
+        part = full[:, j * cols : (j + 1) * cols]
+        cos_ref[j] = part[:rows].astype(jnp.bfloat16)
+        sin_ref[j] = part[rows : 2 * rows].astype(jnp.bfloat16)
+        weight_ref[pl.ds(j, 1), :] = part[2 * rows : 2 * rows + 1]
 
 
 def local(references, particles, defocus_bin, contrast_table, noise_power, class_prior):
@@ -123,7 +129,7 @@
     crossed_spec = pl.BlockSpec((CLS_STEP, rows, columns), lambda i: (i, 0, 0))
     row_spec = pl.BlockSpec((CLS_STEP, columns), lambda i: (i, 0))
     log_norm = pl.pallas_call(
-        norm_kernel,
+        functools.partial(norm_kernel, columns),
         grid=(steps,),
         in_specs=[table_spec, crossed_spec, crossed_spec, row_spec],
         out_specs=pl.BlockSpec((1, columns), lambda i: (0, 0)),
@@ -133,7 +139,7 @@
     )(table, crossed_real, crossed_imag, bias)
     shift = bias - log_norm
     spectra_cos, spectra_sin, class_weight = pl.pallas_call(
-        spectra_kernel,
+        functools.partial(spectra_kernel, columns),
         grid=(steps,),
         in_specs=[
             table_spec,

time: 188 us -> 161 us (0.86)
  Pallas kernels: 48.1 us -> 21.3 us
    pallas_call x2, Pallas kernels: 48.1 us -> 21.3 us  [the longest x1 10.8 us: local(): pl.pallas_call(functools.partial(norm_kernel, columns), grid=(steps,), in...]
where the time goes in v9:
time: 161 us
  blocking collectives  59.5 us (37%)
  local copies, waits for them, and re-layouts  23.6 us (15%)
  waiting for transfers between devices  23.1 us (14%)
  Pallas kernels  21.3 us (13%)
  matrix products  13.3 us (8%)
  starting transfers between devices  12.2 us (8%)
  other arithmetic  6.79 us (4%)
    all_to_all x1, blocking collectives, local(): own = jnp.sum(lax.all_to_all(packed, 'y', 1, 1, tiled=True), 1)  23.4 us
    all_to_all x1, waiting for transfers between devices, local(): gathered = lax.all_to_all(copies, DEV, 0, 0, tiled=True)  23.1 us
    all_gather x1, blocking collectives, local(): own = jnp.sum(lax.all_gather(own, GRP, axis=0, tiled=False), 0)  18.5 us
    all_to_all x1, blocking collectives, local(): own = jnp.sum(lax.all_to_all(own, 'z', 0, 0, tiled=True), 0)  17.6 us
    all_to_all x1, starting transfers between devices, local(): gathered = lax.all_to_all(copies, DEV, 0, 0, tiled=True)  12.2 us
    pallas_call x1, Pallas kernels, local(): pl.pallas_call(functools.partial(norm_kernel, columns), grid=(steps,), in...  10.8 us
    pallas_call x1, Pallas kernels, local(): pl.pallas_call(functools.partial(spectra_kernel, columns), grid=(steps,),...  10.6 us
    convert_element_type x1, local copies, waits for them, and re-layouts, local(): crossed_real = jnp.einsum('kmc,mcb->kmb', class_grid, weighted, preferred...  6.24 us
  transfers between devices with their start and end apart: 1, of which 1 were waited for; matrix products, arithmetic and copies ran while one was open for 2% of the time, Pallas kernels for 0%

profile of v9, /device:TPU:1, one launch (start us, length us, event | category | flops | bytes accessed | tf_op | source)
XLA Modules:
  0.0 160.6 jit_solution(9802440540558914310)
XLA Ops:
  0.6 0.0 copy-start
  0.6 0.0 copy-start.6
  0.7 0.0 copy-start.8
  0.7 0.0 copy-start.5
  0.7 2.0 %broadcast_in_dim.20 = bf16[32,6,2048]{2,1,0:T(8,128)(2,1)} broadcast(bf16[6,2048]{1,0:T(8,128)(2,1)} %param.6), dimensions={1,2} | broadcast | bytes 811008 | tf_op jit(solution)/shard_map/broadcast_in_dim | solution.py:106
  2.7 12.2 %all-to-all-start = ((bf16[32,6,2048]{2,1,0:T(8,128)(2,1)}), bf16[32,6,2048]{2,1,0:T(8,128)(2,1)}, u32[]{:S(2)}, u32[]{:S(2)}) async-start(bf16[32,6,2048]{2,1,0:T(8,128)(2,1)} %broadcast_in_dim.20), calls=%async_computation | async-start | bytes 2097152 | tf_op jit(solution)/shard_map/all_to_all | solution.py:107
  14.9 0.1 pad.1.clone
  14.9 0.1 pad.2.clone
  15.0 0.1 multiply_convert_fusion.1
  15.1 0.7 copy.54.table_ref
  15.8 0.1 fusion.21
  15.9 0.7 maximum_maximum_fusion.turn_ref
  16.6 0.0 copy-done
  16.6 0.0 copy-done.6
  16.6 0.0 copy-done.8
  16.6 0.1 broadcast_divide_fusion
  16.8 0.0 copy-done.5
  16.8 0.3 fusion.6
  17.1 0.9 fusion.30
  18.0 23.1 %all-to-all-done = bf16[32,6,2048]{2,1,0:T(8,128)(2,1)} async-done(((bf16[32,6,2048]{2,1,0:T(8,128)(2,1)}), bf16[32,6,2048]{2,1,0:T(8,128)(2,1)}, u32[]{:S(2)}, u32[]{:S(2)}) %all-to-all-start) | async-done | bytes 786464 | tf_op jit(solution)/shard_map/all_to_all | solution.py:107
  41.0 2.9 %reshape.180 = bf16[192,32,64]{2,1,0:T(8,128)(2,1)S(1)} reshape(bf16[32,6,2048]{2,1,0:T(8,128)(2,1)} %all-to-all-done) | data formatting | bytes 1572864 | tf_op jit(solution)/shard_map/reshape | solution.py:108
  43.9 0.9 multiply_reduce_fusion
  44.8 2.2 %copy.49 = bf16[192,32,64]{0,2,1:T(8,128)(2,1)} copy(bf16[192,32,64]{2,1,0:T(8,128)(2,1)S(1)} %reshape.180) | data formatting | bytes 1572864 | tf_op jit(solution)/shard_map/reshape | solution.py:108
  46.9 0.0 copy-start.1
  46.9 0.0 copy-start.2
  46.9 2.4 %fusion.31 = bf16[32,256,192]{1,2,0:T(8,128)(2,1)S(1)} fusion(bf16[32,64,256]{2,1,0:T(8,128)(2,1)S(1)} %fusion.6, bf16[192,32,64]{0,2,1:T(8,128)(2,1)} %copy.49), kind=kOutput, calls=%fused_computation.51 | convolution fusion | flops 201326592 | bytes 4980736 | tf_op jit(solution)/shard_map/kmc,mcb->kmb/dot_general | solution.py:114
  49.3 0.0 copy-done.1
  49.3 0.0 copy-done.2
  49.3 1.0 fusion.10
  50.4 0.0 copy-start.7
  50.4 6.2 %fusion = (bf16[192,32,256]{2,1,0:T(8,128)(2,1)}, bf16[192,32,256]{2,1,0:T(8,128)(2,1)}) fusion(bf16[32,256,192]{1,2,0:T(8,128)(2,1)S(1)} %fusion.31, bf16[32,256,192]{1,2,0:T(8,128)(2,1)S(1)} %fusion.10), kind=kLoop, calls=%fused_computation.2 | loop fusion | bytes 12582912 | tf_op jit(solution)/shard_map/convert_element_type | solution.py:116
  56.6 0.0 copy-done.7
  56.6 1.1 fusion.9.bias_ref
  57.7 0.0 copy-start.4
  57.7 10.8 %shard_map.77 = f32[1,256]{1,0:T(1,128)} custom-call(bf16[128,64]{1,0:T(8,128)(2,1)} %copy.54.table_ref, bf16[192,32,256]{2,1,0:T(8,128)(2,1)} %get-tuple-element.14.real_ref, bf16[192,32,256]{2,1,0:T(8,128)(2,1)} %get-tuple-element.15.imag_ref, f32[192,256]{1,0:T(8,128)} %fusion.9.bias_ref), custom_call_target="tpu_custom_call" | custom-call | tf_op jit(solution)/shard_map/pallas_call | solution.py:131
  68.5 0.0 copy-done.4
  68.5 1.3 broadcast_subtract_fusion.shift_ref
  69.8 10.6 %shard_map.78 = (bf16[192,32,256]{2,1,0:T(8,128)(2,1)}, bf16[192,32,256]{2,1,0:T(8,128)(2,1)}, f32[192,256]{1,0:T(8,128)}) custom-call(bf16[128,64]{1,0:T(8,128)(2,1)} %copy.54.table_ref, bf16[192,32,256]{2,1,0:T(8,128)(2,1)} %get-tuple-element.14.real_ref, bf16[192,32,256]{2,1,0:T(8,128)(2,1)} %get-tuple-element.15.imag_ref, ...), custom_call_target="tpu_custom_call" | custom-call | tf_op jit(solution)/shard_map/pallas_call | solution.py:141
  80.3 1.3 fusion.27
  81.7 1.0 reduce_sum.46
  82.7 0.2 concatenate.22
  82.9 0.0 copy-start.3
  82.9 4.0 %fusion.2 = f32[32,64,192]{2,1,0:T(8,128)S(1)} fusion(bf16[192,32,256]{2,1,0:T(8,128)(2,1)} %get-tuple-element.6, bf16[32,32,256]{2,1,0:T(8,128)(2,1)S(1)} %copy-done.2, bf16[32,32,256]{2,1,0:T(8,128)(2,1)S(1)} %get-tuple-element.8), kind=kOutput, calls=%fused_computation.4 | convolution fusion | flops 203423744 | bytes 5767168 | tf_op jit(solution)/shard_map/kmb,mcb->kmc/dot_general | solution.py:162
  86.9 0.0 copy-done.3
  87.0 3.4 %add_bitcast_fusion = f32[192,32,64]{0,2,1:T(8,128)} fusion(f32[32,64,192]{2,1,0:T(8,128)S(1)} %fusion.2, bf16[32,64,256]{2,1,0:T(8,128)(2,1)S(1)} %fusion.6, bf16[192,32,256]{2,1,0:T(8,128)(2,1)S(1)} %copy-done.3), kind=kOutput, calls=%fused_computation.11 | convolution fusion | flops 201719808 | bytes 7340032 | tf_op jit(solution)/shard_map/kmb,mcb->kmc/dot_general | solution.py:160
  90.3 3.2 %copy.57 = f32[192,32,64]{2,1,0:T(8,128)S(1)} copy(f32[192,32,64]{0,2,1:T(8,128)} %add_bitcast_fusion) | data formatting | bytes 3145728 | tf_op jit(solution)/shard_map/add | solution.py:160
  93.5 2.1 %concatenate.18 = f32[8,4,6,2048]{3,2,1,0:T(8,128)} reshape(f32[192,32,64]{2,1,0:T(8,128)S(1)} %copy.57) | data formatting | bytes 3145728 | tf_op jit(solution)/shard_map/concatenate | solution.py:169
  95.6 2.5 %concatenate.21 = f32[8,4,6,2176]{3,2,1,0:T(8,128)S(1)} concatenate(f32[8,4,6,2048]{3,2,1,0:T(8,128)} %concatenate.18, f32[8,4,6,32]{3,2,1,0:T(8,128)S(1)} %concatenate.19, f32[8,4,6,1]{3,2,1,0:T(8,128)S(1)} %concatenate.22, f32[8,4,6,95]{3,2,1,0:T(8,128)S(1)} %broadcast_in_dim.41), dimensions={3} | concatenate | bytes 3342336 | tf_op jit(solution)/shard_map/concatenate | solution.py:169
  98.2 1.0 copy.60
  99.1 23.4 %all_to_all.15 = f32[8,4,6,2176]{3,0,2,1:T(8,128)S(1)} all-to-all(f32[8,4,6,2176]{3,0,2,1:T(8,128)S(1)} %copy.60), channel_id=1, replica_groups=mesh['x'=4,'core'=2,'z'=8,'y'=4] {'y'}, dimensions={1} | all-to-all | bytes 3342336 | tf_op jit(solution)/shard_map/all_to_all | solution.py:173
  122.6 0.1 reduce_sum.47
  122.7 0.1 copy.61
  122.8 17.6 %all_to_all.16 = f32[8,6,2176]{2,1,0:T(8,128)S(1)} all-to-all(f32[8,6,2176]{2,1,0:T(8,128)S(1)} %copy.61), channel_id=1, replica_groups=mesh['x'=4,'core'=2,'z'=8,'y'=4] {'z'}, dimensions={0} | all-to-all | bytes 835584 | tf_op jit(solution)/shard_map/all_to_all | solution.py:174
  140.5 18.5 %all-gather.1 = f32[8,6,2176]{2,1,0:T(8,128)S(1)} all-gather(f32[1,6,2176]{2,1,0:T(8,128)S(1)} %bitcast.25), channel_id=2, replica_groups=mesh['x'=4,'core'=2,'z'=8,'y'=4] {'x','core'}, dimensions={0}, use_global_device_ids=true | all-gather | bytes 470016 | tf_op jit(solution)/shard_map/all_gather | solution.py:175
  159.0 0.7 fusion.23
  159.7 0.1 div.21
  159.7 0.2 div.22
  160.0 0.6 slice_divide_fusion
  (10 shorter events, 0.1 us)
Async XLA Ops:
  0.6 16.0 %copy-start = (f32[64,32]{0,1:T(8,128)S(1)}, f32[64,32]{0,1:T(8,128)}, u32[]{:S(2)}) copy-start(f32[64,32]{0,1:T(8,128)} %param.9) | copy-start | bytes 24580
  0.6 16.0 %copy-start.6 = (f32[32]{0:T(128)S(1)}, f32[32]{0:T(128)}, u32[]{:S(2)}) copy-start(f32[32]{0:T(128)} %param.10) | copy-start | bytes 388
  0.7 16.0 %copy-start.8 = (s32[256]{0:T(256)S(1)}, s32[256]{0:T(256)}, u32[]{:S(2)}) copy-start(s32[256]{0:T(256)} %param.8) | copy-start | bytes 3076
  0.7 16.1 %copy-start.5 = (bf16[2048,256]{1,0:T(8,128)(2,1)S(1)}, bf16[2048,256]{1,0:T(8,128)(2,1)}, u32[]{:S(2)}) copy-start(bf16[2048,256]{1,0:T(8,128)(2,1)} %param.7) | copy-start | bytes 3145732
  2.7 38.4 %all-to-all-start = ((bf16[32,6,2048]{2,1,0:T(8,128)(2,1)}), bf16[32,6,2048]{2,1,0:T(8,128)(2,1)}, u32[]{:S(2)}, u32[]{:S(2)}) async-start(bf16[32,6,2048]{2,1,0:T(8,128)(2,1)} %broadcast_in_dim.20), calls=%async_computation | async-start | bytes 2097152 | tf_op jit(solution)/shard_map/all_to_all | solution.py:107
  46.9 2.4 %copy-start.1 = (bf16[192,32,64]{0,2,1:T(8,128)(2,1)S(1)}, bf16[192,32,64]{0,2,1:T(8,128)(2,1)}, u32[]{:S(2)}) copy-start(bf16[192,32,64]{0,2,1:T(8,128)(2,1)} %copy.49) | copy-start | bytes 2359300
  46.9 2.4 %copy-start.2 = (bf16[32,32,256]{2,1,0:T(8,128)(2,1)S(1)}, bf16[32,32,256]{2,1,0:T(8,128)(2,1)}, u32[]{:S(2)}) copy-start(bf16[32,32,256]{2,1,0:T(8,128)(2,1)} %get-tuple-element.9) | copy-start | bytes 1572868
  50.4 6.3 %copy-start.7 = (f32[192]{0:T(256)S(1)}, f32[192]{0:T(256)}, u32[]{:S(2)}) copy-start(f32[192]{0:T(256)} %param.11) | copy-start | bytes 2308
  57.7 10.8 %copy-start.4 = (f32[192,256]{1,0:T(8,128)S(1)}, f32[192,256]{1,0:T(8,128)}, u32[]{:S(2)}) copy-start(f32[192,256]{1,0:T(8,128)} %fusion.9.bias_ref) | copy-start | bytes 589828
  82.9 4.0 %copy-start.3 = (bf16[192,32,256]{2,1,0:T(8,128)(2,1)S(1)}, bf16[192,32,256]{2,1,0:T(8,128)(2,1)}, u32[]{:S(2)}) copy-start(bf16[192,32,256]{2,1,0:T(8,128)(2,1)} %get-tuple-element.5) | copy-start | bytes 9437188

commit v10 on v7

--- a/solution.py
+++ b/solution.py
@@ -12,7 +12,7 @@
 M = 32
 R = 128
 CLS_DEV = 6
-CLS_STEP = 24
+CLS_STEP = 48
 GRP = ("x", "core")
 DEV = ("z", "y")
 
@@ -78,9 +78,11 @@
 
 
 def spectra_kernel(
-    table_ref, real_ref, imag_ref, shift_ref, turn_ref, cos_ref, sin_ref, weight_ref
+    cols, table_ref, real_ref, imag_ref, bias_ref, norm_ref, turn_ref, cos_ref, sin_ref, weight_ref
 ):
-    responsibility = jnp.exp(block_scores(table_ref, real_ref, imag_ref, shift_ref))
+    norm_row = jnp.concatenate([norm_ref[...]] * (bias_ref.shape[1] // cols), 1)
+    scores = block_scores(table_ref, real_ref, imag_ref, bias_ref)
+    responsibility = jnp.exp(scores - norm_row)
     full = jnp.dot(
         turn_ref[...], responsibility.astype(jnp.bfloat16), preferred_element_type=jnp.float32
     )
@@ -134,15 +136,15 @@
         scratch_shapes=[pltpu.VMEM((1, columns), jnp.float32)] * 2,
         compiler_params=pltpu.CompilerParams(dimension_semantics=("arbitrary",)),
     )(table, crossed_real, crossed_imag, bias)
-    shift = bias - jnp.tile(log_norm, (1, classes_total))
     spectra_cos, spectra_sin, class_weight = pl.pallas_call(
-        spectra_kernel,
+        functools.partial(spectra_kernel, columns),
         grid=(steps,),
         in_specs=[
             table_spec,
             crossed_spec,
             crossed_spec,
             row_spec,
+            pl.BlockSpec((1, columns), lambda i: (0, 0)),
             pl.BlockSpec(turn.shape, lambda i: (0, 0)),
         ],
         out_specs=[crossed_spec, crossed_spec, row_spec],
@@ -152,7 +154,7 @@
             jax.ShapeDtypeStruct((1, width), jnp.float32),
         ],
         compiler_params=pltpu.CompilerParams(dimension_semantics=("arbitrary",)),
-    )(table, crossed_real, crossed_imag, shift, turn)
+    )(table, crossed_real, crossed_imag, bias, log_norm, turn)
 
     spectra_cos = spectra_cos.reshape(M, classes_total, columns)
     spectra_sin = spectra_sin.reshape(M, classes_total, columns)

time: 159 us -> 156 us (0.981)
    unnamed x30 -> x26, local copies, waits for them, and re-layouts: 18.1 us -> 17.2 us
where the time goes in v10:
time: 156 us
  blocking collectives  59.3 us (38%)
  local copies, waits for them, and re-layouts  31.2 us (20%)
  Pallas kernels  20.5 us (13%)
  waiting for transfers between devices  17.9 us (11%)
  starting transfers between devices  12.1 us (8%)
  matrix products  7.95 us (5%)
  other arithmetic  5.57 us (4%)
    all_to_all x1, blocking collectives, local(): own = jnp.sum(lax.all_to_all(packed, 'y', 1, 1, tiled=True), 1)  22.8 us
    all_to_all x1, blocking collectives, local(): own = jnp.sum(lax.all_to_all(own, 'z', 0, 0, tiled=True), 0)  19 us
    all_to_all x1, waiting for transfers between devices, local(): gathered = lax.all_to_all(copies, DEV, 0, 0, tiled=True)  17.9 us
    all_gather x1, blocking collectives, local(): own = jnp.sum(lax.all_gather(own, GRP, axis=0, tiled=False), 0)  17.5 us
    unnamed x26, local copies, waits for them, and re-layouts  17.2 us
    all_to_all x1, starting transfers between devices, local(): gathered = lax.all_to_all(copies, DEV, 0, 0, tiled=True)  12.1 us
    pallas_call x1, Pallas kernels, local(): pl.pallas_call(functools.partial(norm_kernel, columns), grid=(steps,), in...  10.4 us
    pallas_call x1, Pallas kernels, local(): pl.pallas_call(functools.partial(spectra_kernel, columns), grid=(steps,),...  10.1 us
  transfers between devices with their start and end apart: 1, of which 1 were waited for; matrix products, arithmetic and copies ran while one was open for 2% of the time, Pallas kernels for 0%

profile of v10, /device:TPU:1, one launch (start us, length us, event | category | flops | bytes accessed | tf_op | source)
XLA Modules:
  0.0 155.6 jit_solution(9886459471029546781)
XLA Ops:
  0.6 0.0 copy-start
  0.6 0.0 copy-start.6
  0.7 0.0 copy-start.8
  0.7 0.0 copy-start.4
  0.7 1.0 reshape.204
  1.6 0.3 broadcast_bitcast_fusion
  2.0 1.9 %reshape.233 = bf16[32,2,6144]{2,1,0:T(2,128)(2,1)} reshape(bf16[32,6,32,64]{3,2,1,0:T(8,128)(2,1)S(1)} %broadcast_bitcast_fusion) | data formatting | bytes 1572864
  3.9 12.1 %all-to-all-start = ((bf16[32,2,6144]{2,1,0:T(2,128)(2,1)}), bf16[32,2,6144]{2,1,0:T(2,128)(2,1)}, u32[]{:S(2)}, u32[]{:S(2)}) async-start(bf16[32,2,6144]{2,1,0:T(2,128)(2,1)} %reshape.233), calls=%async_computation | async-start | bytes 1572864 | tf_op jit(solution)/shard_map/all_to_all | solution.py:104
  16.0 0.1 multiply_convert_fusion.1
  16.1 0.7 copy.37.table_ref
  16.9 0.1 pad.2.clone
  17.0 0.1 pad.1.clone
  17.0 0.1 fusion.17
  17.1 0.7 maximum_maximum_fusion.turn_ref
  17.8 0.0 copy-done
  17.8 0.0 copy-done.6
  17.8 0.0 copy-done.8
  17.8 0.1 broadcast_divide_fusion
  18.0 0.0 copy-done.4
  18.0 0.3 fusion
  18.3 0.9 fusion.22
  19.2 17.9 %all-to-all-done = bf16[32,2,6144]{2,1,0:T(2,128)(2,1)} async-done(((bf16[32,2,6144]{2,1,0:T(2,128)(2,1)}), bf16[32,2,6144]{2,1,0:T(2,128)(2,1)}, u32[]{:S(2)}, u32[]{:S(2)}) %all-to-all-start) | async-done | bytes 786464 | tf_op jit(solution)/shard_map/all_to_all | solution.py:104
  37.1 3.0 %reshape.234 = bf16[32,6,32,64]{3,2,1,0:T(8,128)(2,1)S(1)} reshape(bf16[32,2,6144]{2,1,0:T(2,128)(2,1)} %all-to-all-done) | data formatting | bytes 1572864
  40.1 0.8 multiply_reduce_fusion
  40.9 2.2 %copy.34 = bf16[32,192,64]{1,2,0:T(8,128)(2,1)} copy(bf16[32,192,64]{2,0,1:T(8,128)(2,1)S(1)} %bitcast.54) | data formatting | bytes 1572864 | tf_op jit(solution)/shard_map/reshape | solution.py:105
  43.0 2.4 %convolution_convert_fusion.1 = bf16[32,256,192]{1,2,0:T(8,128)(2,1)S(1)} fusion(bf16[32,64,256]{2,1,0:T(8,128)(2,1)S(1)} %fusion, bf16[32,192,64]{1,2,0:T(8,128)(2,1)} %copy.34), kind=kOutput, calls=%fused_computation.2 | convolution fusion | flops 202899456 | bytes 4980736 | tf_op jit(solution)/shard_map/mkc,mcb->mkb/dot_general | solution.py:112
  45.4 0.0 copy-done.1
  45.4 0.0 copy-done.2
  45.4 1.0 convolution_convert_fusion
  46.4 3.5 %copy.44 = bf16[4,8,192,256]{3,1,2,0:T(8,128)(2,1)} copy(bf16[4,8,192,256]{3,2,1,0:T(8,128)(2,1)S(1)} %bitcast.57) | data formatting | bytes 6291456
  49.9 3.5 %copy.43 = bf16[4,8,192,256]{3,1,2,0:T(8,128)(2,1)} copy(bf16[4,8,192,256]{3,2,1,0:T(8,128)(2,1)S(1)} %bitcast.55) | data formatting | bytes 6291456
  53.4 0.0 copy-done.7
  53.4 0.4 fusion.2
  53.8 0.9 copy.45
  54.7 10.4 %shard_map.77.norm_ref = f32[1,256]{1,0:T(1,128)} custom-call(bf16[128,64]{1,0:T(8,128)(2,1)} %copy.37.table_ref, bf16[32,49152]{1,0:T(8,128)(2,1)} %bitcast.52, bf16[32,49152]{1,0:T(8,128)(2,1)} %bitcast.50, f32[1,49152]{1,0:T(1,128)} %bitcast.61), custom_call_target="tpu_custom_call" | custom-call | tf_op jit(solution)/shard_map/pallas_call | solution.py:130
  65.1 10.1 %shard_map.78 = (bf16[32,49152]{1,0:T(8,128)(2,1)}, bf16[32,49152]{1,0:T(8,128)(2,1)}, f32[1,49152]{1,0:T(1,128)}) custom-call(bf16[128,64]{1,0:T(8,128)(2,1)} %copy.37.table_ref, bf16[32,49152]{1,0:T(8,128)(2,1)} %bitcast.53, bf16[32,49152]{1,0:T(8,128)(2,1)} %bitcast.51, f32[1,49152]{1,0:T(1,128)} %bitcast.62, f32[1,256]{1,0:T(1,128)} %shard_map.77.norm_ref, ...), custom_call_target="tpu_custom_call" | custom-call | tf_op jit(solution)/shard_map/pallas_call | solution.py:139
  75.2 2.6 %copy.46 = bf16[4,8,192,256]{3,2,1,0:T(8,128)(2,1)S(1)} copy(bf16[4,8,192,256]{3,1,2,0:T(8,128)(2,1)} %bitcast.60) | data formatting | bytes 6291456
  77.9 0.0 copy-start.3
  77.9 1.1 fusion.23
  79.0 0.8 copy-done.3
  79.8 0.7 copy.47
  80.5 2.5 %add_bitcast_fusion = f32[192,32,64]{0,2,1:T(8,128)} fusion(f32[32,64,192]{2,1,0:T(8,128)S(1)} %fusion.23, bf16[32,192,256]{2,1,0:T(8,128)(2,1)S(1)} %bitcast.58, bf16[32,32,256]{2,1,0:T(8,128)(2,1)S(1)} %copy-done.2, bf16[32,32,256]{2,1,0:T(8,128)(2,1)S(1)} %get-tuple-element.8), kind=kOutput, calls=%fused_computation.5 | convolution fusion | flops 203816960 | bytes 7340032 | tf_op jit(solution)/shard_map/mkb,mcb->kmc/dot_general | solution.py:163
  83.0 3.2 %copy.38 = f32[192,32,64]{2,1,0:T(8,128)S(1)} copy(f32[192,32,64]{0,2,1:T(8,128)} %add_bitcast_fusion) | data formatting | bytes 3145728 | tf_op jit(solution)/shard_map/add | solution.py:161
  86.2 0.0 copy-start.5
  86.2 2.1 %concatenate.16 = f32[8,4,6,2048]{3,2,1,0:T(8,128)} reshape(f32[192,32,64]{2,1,0:T(8,128)S(1)} %copy.38) | data formatting | bytes 3145728 | tf_op jit(solution)/shard_map/concatenate | solution.py:170
  88.3 0.5 broadcast.237
  88.8 0.0 copy-done.5
  88.8 1.1 reduce.9
  89.9 0.1 dot_general.32
  89.9 0.4 fusion.4
  90.4 0.1 reshape.211
  90.4 0.1 reduce_sum.49
  90.6 0.2 concatenate.19
  90.8 2.5 %concatenate.18 = f32[8,4,6,2176]{3,2,1,0:T(8,128)S(1)} concatenate(f32[8,4,6,2048]{3,2,1,0:T(8,128)} %concatenate.16, f32[8,4,6,32]{3,2,1,0:T(8,128)S(1)} %fusion.4, f32[8,4,6,1]{3,2,1,0:T(8,128)S(1)} %concatenate.19, f32[8,4,6,95]{3,2,1,0:T(8,128)S(1)} %broadcast_in_dim.41), dimensions={3} | concatenate | bytes 3342336 | tf_op jit(solution)/shard_map/concatenate | solution.py:170
  93.3 1.0 copy.40
  94.3 22.8 %all_to_all.15 = f32[8,4,6,2176]{3,0,2,1:T(8,128)S(1)} all-to-all(f32[8,4,6,2176]{3,0,2,1:T(8,128)S(1)} %copy.40), channel_id=1, replica_groups=mesh['x'=4,'core'=2,'z'=8,'y'=4] {'y'}, dimensions={1} | all-to-all | bytes 3342336 | tf_op jit(solution)/shard_map/all_to_all | solution.py:174
  117.1 0.1 reduce_sum.50
  117.2 0.1 copy.41
  117.3 19.0 %all_to_all.16 = f32[8,6,2176]{2,1,0:T(8,128)S(1)} all-to-all(f32[8,6,2176]{2,1,0:T(8,128)S(1)} %copy.41), channel_id=1, replica_groups=mesh['x'=4,'core'=2,'z'=8,'y'=4] {'z'}, dimensions={0} | all-to-all | bytes 835584 | tf_op jit(solution)/shard_map/all_to_all | solution.py:175
  136.4 17.5 %all-gather.1 = f32[8,6,2176]{2,1,0:T(8,128)S(1)} all-gather(f32[1,6,2176]{2,1,0:T(8,128)S(1)} %bitcast.65), channel_id=2, replica_groups=mesh['x'=4,'core'=2,'z'=8,'y'=4] {'x','core'}, dimensions={0}, use_global_device_ids=true | all-gather | bytes 470016 | tf_op jit(solution)/shard_map/all_gather | solution.py:176
  153.9 0.7 fusion.19
  154.6 0.1 div.21
  154.7 0.2 div.22
  154.9 0.6 slice_divide_fusion
  (13 shorter events, 0.1 us)
Async XLA Ops:
  0.6 17.2 %copy-start = (f32[64,32]{0,1:T(8,128)S(1)}, f32[64,32]{0,1:T(8,128)}, u32[]{:S(2)}) copy-start(f32[64,32]{0,1:T(8,128)} %param.9) | copy-start | bytes 24580
  0.6 17.2 %copy-start.6 = (f32[32]{0:T(128)S(1)}, f32[32]{0:T(128)}, u32[]{:S(2)}) copy-start(f32[32]{0:T(128)} %param.10) | copy-start | bytes 388
  0.7 17.2 %copy-start.8 = (s32[256]{0:T(256)S(1)}, s32[256]{0:T(256)}, u32[]{:S(2)}) copy-start(s32[256]{0:T(256)} %param.8) | copy-start | bytes 3076
  0.7 17.3 %copy-start.4 = (bf16[2048,256]{1,0:T(8,128)(2,1)S(1)}, bf16[2048,256]{1,0:T(8,128)(2,1)}, u32[]{:S(2)}) copy-start(bf16[2048,256]{1,0:T(8,128)(2,1)} %param.7) | copy-start | bytes 3145732
  3.9 33.2 %all-to-all-start = ((bf16[32,2,6144]{2,1,0:T(2,128)(2,1)}), bf16[32,2,6144]{2,1,0:T(2,128)(2,1)}, u32[]{:S(2)}, u32[]{:S(2)}) async-start(bf16[32,2,6144]{2,1,0:T(2,128)(2,1)} %reshape.233), calls=%async_computation | async-start | bytes 1572864 | tf_op jit(solution)/shard_map/all_to_all | solution.py:104
  43.0 2.4 %copy-start.1 = (bf16[32,192,64]{1,2,0:T(8,128)(2,1)S(1)}, bf16[32,192,64]{1,2,0:T(8,128)(2,1)}, u32[]{:S(2)}) copy-start(bf16[32,192,64]{1,2,0:T(8,128)(2,1)} %copy.34) | copy-start | bytes 2359300
  43.0 2.4 %copy-start.2 = (bf16[32,32,256]{2,1,0:T(8,128)(2,1)S(1)}, bf16[32,32,256]{2,1,0:T(8,128)(2,1)}, u32[]{:S(2)}) copy-start(bf16[32,32,256]{2,1,0:T(8,128)(2,1)} %get-tuple-element.9) | copy-start | bytes 1572868
  49.9 3.5 %copy-start.7 = (f32[192]{0:T(256)S(1)}, f32[192]{0:T(256)}, u32[]{:S(2)}) copy-start(f32[192]{0:T(256)} %param.11) | copy-start | bytes 2308
  77.9 1.9 %copy-start.3 = (bf16[32,49152]{1,0:T(8,128)(2,1)S(1)}, bf16[32,49152]{1,0:T(8,128)(2,1)}, u32[]{:S(2)}) copy-start(bf16[32,49152]{1,0:T(8,128)(2,1)} %get-tuple-element.6) | copy-start | bytes 9437188
  86.2 2.6 %copy-start.5 = (f32[1,49152]{1,0:T(1,128)S(1)}, f32[1,49152]{1,0:T(1,128)}, u32[]{:S(2)}) copy-start(f32[1,49152]{1,0:T(1,128)} %get-tuple-element.7) | copy-start | bytes 589828

commit v11 on v10

--- a/solution.py
+++ b/solution.py
@@ -168,12 +168,20 @@
 
     width = numer_all.shape[1]
     packed = jnp.concatenate(
-        [numer_all, cycles_all, mass_all[:, None], jnp.zeros((classes_total, 95), jnp.float32)], 1
-    )
-    packed = packed.reshape(lax.axis_size("z"), lax.axis_size("y"), CLS_DEV, packed.shape[1])
+        [numer_all, cycles_all, mass_all[:, None], jnp.zeros((classes_total, 223), jnp.float32)], 1
+    )
+    core = lax.axis_index("core")
+    core_count = lax.axis_size("core")
+    half = packed.shape[1] // core_count
+    mine = lax.dynamic_slice_in_dim(packed, core * half, half, 1)
+    other = lax.dynamic_slice_in_dim(packed, (1 - core) * half, half, 1)
+    packed = mine + lax.ppermute(other, "core", [(0, 1), (1, 0)])
+    packed = packed.reshape(lax.axis_size("z"), lax.axis_size("y"), CLS_DEV, half)
     own = jnp.sum(lax.all_to_all(packed, "y", 1, 1, tiled=True), 1)
     own = jnp.sum(lax.all_to_all(own, "z", 0, 0, tiled=True), 0)
-    own = jnp.sum(lax.all_gather(own, GRP, axis=0, tiled=False), 0)
+    own = lax.all_gather(own, GRP, axis=0, tiled=False)
+    own = jnp.sum(own.reshape(lax.axis_size("x"), core_count, CLS_DEV, half), 0)
+    own = jnp.concatenate([own[0], own[1]], 1)
     numerator = own[:, :width]
     cycle_sum = own[:, width : width + Q]
     class_mass = own[:, width + Q]

time: 156 us -> 142 us (0.910)
  blocking collectives: 59.3 us -> 45.2 us
  local copies, waits for them, and re-layouts: 31.2 us -> 26.4 us
  starting transfers between devices: 12.1 us -> 15 us
  waiting for transfers between devices: 17.9 us -> 20 us
    all_to_all x1, blocking collectives: 22.8 us -> 16.1 us  [local(): own = jnp.sum(lax.all_to_all(packed, 'y', 1, 1, tiled=True), 1)]
    all_to_all x1, blocking collectives: 19 us -> 12.9 us  [local(): own = jnp.sum(lax.all_to_all(own, 'z', 0, 0, tiled=True), 0)]
    concatenate x4 -> x1, local copies, waits for them, and re-layouts: 5.8 us -> 1.14 us  [local(): jnp.concatenate([numer_all, cycles_all, mass_all[:, None], jnp.zeros((cla...]
    add x1 -> x0, local copies, waits for them, and re-layouts: 3.17 us -> none  [local(): jnp.einsum('mkb,mcb->kmc', spectra_cos, weighted, preferred_element_type=...]
    ppermute x0 -> x1, starting transfers between devices: none -> 2.88 us  [local(): packed = mine + lax.ppermute(other, 'core', [(0, 1), (1, 0)])]
    reshape x0 -> x3, local copies, waits for them, and re-layouts: none -> 2.34 us  [the longest x1 1.71 us: local(): numer_all = numer_all.reshape(classes_total, 2 * M * Q)]
    ppermute x0 -> x1, waiting for transfers between devices: none -> 2.05 us  [local(): packed = mine + lax.ppermute(other, 'core', [(0, 1), (1, 0)])]
    unnamed x26 -> x30, local copies, waits for them, and re-layouts: 17.2 us -> 17.2 us
  transfers between devices with their start and end apart: 1 -> 2, of which waited for: 1 -> 2; matrix products, arithmetic and copies ran while one was open for 2% -> 2% of each run, Pallas kernels for 0% -> 0%
where the time goes in v11:
time: 142 us
  blocking collectives  45.2 us (32%)
  local copies, waits for them, and re-layouts  26.4 us (19%)
  Pallas kernels  20.6 us (15%)
  waiting for transfers between devices  20 us (14%)
  starting transfers between devices  15 us (11%)
  matrix products  7.93 us (6%)
  other arithmetic  5.58 us (4%)
    all_to_all x1, waiting for transfers between devices, local(): gathered = lax.all_to_all(copies, DEV, 0, 0, tiled=True)  17.9 us
    unnamed x30, local copies, waits for them, and re-layouts  17.2 us
    all_gather x1, blocking collectives, local(): own = lax.all_gather(own, GRP, axis=0, tiled=False)  16.2 us
    all_to_all x1, blocking collectives, local(): own = jnp.sum(lax.all_to_all(packed, 'y', 1, 1, tiled=True), 1)  16.1 us
    all_to_all x1, blocking collectives, local(): own = jnp.sum(lax.all_to_all(own, 'z', 0, 0, tiled=True), 0)  12.9 us
    all_to_all x1, starting transfers between devices, local(): gathered = lax.all_to_all(copies, DEV, 0, 0, tiled=True)  12.1 us
    pallas_call x1, Pallas kernels, local(): pl.pallas_call(functools.partial(norm_kernel, columns), grid=(steps,), in...  10.5 us
    pallas_call x1, Pallas kernels, local(): pl.pallas_call(functools.partial(spectra_kernel, columns), grid=(steps,),...  10.1 us
  transfers between devices with their start and end apart: 2, of which 2 were waited for; matrix products, arithmetic and copies ran while one was open for 2% of the time, Pallas kernels for 0%

profile of v11, /device:TPU:1, one launch (start us, length us, event | category | flops | bytes accessed | tf_op | source)
XLA Modules:
  0.0 141.7 jit_solution(10177339799891527516)
XLA Ops:
  0.6 0.0 copy-start
  0.6 0.9 reshape.203
  1.5 0.3 broadcast_bitcast_fusion
  1.9 0.0 copy-start.8
  1.9 0.0 copy-start.10
  1.9 0.0 copy-start.5
  1.9 1.9 %reshape.232 = bf16[32,2,6144]{2,1,0:T(2,128)(2,1)} reshape(bf16[32,6,32,64]{3,2,1,0:T(8,128)(2,1)S(1)} %broadcast_bitcast_fusion) | data formatting | bytes 1572864
  3.8 12.1 %all-to-all-start = ((bf16[32,2,6144]{2,1,0:T(2,128)(2,1)}), bf16[32,2,6144]{2,1,0:T(2,128)(2,1)}, u32[]{:S(2)}, u32[]{:S(2)}) async-start(bf16[32,2,6144]{2,1,0:T(2,128)(2,1)} %reshape.232), calls=%async_computation | async-start | bytes 1572864 | tf_op jit(solution)/shard_map/all_to_all | solution.py:104
  16.0 0.1 multiply_convert_fusion.1
  16.1 0.7 copy.42.table_ref
  16.8 0.1 pad.4.clone
  16.9 0.1 pad.3.clone
  17.0 0.1 fusion.14
  17.1 0.7 maximum_maximum_fusion.turn_ref
  17.7 0.0 copy-done
  17.7 0.0 copy-done.8
  17.7 0.0 copy-done.10
  17.8 0.1 broadcast_divide_fusion
  17.9 0.0 copy-start.7
  17.9 0.0 copy-done.5
  17.9 0.3 fusion
  18.2 0.9 fusion.23
  19.1 17.9 %all-to-all-done = bf16[32,2,6144]{2,1,0:T(2,128)(2,1)} async-done(((bf16[32,2,6144]{2,1,0:T(2,128)(2,1)}), bf16[32,2,6144]{2,1,0:T(2,128)(2,1)}, u32[]{:S(2)}, u32[]{:S(2)}) %all-to-all-start) | async-done | bytes 786464 | tf_op jit(solution)/shard_map/all_to_all | solution.py:104
  37.0 3.0 %reshape.233 = bf16[32,6,32,64]{3,2,1,0:T(8,128)(2,1)S(1)} reshape(bf16[32,2,6144]{2,1,0:T(2,128)(2,1)} %all-to-all-done) | data formatting | bytes 1572864
  40.0 0.8 multiply_reduce_fusion
  40.8 2.2 %copy.39 = bf16[32,192,64]{1,2,0:T(8,128)(2,1)} copy(bf16[32,192,64]{2,0,1:T(8,128)(2,1)S(1)} %bitcast.55) | data formatting | bytes 1572864 | tf_op jit(solution)/shard_map/reshape | solution.py:105
  42.9 2.4 %convolution_convert_fusion.1 = bf16[32,256,192]{1,2,0:T(8,128)(2,1)S(1)} fusion(bf16[32,64,256]{2,1,0:T(8,128)(2,1)S(1)} %fusion, bf16[32,192,64]{1,2,0:T(8,128)(2,1)} %copy.39), kind=kOutput, calls=%fused_computation.2 | convolution fusion | flops 202899456 | bytes 4980736 | tf_op jit(solution)/shard_map/mkc,mcb->mkb/dot_general | solution.py:112
  45.3 0.0 copy-done.1
  45.3 1.0 convolution_convert_fusion
  46.4 3.5 %copy.50 = bf16[4,8,192,256]{3,1,2,0:T(8,128)(2,1)} copy(bf16[4,8,192,256]{3,2,1,0:T(8,128)(2,1)S(1)} %bitcast.58) | data formatting | bytes 6291456
  49.9 3.5 %copy.49 = bf16[4,8,192,256]{3,1,2,0:T(8,128)(2,1)} copy(bf16[4,8,192,256]{3,2,1,0:T(8,128)(2,1)S(1)} %bitcast.56) | data formatting | bytes 6291456
  53.4 0.4 fusion.2
  53.7 0.9 copy.51
  54.6 10.5 %shard_map.77.norm_ref = f32[1,256]{1,0:T(1,128)} custom-call(bf16[128,64]{1,0:T(8,128)(2,1)} %copy.42.table_ref, bf16[32,49152]{1,0:T(8,128)(2,1)} %bitcast.53, bf16[32,49152]{1,0:T(8,128)(2,1)} %bitcast.51, f32[1,49152]{1,0:T(1,128)} %bitcast.63), custom_call_target="tpu_custom_call" | custom-call | tf_op jit(solution)/shard_map/pallas_call | solution.py:130
  65.1 10.1 %shard_map.78 = (bf16[32,49152]{1,0:T(8,128)(2,1)}, bf16[32,49152]{1,0:T(8,128)(2,1)}, f32[1,49152]{1,0:T(1,128)}) custom-call(bf16[128,64]{1,0:T(8,128)(2,1)} %copy.42.table_ref, bf16[32,49152]{1,0:T(8,128)(2,1)} %bitcast.54, bf16[32,49152]{1,0:T(8,128)(2,1)} %bitcast.52, f32[1,49152]{1,0:T(1,128)} %bitcast.64, f32[1,256]{1,0:T(1,128)} %shard_map.77.norm_ref, ...), custom_call_target="tpu_custom_call" | custom-call | tf_op jit(solution)/shard_map/pallas_call | solution.py:139
  75.2 2.6 %copy.52 = bf16[4,8,192,256]{3,2,1,0:T(8,128)(2,1)S(1)} copy(bf16[4,8,192,256]{3,1,2,0:T(8,128)(2,1)} %bitcast.62) | data formatting | bytes 6291456
  77.9 1.1 fusion.24
  79.0 0.8 copy-done.4
  79.7 0.7 copy.53
  80.5 1.1 convolution_add_fusion
  81.6 1.7 %copy.43 = f32[192,2048]{1,0:T(8,128)} copy(f32[192,2048]{0,1:T(8,128)S(1)} %bitcast.60) | data formatting | bytes 3145728 | tf_op jit(solution)/shard_map/reshape | solution.py:164
  83.3 0.5 broadcast.234
  83.8 0.0 copy-done.6
  83.8 1.1 reduce.6
  85.0 0.1 reshape.211
  85.0 1.8 %fusion.20 = f32[192,32]{1,0:T(8,128)} fusion(f32[192,256]{1,0:T(8,128)S(1)} %reshape.211, f32[32,256]{1,0:T(8,128)} %copy-done.7, f32[32]{0:T(128)} %param.10), kind=kOutput, calls=%fused_computation.47 | convolution fusion | flops 18890752 | bytes 254080 | tf_op jit(solution)/shard_map/dot_general | solution.py:166
  86.8 0.1 reduce_sum.49
  86.9 0.8 copy.45
  87.7 0.0 copy-done.2
  87.7 1.1 concatenate.14
  88.8 0.1 constant_dynamic-slice_fusion
  88.9 2.9 %collective-permute-start = (f32[192,1152]{1,0:T(8,128)S(1)}, f32[192,1152]{1,0:T(8,128)S(1)}, u32[]{:S(2)}, u32[]{:S(2)}) collective-permute-start(f32[192,1152]{1,0:T(8,128)S(1)} %constant_dynamic-slice_fusion), channel_id=1, source_target_pairs={{0,32},{32,0},{1,33},{33,1},{2,34},{34,2},{3,35},{35,3},{4,36},{36... | collective-permute-start | bytes 2654216 | tf_op jit(solution)/shard_map/ppermute | solution.py:178
  91.8 2.1 %collective-permute-done = f32[192,1152]{1,0:T(8,128)S(1)} collective-permute-done((f32[192,1152]{1,0:T(8,128)S(1)}, f32[192,1152]{1,0:T(8,128)S(1)}, u32[]{:S(2)}, u32[]{:S(2)}) %collective-permute-start) | collective-permute-done | bytes 884768 | tf_op jit(solution)/shard_map/ppermute | solution.py:178
  93.9 0.1 dynamic-slice_add_fusion
  94.0 0.1 reshape.212
  94.1 0.5 copy.46
  94.6 16.1 %all_to_all.15 = f32[8,4,6,1152]{3,0,2,1:T(8,128)S(1)} all-to-all(f32[8,4,6,1152]{3,0,2,1:T(8,128)S(1)} %copy.46), channel_id=1, replica_groups=mesh['x'=4,'core'=2,'z'=8,'y'=4] {'y'}, dimensions={1} | all-to-all | bytes 1769472 | tf_op jit(solution)/shard_map/all_to_all | solution.py:180
  110.8 0.1 copy.47
  110.9 12.9 %all_to_all.16 = f32[8,6,1152]{2,1,0:T(8,128)S(1)} all-to-all(f32[8,6,1152]{2,1,0:T(8,128)S(1)} %copy.47), channel_id=1, replica_groups=mesh['x'=4,'core'=2,'z'=8,'y'=4] {'z'}, dimensions={0} | all-to-all | bytes 442368 | tf_op jit(solution)/shard_map/all_to_all | solution.py:181
  123.8 16.2 %all-gather.1 = f32[8,6,1152]{2,1,0:T(8,128)S(1)} all-gather(f32[1,6,1152]{2,1,0:T(8,128)S(1)} %bitcast.69), channel_id=2, replica_groups=mesh['x'=4,'core'=2,'z'=8,'y'=4] {'x','core'}, dimensions={0}, use_global_device_ids=true | all-gather | bytes 248832 | tf_op jit(solution)/shard_map/all_gather | solution.py:182
  140.0 0.7 fusion.16
  140.7 0.1 div.21
  140.8 0.2 div.22
  141.0 0.7 fusion.4
  (21 shorter events, 0.2 us)
Async XLA Ops:
  0.6 17.1 %copy-start = (f32[64,32]{0,1:T(8,128)S(1)}, f32[64,32]{0,1:T(8,128)}, u32[]{:S(2)}) copy-start(f32[64,32]{0,1:T(8,128)} %param.9) | copy-start | bytes 24580
  1.9 15.9 %copy-start.8 = (f32[32]{0:T(128)S(1)}, f32[32]{0:T(128)}, u32[]{:S(2)}) copy-start(f32[32]{0:T(128)} %param.10) | copy-start | bytes 388
  1.9 15.9 %copy-start.10 = (s32[256]{0:T(256)S(1)}, s32[256]{0:T(256)}, u32[]{:S(2)}) copy-start(s32[256]{0:T(256)} %param.8) | copy-start | bytes 3076
  1.9 16.0 %copy-start.5 = (bf16[2048,256]{1,0:T(8,128)(2,1)S(1)}, bf16[2048,256]{1,0:T(8,128)(2,1)}, u32[]{:S(2)}) copy-start(bf16[2048,256]{1,0:T(8,128)(2,1)} %param.7) | copy-start | bytes 3145732
  3.8 33.2 %all-to-all-start = ((bf16[32,2,6144]{2,1,0:T(2,128)(2,1)}), bf16[32,2,6144]{2,1,0:T(2,128)(2,1)}, u32[]{:S(2)}, u32[]{:S(2)}) async-start(bf16[32,2,6144]{2,1,0:T(2,128)(2,1)} %reshape.232), calls=%async_computation | async-start | bytes 1572864 | tf_op jit(solution)/shard_map/all_to_all | solution.py:104
  17.9 35.4 %copy-start.7 = (f32[32,256]{1,0:T(8,128)}, f32[32,256]{1,0:T(8,128)S(1)}, u32[]{:S(2)}) copy-start(f32[32,256]{1,0:T(8,128)S(1)} %get-tuple-element.15) | copy-start | bytes 98308
  42.9 2.4 %copy-start.1 = (bf16[32,192,64]{1,2,0:T(8,128)(2,1)S(1)}, bf16[32,192,64]{1,2,0:T(8,128)(2,1)}, u32[]{:S(2)}) copy-start(bf16[32,192,64]{1,2,0:T(8,128)(2,1)} %copy.39) | copy-start | bytes 2359300
  42.9 2.4 %copy-start.3 = (bf16[32,32,256]{2,1,0:T(8,128)(2,1)S(1)}, bf16[32,32,256]{2,1,0:T(8,128)(2,1)}, u32[]{:S(2)}) copy-start(bf16[32,32,256]{2,1,0:T(8,128)(2,1)} %get-tuple-element.9) | copy-start | bytes 1572868
  49.9 3.5 %copy-start.9 = (f32[192]{0:T(256)S(1)}, f32[192]{0:T(256)}, u32[]{:S(2)}) copy-start(f32[192]{0:T(256)} %param.11) | copy-start | bytes 2308
  77.8 1.9 %copy-start.4 = (bf16[32,49152]{1,0:T(8,128)(2,1)S(1)}, bf16[32,49152]{1,0:T(8,128)(2,1)}, u32[]{:S(2)}) copy-start(bf16[32,49152]{1,0:T(8,128)(2,1)} %get-tuple-element.6) | copy-start | bytes 9437188
  81.6 2.2 %copy-start.6 = (f32[1,49152]{1,0:T(1,128)S(1)}, f32[1,49152]{1,0:T(1,128)}, u32[]{:S(2)}) copy-start(f32[1,49152]{1,0:T(1,128)} %get-tuple-element.7) | copy-start | bytes 589828
  83.3 4.4 %copy-start.2 = (f32[192,2048]{1,0:T(8,128)S(1)}, f32[192,2048]{1,0:T(8,128)}, u32[]{:S(2)}) copy-start(f32[192,2048]{1,0:T(8,128)} %copy.43) | copy-start | bytes 4718596
  88.9 4.9 %collective-permute-start = (f32[192,1152]{1,0:T(8,128)S(1)}, f32[192,1152]{1,0:T(8,128)S(1)}, u32[]{:S(2)}, u32[]{:S(2)}) collective-permute-start(f32[192,1152]{1,0:T(8,128)S(1)} %constant_dynamic-slice_fusion), channel_id=1, source_target_pairs={{0,32},{32,0},{1,33},{33,1},{2,34},{34,2},{3,35},{35,3},{4,36},{36... | collective-permute-start | bytes 2654216 | tf_op jit(solution)/shard_map/ppermute | solution.py:178

commit v12 on v11

--- a/solution.py
+++ b/solution.py
@@ -99,9 +99,16 @@
     dev_count = lax.axis_size(DEV)
     classes_total = CLS_DEV * dev_count
 
+    core = lax.axis_index("core")
     own_rows = jnp.transpose(references.reshape(CLS_DEV, M, 2 * Q), (1, 0, 2))
-    copies = jnp.broadcast_to(own_rows[None], (dev_count,) + own_rows.shape)
+    freq_half = M // 2
+    own_half = lax.dynamic_slice_in_dim(own_rows, core * freq_half, freq_half, 0)
+    copies = jnp.broadcast_to(own_half[None], (dev_count,) + own_half.shape)
     gathered = lax.all_to_all(copies, DEV, 0, 0, tiled=True)
+    partner = lax.ppermute(gathered, "core", [(0, 1), (1, 0)])
+    low = jnp.where(core == 0, gathered, partner)
+    high = jnp.where(core == 0, partner, gathered)
+    gathered = jnp.concatenate([low, high], 1)
     grid_rows = jnp.transpose(gathered, (1, 0, 2, 3)).reshape(M, classes_total, 2 * Q)
     factor = jnp.where(jnp.arange(M) == 0, 1.0, 2.0).astype(jnp.float32)
     squares = jnp.sum(grid_rows.astype(jnp.float32) ** 2 * factor[:, None, None], axis=0)
@@ -170,7 +177,6 @@
     packed = jnp.concatenate(
         [numer_all, cycles_all, mass_all[:, None], jnp.zeros((classes_total, 223), jnp.float32)], 1
     )
-    core = lax.axis_index("core")
     core_count = lax.axis_size("core")
     half = packed.shape[1] // core_count
     mine = lax.dynamic_slice_in_dim(packed, core * half, half, 1)

time: 142 us -> 132 us (0.930)
  waiting for transfers between devices: 20 us -> 14.8 us
  local copies, waits for them, and re-layouts: 26.4 us -> 23 us
  matrix products: 7.93 us -> 5.88 us
    all_to_all x1, waiting for transfers between devices: 17.9 us -> 11.6 us  [local(): gathered = lax.all_to_all(copies, DEV, 0, 0, tiled=True)]
    unnamed x30 -> x20, local copies, waits for them, and re-layouts: 17.2 us -> 13.7 us
    ppermute x0 -> x1, starting transfers between devices: none -> 2.76 us  [local(): partner = lax.ppermute(gathered, 'core', [(0, 1), (1, 0)])]
    ppermute x1, starting transfers between devices: 2.88 us -> 0.47 us  [local(): packed = mine + lax.ppermute(other, 'core', [(0, 1), (1, 0)])]
    concatenate x0 -> x1, other arithmetic: none -> 1.58 us  [local(): gathered = jnp.concatenate([low, high], 1)]
  transfers between devices with their start and end apart: 2 -> 3, of which waited for: 2 -> 3; matrix products, arithmetic and copies ran while one was open for 2% -> 2% of each run, Pallas kernels for 0% -> 0%
where the time goes in v12:
time: 132 us; the launch traced here: 131 us
  blocking collectives  44.5 us (34%)
  local copies, waits for them, and re-layouts  23 us (17%)
  Pallas kernels  20.3 us (15%)
  starting transfers between devices  15.3 us (12%)
  waiting for transfers between devices  14.8 us (11%)
  other arithmetic  6.59 us (5%)
  matrix products  5.88 us (4%)
    all_gather x1, blocking collectives, local(): own = lax.all_gather(own, GRP, axis=0, tiled=False)  16.2 us
    all_to_all x1, blocking collectives, local(): own = jnp.sum(lax.all_to_all(packed, 'y', 1, 1, tiled=True), 1)  15.3 us
    unnamed x20, local copies, waits for them, and re-layouts  13.7 us
    all_to_all x1, blocking collectives, local(): own = jnp.sum(lax.all_to_all(own, 'z', 0, 0, tiled=True), 0)  13 us
    all_to_all x1, starting transfers between devices, local(): gathered = lax.all_to_all(copies, DEV, 0, 0, tiled=True)  12 us
    all_to_all x1, waiting for transfers between devices, local(): gathered = lax.all_to_all(copies, DEV, 0, 0, tiled=True)  11.6 us
    pallas_call x1, Pallas kernels, local(): pl.pallas_call(functools.partial(norm_kernel, columns), grid=(steps,), in...  10.4 us
    pallas_call x1, Pallas kernels, local(): pl.pallas_call(functools.partial(spectra_kernel, columns), grid=(steps,),...  9.92 us
  transfers between devices with their start and end apart: 3, of which 3 were waited for; matrix products, arithmetic and copies ran while one was open for 2% of the time, Pallas kernels for 0%

profile of v12, /device:TPU:1, one launch (start us, length us, event | category | flops | bytes accessed | tf_op | source)
XLA Modules:
  0.0 131.3 jit_solution(1970371757324860476)
XLA Ops:
  0.6 0.0 copy-start
  0.6 0.0 copy-start.2
  0.7 1.0 reshape.203
  1.6 0.1 broadcast_bitcast_fusion
  1.7 1.2 reshape.232
  2.9 12.0 %all-to-all-start = ((bf16[32,2,3072]{2,1,0:T(2,128)(2,1)}), bf16[32,2,3072]{2,1,0:T(2,128)(2,1)S(1)}, u32[]{:S(2)}, u32[]{:S(2)}) async-start(bf16[32,2,3072]{2,1,0:T(2,128)(2,1)} %reshape.232), calls=%async_computation | async-start | bytes 786432 | tf_op jit(solution)/shard_map/all_to_all | solution.py:107
  15.0 0.1 multiply_convert_fusion.1
  15.1 0.7 copy.42.table_ref
  15.8 0.1 pad.4.clone
  15.9 0.1 pad.3.clone
  16.0 0.1 fusion.14
  16.1 0.0 copy-done
  16.1 0.8 broadcast_divide_fusion
  16.9 0.0 copy-done.2
  16.9 0.3 fusion
  17.2 11.6 %all-to-all-done = bf16[32,2,3072]{2,1,0:T(2,128)(2,1)S(1)} async-done(((bf16[32,2,3072]{2,1,0:T(2,128)(2,1)}), bf16[32,2,3072]{2,1,0:T(2,128)(2,1)S(1)}, u32[]{:S(2)}, u32[]{:S(2)}) %all-to-all-start) | async-done | bytes 393248 | tf_op jit(solution)/shard_map/all_to_all | solution.py:107
  28.8 0.5 reshape.233
  29.2 2.8 %collective-permute-start = (bf16[32,16,6,64]{3,1,2,0:T(8,128)(2,1)S(1)}, bf16[32,16,6,64]{3,1,2,0:T(8,128)(2,1)S(1)}, u32[]{:S(2)}, u32[]{:S(2)}) collective-permute-start(bf16[32,16,6,64]{3,1,2,0:T(8,128)(2,1)S(1)} %bitcast.62), channel_id=1, source_target_pairs={{0,32},{32,0},{1,33},{33,1},{2,34},{34,2},{3,35},{35,3},{4,36},{36... | collective-permute-start | bytes 1179656 | tf_op jit(solution)/shard_map/ppermute | solution.py:108
  32.0 0.7 maximum_maximum_fusion.turn_ref
  32.7 0.1 fusion.23
  32.8 1.2 collective-permute-done
  33.9 0.1 broadcast_select_fusion.1
  34.0 1.6 %pad_maximum_fusion = bf16[32,32,6,64]{3,1,2,0:T(8,128)(2,1)} fusion(bf16[32,16,6,64]{3,1,2,0:T(8,128)(2,1)S(1)} %get-tuple-element.9, bf16[32,16,6,64]{3,1,2,0:T(8,128)(2,1)S(1)} %get-tuple-element.8), kind=kLoop, calls=%fused_computation.6 | loop fusion | flops 1572864 | bytes 1572864 | tf_op jit(solution)/shard_map/concatenate | solution.py:111
  35.6 0.9 multiply_reduce_fusion
  36.5 2.4 %copy.39 = bf16[32,192,64]{1,2,0:T(8,128)(2,1)S(1)} copy(bf16[32,192,64]{2,0,1:T(8,128)(2,1)} %bitcast.59) | data formatting | bytes 1572864 | tf_op jit(solution)/shard_map/reshape | solution.py:112
  38.9 1.0 convolution_convert_fusion.1
  39.9 1.0 convolution_convert_fusion
  41.0 3.5 %copy.50 = bf16[4,8,192,256]{3,1,2,0:T(8,128)(2,1)} copy(bf16[4,8,192,256]{3,2,1,0:T(8,128)(2,1)S(1)} %bitcast.56) | data formatting | bytes 6291456
  44.5 3.5 %copy.49 = bf16[4,8,192,256]{3,1,2,0:T(8,128)(2,1)} copy(bf16[4,8,192,256]{3,2,1,0:T(8,128)(2,1)S(1)} %bitcast.54) | data formatting | bytes 6291456
  47.9 0.0 copy-done.4
  47.9 0.0 copy-done.5
  48.0 0.4 fusion.2
  48.3 0.9 copy.51
  49.2 10.4 %shard_map.77.norm_ref = f32[1,256]{1,0:T(1,128)} custom-call(bf16[128,64]{1,0:T(8,128)(2,1)} %copy.42.table_ref, bf16[32,49152]{1,0:T(8,128)(2,1)} %bitcast.52, bf16[32,49152]{1,0:T(8,128)(2,1)} %bitcast.50, f32[1,49152]{1,0:T(1,128)} %bitcast.63), custom_call_target="tpu_custom_call" | custom-call | tf_op jit(solution)/shard_map/pallas_call | solution.py:137
  59.7 9.9 %shard_map.78 = (bf16[32,49152]{1,0:T(8,128)(2,1)}, bf16[32,49152]{1,0:T(8,128)(2,1)}, f32[1,49152]{1,0:T(1,128)}) custom-call(bf16[128,64]{1,0:T(8,128)(2,1)} %copy.42.table_ref, bf16[32,49152]{1,0:T(8,128)(2,1)} %bitcast.53, bf16[32,49152]{1,0:T(8,128)(2,1)} %bitcast.51, f32[1,49152]{1,0:T(1,128)} %bitcast.64, f32[1,256]{1,0:T(1,128)} %shard_map.77.norm_ref, ...), custom_call_target="tpu_custom_call" | custom-call | tf_op jit(solution)/shard_map/pallas_call | solution.py:146
  69.6 2.6 %copy.52 = bf16[4,8,192,256]{3,2,1,0:T(8,128)(2,1)S(1)} copy(bf16[4,8,192,256]{3,1,2,0:T(8,128)(2,1)} %bitcast.61) | data formatting | bytes 6291456
  72.2 0.0 copy-start.1
  72.2 1.1 fusion.24
  73.3 0.8 copy-done.1
  74.1 0.7 copy.53
  74.8 1.1 convolution_add_fusion
  76.0 1.7 %copy.43 = f32[192,2048]{1,0:T(8,128)} copy(f32[192,2048]{0,1:T(8,128)S(1)} %bitcast.58) | data formatting | bytes 3145728 | tf_op jit(solution)/shard_map/reshape | solution.py:171
  77.7 0.5 broadcast.234
  78.2 0.0 copy-done.3
  78.2 1.1 reduce.6
  79.3 0.1 reshape.211
  79.4 0.4 fusion.20
  79.8 0.1 reduce_sum.49
  79.9 0.1 copy.45
  80.0 1.5 %concatenate.18 = f32[192,2304]{1,0:T(8,128)S(1)} concatenate(f32[192,2048]{1,0:T(8,128)} %copy.43, f32[192,32]{1,0:T(8,128)S(1)} %fusion.20, f32[192,1]{1,0:T(8,128)S(1)} %copy.45, f32[192,223]{1,0:T(8,128)S(1)} %broadcast_in_dim.44), dimensions={1} | concatenate | bytes 3538944 | tf_op jit(solution)/shard_map/concatenate | solution.py:177
  81.6 0.1 constant_dynamic-slice_fusion
  81.6 0.5 collective-permute-start.1
  82.1 2.1 %collective-permute-done.1 = f32[192,1152]{1,0:T(8,128)S(1)} collective-permute-done((f32[192,1152]{1,0:T(8,128)S(1)}, f32[192,1152]{1,0:T(8,128)S(1)}, u32[]{:S(2)}, u32[]{:S(2)}) %collective-permute-start.1) | collective-permute-done | bytes 884768 | tf_op jit(solution)/shard_map/ppermute | solution.py:184
  84.2 0.1 dynamic-slice_add_fusion
  84.3 0.1 reshape.212
  84.4 0.5 copy.46
  84.9 15.3 %all_to_all.15 = f32[8,4,6,1152]{3,0,2,1:T(8,128)S(1)} all-to-all(f32[8,4,6,1152]{3,0,2,1:T(8,128)S(1)} %copy.46), channel_id=1, replica_groups=mesh['x'=4,'core'=2,'z'=8,'y'=4] {'y'}, dimensions={1} | all-to-all | bytes 1769472 | tf_op jit(solution)/shard_map/all_to_all | solution.py:186
  100.3 0.1 copy.47
  100.4 13.0 %all_to_all.16 = f32[8,6,1152]{2,1,0:T(8,128)S(1)} all-to-all(f32[8,6,1152]{2,1,0:T(8,128)S(1)} %copy.47), channel_id=1, replica_groups=mesh['x'=4,'core'=2,'z'=8,'y'=4] {'z'}, dimensions={0} | all-to-all | bytes 442368 | tf_op jit(solution)/shard_map/all_to_all | solution.py:187
  113.4 16.2 %all-gather.1 = f32[8,6,1152]{2,1,0:T(8,128)S(1)} all-gather(f32[1,6,1152]{2,1,0:T(8,128)S(1)} %bitcast.68), channel_id=2, replica_groups=mesh['x'=4,'core'=2,'z'=8,'y'=4] {'x','core'}, dimensions={0}, use_global_device_ids=true | all-gather | bytes 248832 | tf_op jit(solution)/shard_map/all_gather | solution.py:188
  129.7 0.7 fusion.16
  130.3 0.1 div.21
  130.4 0.2 div.22
  130.6 0.7 fusion.4
  (16 shorter events, 0.2 us)
Async XLA Ops:
  0.6 15.4 %copy-start = (f32[64,32]{0,1:T(8,128)S(1)}, f32[64,32]{0,1:T(8,128)}, u32[]{:S(2)}) copy-start(f32[64,32]{0,1:T(8,128)} %param.9) | copy-start | bytes 24580
  0.6 16.3 %copy-start.2 = (bf16[2048,256]{1,0:T(8,128)(2,1)S(1)}, bf16[2048,256]{1,0:T(8,128)(2,1)}, u32[]{:S(2)}) copy-start(bf16[2048,256]{1,0:T(8,128)(2,1)} %param.7) | copy-start | bytes 3145732
  2.9 25.8 %all-to-all-start = ((bf16[32,2,3072]{2,1,0:T(2,128)(2,1)}), bf16[32,2,3072]{2,1,0:T(2,128)(2,1)S(1)}, u32[]{:S(2)}, u32[]{:S(2)}) async-start(bf16[32,2,3072]{2,1,0:T(2,128)(2,1)} %reshape.232), calls=%async_computation | async-start | bytes 786432 | tf_op jit(solution)/shard_map/all_to_all | solution.py:107
  29.2 4.7 %collective-permute-start = (bf16[32,16,6,64]{3,1,2,0:T(8,128)(2,1)S(1)}, bf16[32,16,6,64]{3,1,2,0:T(8,128)(2,1)S(1)}, u32[]{:S(2)}, u32[]{:S(2)}) collective-permute-start(bf16[32,16,6,64]{3,1,2,0:T(8,128)(2,1)S(1)} %bitcast.62), channel_id=1, source_target_pairs={{0,32},{32,0},{1,33},{33,1},{2,34},{34,2},{3,35},{35,3},{4,36},{36... | collective-permute-start | bytes 1179656 | tf_op jit(solution)/shard_map/ppermute | solution.py:108
  44.5 3.5 %copy-start.4 = (f32[32]{0:T(128)S(1)}, f32[32]{0:T(128)}, u32[]{:S(2)}) copy-start(f32[32]{0:T(128)} %param.10) | copy-start | bytes 388
  44.5 3.5 %copy-start.5 = (f32[192]{0:T(256)S(1)}, f32[192]{0:T(256)}, u32[]{:S(2)}) copy-start(f32[192]{0:T(256)} %param.11) | copy-start | bytes 2308
  72.2 1.9 %copy-start.1 = (bf16[32,49152]{1,0:T(8,128)(2,1)S(1)}, bf16[32,49152]{1,0:T(8,128)(2,1)}, u32[]{:S(2)}) copy-start(bf16[32,49152]{1,0:T(8,128)(2,1)} %get-tuple-element.6) | copy-start | bytes 9437188
  76.0 2.2 %copy-start.3 = (f32[1,49152]{1,0:T(1,128)S(1)}, f32[1,49152]{1,0:T(1,128)}, u32[]{:S(2)}) copy-start(f32[1,49152]{1,0:T(1,128)} %get-tuple-element.7) | copy-start | bytes 589828
  81.6 2.5 %collective-permute-start.1 = (f32[192,1152]{1,0:T(8,128)S(1)}, f32[192,1152]{1,0:T(8,128)S(1)}, u32[]{:S(2)}, u32[]{:S(2)}) collective-permute-start(f32[192,1152]{1,0:T(8,128)S(1)} %constant_dynamic-slice_fusion), channel_id=1, source_target_pairs={{0,32},{32,0},{1,33},{33,1},{2,34},{34,2},{3,35},{35,3},{4,36},{36... | collective-permute-start | bytes 2654216 | tf_op jit(solution)/shard_map/ppermute | solution.py:184

commit v13 on v12

--- a/solution.py
+++ b/solution.py
@@ -104,12 +104,11 @@
     freq_half = M // 2
     own_half = lax.dynamic_slice_in_dim(own_rows, core * freq_half, freq_half, 0)
     copies = jnp.broadcast_to(own_half[None], (dev_count,) + own_half.shape)
-    gathered = lax.all_to_all(copies, DEV, 0, 0, tiled=True)
+    gathered = lax.all_to_all(copies, DEV, 0, 2, tiled=True)[0]
     partner = lax.ppermute(gathered, "core", [(0, 1), (1, 0)])
     low = jnp.where(core == 0, gathered, partner)
     high = jnp.where(core == 0, partner, gathered)
-    gathered = jnp.concatenate([low, high], 1)
-    grid_rows = jnp.transpose(gathered, (1, 0, 2, 3)).reshape(M, classes_total, 2 * Q)
+    grid_rows = jnp.concatenate([low, high], 0)
     factor = jnp.where(jnp.arange(M) == 0, 1.0, 2.0).astype(jnp.float32)
     squares = jnp.sum(grid_rows.astype(jnp.float32) ** 2 * factor[:, None, None], axis=0)
     cycle_power = squares[:, :Q] + squares[:, Q:]

time: 132 us -> 131 us (level)
    reshape x1 -> x0, local copies, waits for them, and re-layouts: 2.39 us -> none  [local(): jnp.transpose(gathered, (1, 0, 2, 3)).reshape(M, classes_total, 2 * Q)]
    concatenate x1 -> x0, other arithmetic: 1.58 us -> none  [local(): gathered = jnp.concatenate([low, high], 1)]
    squeeze x0 -> x1, local copies, waits for them, and re-layouts: none -> 1.45 us  [local(): gathered = lax.all_to_all(copies, DEV, 0, 2, tiled=True)[0]]
    dot_general x1, matrix products: 0.38 us -> 1.77 us  [local(): jnp.dot(class_weight, power_term.T, precision=lax.Precision.HIGHEST)]
    unnamed x20 -> x26, local copies, waits for them, and re-layouts: 13.7 us -> 13.7 us
where the time goes in v13:
time: 131 us; the launch traced here: 130 us
  blocking collectives  44.5 us (34%)
  local copies, waits for them, and re-layouts  22.3 us (17%)
  Pallas kernels  20.4 us (16%)
  waiting for transfers between devices  15.3 us (12%)
  starting transfers between devices  15 us (11%)
  matrix products  6.62 us (5%)
  other arithmetic  5.45 us (4%)
    all_gather x1, blocking collectives, local(): own = lax.all_gather(own, GRP, axis=0, tiled=False)  16.2 us
    all_to_all x1, blocking collectives, local(): own = jnp.sum(lax.all_to_all(packed, 'y', 1, 1, tiled=True), 1)  15.3 us
    unnamed x26, local copies, waits for them, and re-layouts  13.7 us
    all_to_all x1, blocking collectives, local(): own = jnp.sum(lax.all_to_all(own, 'z', 0, 0, tiled=True), 0)  13 us
    all_to_all x1, waiting for transfers between devices, local(): gathered = lax.all_to_all(copies, DEV, 0, 2, tiled=True)[0]  12.2 us
    all_to_all x1, starting transfers between devices, local(): gathered = lax.all_to_all(copies, DEV, 0, 2, tiled=True)[0]  12 us
    pallas_call x1, Pallas kernels, local(): pl.pallas_call(functools.partial(norm_kernel, columns), grid=(steps,), in...  10.5 us
    pallas_call x1, Pallas kernels, local(): pl.pallas_call(functools.partial(spectra_kernel, columns), grid=(steps,),...  9.93 us
  transfers between devices with their start and end apart: 3, of which 3 were waited for; matrix products, arithmetic and copies ran while one was open for 2% of the time, Pallas kernels for 0%

profile of v13, /device:TPU:1, one launch (start us, length us, event | category | flops | bytes accessed | tf_op | source)
XLA Modules:
  0.0 130.5 jit_solution(15262857753311060670)
XLA Ops:
  0.6 0.0 copy-start
  0.6 0.0 copy-start.6
  0.7 0.0 copy-start.7
  0.7 0.0 copy-start.3
  0.7 1.0 reshape.200
  1.7 0.1 broadcast_bitcast_fusion
  1.8 1.2 reshape.228
  2.9 12.0 %all-to-all-start = ((bf16[32,2,3072]{2,1,0:T(2,128)(2,1)}), bf16[32,2,3072]{2,1,0:T(2,128)(2,1)S(1)}, u32[]{:S(2)}, u32[]{:S(2)}) async-start(bf16[32,2,3072]{2,1,0:T(2,128)(2,1)} %reshape.228), calls=%async_computation | async-start | bytes 786432 | tf_op jit(solution)/shard_map/all_to_all | solution.py:107
  15.0 0.1 multiply_convert_fusion.1
  15.1 0.7 copy.47.table_ref
  15.8 0.1 pad.4.clone
  15.9 0.1 pad.3.clone
  16.0 0.1 fusion.14
  16.1 0.0 copy-done
  16.1 0.0 copy-done.6
  16.1 0.0 copy-done.7
  16.1 0.2 broadcast_divide_fusion
  16.3 0.0 copy-start.5
  16.3 0.0 copy-done.3
  16.3 0.3 fusion
  16.6 12.2 %all-to-all-done = bf16[32,2,3072]{2,1,0:T(2,128)(2,1)S(1)} async-done(((bf16[32,2,3072]{2,1,0:T(2,128)(2,1)}), bf16[32,2,3072]{2,1,0:T(2,128)(2,1)S(1)}, u32[]{:S(2)}, u32[]{:S(2)}) %all-to-all-start) | async-done | bytes 393248 | tf_op jit(solution)/shard_map/all_to_all | solution.py:107
  28.8 0.5 reshape.229
  29.3 1.5 %copy.44 = bf16[16,192,64]{1,2,0:T(8,128)(2,1)} copy(bf16[16,192,64]{2,0,1:T(8,128)(2,1)S(1)} %bitcast.59) | data formatting | bytes 786432 | tf_op jit(solution)/shard_map/squeeze | solution.py:107
  30.7 2.5 %collective-permute-start = (bf16[16,192,64]{1,2,0:T(8,128)(2,1)}, bf16[16,192,64]{1,2,0:T(8,128)(2,1)S(1)}, u32[]{:S(2)}, u32[]{:S(2)}) collective-permute-start(bf16[16,192,64]{1,2,0:T(8,128)(2,1)} %copy.44), channel_id=1, source_target_pairs={{0,32},{32,0},{1,33},{33,1},{2,34},{34,2},{3,35},{35,3},{4,36},{36... | collective-permute-start | bytes 1179656 | tf_op jit(solution)/shard_map/ppermute | solution.py:108
  33.2 0.7 maximum_maximum_fusion.turn_ref
  33.9 0.1 fusion.24
  34.0 1.0 collective-permute-done
  35.0 1.1 broadcast_select_fusion.1
  36.1 1.0 convolution_convert_fusion.1
  37.1 0.3 multiply_reduce_fusion
  37.5 1.0 convolution_convert_fusion
  38.5 3.5 %copy.55 = bf16[4,8,192,256]{3,1,2,0:T(8,128)(2,1)} copy(bf16[4,8,192,256]{3,2,1,0:T(8,128)(2,1)S(1)} %bitcast.53) | data formatting | bytes 6291456
  42.0 3.5 %copy.54 = bf16[4,8,192,256]{3,1,2,0:T(8,128)(2,1)} copy(bf16[4,8,192,256]{3,2,1,0:T(8,128)(2,1)S(1)} %bitcast.52) | data formatting | bytes 6291456
  45.5 0.4 fusion.2
  45.9 0.9 copy.56
  46.7 10.5 %shard_map.77.norm_ref = f32[1,256]{1,0:T(1,128)} custom-call(bf16[128,64]{1,0:T(8,128)(2,1)} %copy.47.table_ref, bf16[32,49152]{1,0:T(8,128)(2,1)} %bitcast.50, bf16[32,49152]{1,0:T(8,128)(2,1)} %bitcast.48, f32[1,49152]{1,0:T(1,128)} %bitcast.60), custom_call_target="tpu_custom_call" | custom-call | tf_op jit(solution)/shard_map/pallas_call | solution.py:136
  57.2 9.9 %shard_map.78 = (bf16[32,49152]{1,0:T(8,128)(2,1)}, bf16[32,49152]{1,0:T(8,128)(2,1)}, f32[1,49152]{1,0:T(1,128)}) custom-call(bf16[128,64]{1,0:T(8,128)(2,1)} %copy.47.table_ref, bf16[32,49152]{1,0:T(8,128)(2,1)} %bitcast.51, bf16[32,49152]{1,0:T(8,128)(2,1)} %bitcast.49, f32[1,49152]{1,0:T(1,128)} %bitcast.61, f32[1,256]{1,0:T(1,128)} %shard_map.77.norm_ref, ...), custom_call_target="tpu_custom_call" | custom-call | tf_op jit(solution)/shard_map/pallas_call | solution.py:145
  67.2 2.6 %copy.57 = bf16[4,8,192,256]{3,2,1,0:T(8,128)(2,1)S(1)} copy(bf16[4,8,192,256]{3,1,2,0:T(8,128)(2,1)} %bitcast.58) | data formatting | bytes 6291456
  69.8 1.1 fusion.25
  70.9 0.8 copy-done.2
  71.7 0.7 copy.58
  72.4 1.1 convolution_add_fusion
  73.6 1.7 %copy.48 = f32[192,2048]{1,0:T(8,128)} copy(f32[192,2048]{0,1:T(8,128)S(1)} %bitcast.56) | data formatting | bytes 3145728 | tf_op jit(solution)/shard_map/reshape | solution.py:170
  75.3 0.5 broadcast.233
  75.8 1.1 reduce.5
  76.9 0.1 reshape.207
  77.0 1.8 %fusion.21 = f32[192,32]{1,0:T(8,128)} fusion(f32[192,256]{1,0:T(8,128)S(1)} %reshape.207, f32[32,256]{1,0:T(8,128)} %copy-done.5, f32[32]{0:T(128)} %param.10), kind=kOutput, calls=%fused_computation.52 | convolution fusion | flops 18890752 | bytes 254080 | tf_op jit(solution)/shard_map/dot_general | solution.py:172
  78.7 0.1 reduce_sum.46
  78.9 0.8 copy.50
  79.6 1.1 concatenate.18
  80.8 0.1 constant_dynamic-slice_fusion
  80.9 0.5 collective-permute-start.1
  81.3 2.1 %collective-permute-done.1 = f32[192,1152]{1,0:T(8,128)S(1)} collective-permute-done((f32[192,1152]{1,0:T(8,128)S(1)}, f32[192,1152]{1,0:T(8,128)S(1)}, u32[]{:S(2)}, u32[]{:S(2)}) %collective-permute-start.1) | collective-permute-done | bytes 884768 | tf_op jit(solution)/shard_map/ppermute | solution.py:183
  83.4 0.1 dynamic-slice_add_fusion
  83.5 0.1 reshape.208
  83.6 0.5 copy.51
  84.2 15.3 %all_to_all.25 = f32[8,4,6,1152]{3,0,2,1:T(8,128)S(1)} all-to-all(f32[8,4,6,1152]{3,0,2,1:T(8,128)S(1)} %copy.51), channel_id=1, replica_groups=mesh['x'=4,'core'=2,'z'=8,'y'=4] {'y'}, dimensions={1} | all-to-all | bytes 1769472 | tf_op jit(solution)/shard_map/all_to_all | solution.py:185
  99.5 0.1 copy.52
  99.6 13.0 %all_to_all.26 = f32[8,6,1152]{2,1,0:T(8,128)S(1)} all-to-all(f32[8,6,1152]{2,1,0:T(8,128)S(1)} %copy.52), channel_id=1, replica_groups=mesh['x'=4,'core'=2,'z'=8,'y'=4] {'z'}, dimensions={0} | all-to-all | bytes 442368 | tf_op jit(solution)/shard_map/all_to_all | solution.py:186
  112.6 16.2 %all-gather.1 = f32[8,6,1152]{2,1,0:T(8,128)S(1)} all-gather(f32[1,6,1152]{2,1,0:T(8,128)S(1)} %bitcast.65), channel_id=2, replica_groups=mesh['x'=4,'core'=2,'z'=8,'y'=4] {'x','core'}, dimensions={0}, use_global_device_ids=true | all-gather | bytes 248832 | tf_op jit(solution)/shard_map/all_gather | solution.py:187
  128.9 0.7 fusion.16
  129.6 0.1 div.21
  129.6 0.2 div.22
  129.8 0.7 fusion.3
  (20 shorter events, 0.2 us)
Async XLA Ops:
  0.6 15.5 %copy-start = (f32[64,32]{0,1:T(8,128)S(1)}, f32[64,32]{0,1:T(8,128)}, u32[]{:S(2)}) copy-start(f32[64,32]{0,1:T(8,128)} %param.9) | copy-start | bytes 24580
  0.6 15.5 %copy-start.6 = (f32[32]{0:T(128)S(1)}, f32[32]{0:T(128)}, u32[]{:S(2)}) copy-start(f32[32]{0:T(128)} %param.10) | copy-start | bytes 388
  0.7 15.5 %copy-start.7 = (s32[256]{0:T(256)S(1)}, s32[256]{0:T(256)}, u32[]{:S(2)}) copy-start(s32[256]{0:T(256)} %param.8) | copy-start | bytes 3076
  0.7 15.6 %copy-start.3 = (bf16[2048,256]{1,0:T(8,128)(2,1)S(1)}, bf16[2048,256]{1,0:T(8,128)(2,1)}, u32[]{:S(2)}) copy-start(bf16[2048,256]{1,0:T(8,128)(2,1)} %param.7) | copy-start | bytes 3145732
  2.9 25.8 %all-to-all-start = ((bf16[32,2,3072]{2,1,0:T(2,128)(2,1)}), bf16[32,2,3072]{2,1,0:T(2,128)(2,1)S(1)}, u32[]{:S(2)}, u32[]{:S(2)}) async-start(bf16[32,2,3072]{2,1,0:T(2,128)(2,1)} %reshape.228), calls=%async_computation | async-start | bytes 786432 | tf_op jit(solution)/shard_map/all_to_all | solution.py:107
  16.3 29.2 %copy-start.5 = (f32[32,256]{1,0:T(8,128)}, f32[32,256]{1,0:T(8,128)S(1)}, u32[]{:S(2)}) copy-start(f32[32,256]{1,0:T(8,128)S(1)} %get-tuple-element.17) | copy-start | bytes 98308
  30.7 4.2 %collective-permute-start = (bf16[16,192,64]{1,2,0:T(8,128)(2,1)}, bf16[16,192,64]{1,2,0:T(8,128)(2,1)S(1)}, u32[]{:S(2)}, u32[]{:S(2)}) collective-permute-start(bf16[16,192,64]{1,2,0:T(8,128)(2,1)} %copy.44), channel_id=1, source_target_pairs={{0,32},{32,0},{1,33},{33,1},{2,34},{34,2},{3,35},{35,3},{4,36},{36... | collective-permute-start | bytes 1179656 | tf_op jit(solution)/shard_map/ppermute | solution.py:108
  42.0 3.5 %copy-start.8 = (f32[192]{0:T(256)S(1)}, f32[192]{0:T(256)}, u32[]{:S(2)}) copy-start(f32[192]{0:T(256)} %param.11) | copy-start | bytes 2308
  69.8 1.9 %copy-start.2 = (bf16[32,49152]{1,0:T(8,128)(2,1)S(1)}, bf16[32,49152]{1,0:T(8,128)(2,1)}, u32[]{:S(2)}) copy-start(bf16[32,49152]{1,0:T(8,128)(2,1)} %get-tuple-element.6) | copy-start | bytes 9437188
  73.6 2.2 %copy-start.4 = (f32[1,49152]{1,0:T(1,128)S(1)}, f32[1,49152]{1,0:T(1,128)}, u32[]{:S(2)}) copy-start(f32[1,49152]{1,0:T(1,128)} %get-tuple-element.7) | copy-start | bytes 589828
  75.3 4.4 %copy-start.1 = (f32[192,2048]{1,0:T(8,128)S(1)}, f32[192,2048]{1,0:T(8,128)}, u32[]{:S(2)}) copy-start(f32[192,2048]{1,0:T(8,128)} %copy.48) | copy-start | bytes 4718596
  80.9 2.5 %collective-permute-start.1 = (f32[192,1152]{1,0:T(8,128)S(1)}, f32[192,1152]{1,0:T(8,128)S(1)}, u32[]{:S(2)}, u32[]{:S(2)}) collective-permute-start(f32[192,1152]{1,0:T(8,128)S(1)} %constant_dynamic-slice_fusion), channel_id=1, source_target_pairs={{0,32},{32,0},{1,33},{33,1},{2,34},{34,2},{3,35},{35,3},{4,36},{36... | collective-permute-start | bytes 2654216 | tf_op jit(solution)/shard_map/ppermute | solution.py:183

commit v14 on v13

--- a/solution.py
+++ b/solution.py
@@ -48,7 +48,10 @@
 
 
 def block_scores(table_ref, real_ref, imag_ref, shift_ref):
-    crossed = jnp.concatenate([real_ref[...], imag_ref[...]], 0)
+    classes = real_ref.shape[1]
+    crossed = jnp.concatenate(
+        [jnp.concatenate([real_ref[:, j, :], imag_ref[:, j, :]], 0) for j in range(classes)], 1
+    )
     raw = jnp.dot(table_ref[...], crossed, preferred_element_type=jnp.float32)
     return raw + shift_ref[...]
 
@@ -87,8 +90,10 @@
         turn_ref[...], responsibility.astype(jnp.bfloat16), preferred_element_type=jnp.float32
     )
     rows = cos_ref.shape[0]
-    cos_ref[...] = full[:rows].astype(jnp.bfloat16)
-    sin_ref[...] = full[rows : 2 * rows].astype(jnp.bfloat16)
+    for j in range(cos_ref.shape[1]):
+        part = full[:, j * cols : (j + 1) * cols]
+        cos_ref[:, j, :] = part[:rows].astype(jnp.bfloat16)
+        sin_ref[:, j, :] = part[rows : 2 * rows].astype(jnp.bfloat16)
     weight_ref[...] = full[2 * rows : 2 * rows + 1]
 
 
@@ -117,10 +122,10 @@
     width = classes_total * columns
     crossed_real = jnp.einsum(
         "mkc,mcb->mkb", grid_rows, weighted, preferred_element_type=jnp.float32
-    ).astype(jnp.bfloat16).reshape(rows, width)
+    ).astype(jnp.bfloat16)
     crossed_imag = jnp.einsum(
         "mkc,mcb->mkb", grid_rows, swapped, preferred_element_type=jnp.float32
-    ).astype(jnp.bfloat16).reshape(rows, width)
+    ).astype(jnp.bfloat16)
     penalty = jnp.dot(cycle_power, power_term, precision=lax.Precision.HIGHEST)
     bias = (class_prior[:, None] - 0.5 * penalty).reshape(1, width)
     table = jnp.transpose(score_table, (2, 0, 1)).reshape(R, 2 * M)
@@ -131,7 +136,7 @@
     block = CLS_STEP * columns
     steps = width // block
     table_spec = pl.BlockSpec((R, 2 * rows), lambda i: (0, 0))
-    crossed_spec = pl.BlockSpec((rows, block), lambda i: (0, i))
+    crossed_spec = pl.BlockSpec((rows, CLS_STEP, columns), lambda i: (0, i, 0))
     row_spec = pl.BlockSpec((1, block), lambda i: (0, i))
     log_norm = pl.pallas_call(
         functools.partial(norm_kernel, columns),
@@ -155,15 +160,13 @@
         ],
         out_specs=[crossed_spec, crossed_spec, row_spec],
         out_shape=[
-            jax.ShapeDtypeStruct((rows, width), jnp.bfloat16),
-            jax.ShapeDtypeStruct((rows, width), jnp.bfloat16),
+            jax.ShapeDtypeStruct((rows, classes_total, columns), jnp.bfloat16),
+            jax.ShapeDtypeStruct((rows, classes_total, columns), jnp.bfloat16),
             jax.ShapeDtypeStruct((1, width), jnp.float32),
         ],
         compiler_params=pltpu.CompilerParams(dimension_semantics=("arbitrary",)),
     )(table, crossed_real, crossed_imag, bias, log_norm, turn)
 
-    spectra_cos = spectra_cos.reshape(M, classes_total, columns)
-    spectra_sin = spectra_sin.reshape(M, classes_total, columns)
     numer_all = jnp.einsum(
         "mkb,mcb->kmc", spectra_cos, weighted, preferred_element_type=jnp.float32
     ) + jnp.einsum("mkb,mcb->kmc", spectra_sin, swapped, preferred_element_type=jnp.float32)

time: 131 us -> 149 us (1.14)
  Pallas kernels: 20.4 us -> 44.2 us
  local copies, waits for them, and re-layouts: 22.3 us -> 11.2 us
  matrix products: 6.62 us -> 12 us
    pallas_call x1, Pallas kernels: 9.93 us -> 25.7 us  [local(): pl.pallas_call(functools.partial(spectra_kernel, columns), grid=(steps,),...]
    unnamed x26 -> x22, local copies, waits for them, and re-layouts: 13.7 us -> 2.67 us
    pallas_call x1, Pallas kernels: 10.5 us -> 18.5 us  [local(): pl.pallas_call(functools.partial(norm_kernel, columns), grid=(steps,), in...]
    dot_general x1, matrix products: 1.12 us -> 3.16 us  [local(): jnp.einsum('mkb,mcb->kmc', spectra_cos, weighted, preferred_element_type=...]
    dot_general x1, matrix products: 1.03 us -> 2.74 us  [local(): jnp.einsum('mkc,mcb->mkb', grid_rows, swapped, preferred_element_type=jnp...]
    dot_general x1, matrix products: 1.04 us -> 2.71 us  [local(): jnp.einsum('mkc,mcb->mkb', grid_rows, weighted, preferred_element_type=jn...]
where the time goes in v14:
time: 149 us
  blocking collectives  44.5 us (30%)
  Pallas kernels  44.2 us (30%)
  waiting for transfers between devices  15.3 us (10%)
  starting transfers between devices  15 us (10%)
  matrix products  12 us (8%)
  local copies, waits for them, and re-layouts  11.2 us (8%)
  other arithmetic  5.45 us (4%)
    pallas_call x1, Pallas kernels, local(): pl.pallas_call(functools.partial(spectra_kernel, columns), grid=(steps,),...  25.7 us
    pallas_call x1, Pallas kernels, local(): pl.pallas_call(functools.partial(norm_kernel, columns), grid=(steps,), in...  18.5 us
    all_gather x1, blocking collectives, local(): own = lax.all_gather(own, GRP, axis=0, tiled=False)  16.2 us
    all_to_all x1, blocking collectives, local(): own = jnp.sum(lax.all_to_all(packed, 'y', 1, 1, tiled=True), 1)  15.3 us
    all_to_all x1, blocking collectives, local(): own = jnp.sum(lax.all_to_all(own, 'z', 0, 0, tiled=True), 0)  13 us
    all_to_all x1, waiting for transfers between devices, local(): gathered = lax.all_to_all(copies, DEV, 0, 2, tiled=True)[0]  12.2 us
    all_to_all x1, starting transfers between devices, local(): gathered = lax.all_to_all(copies, DEV, 0, 2, tiled=True)[0]  12 us
    dot_general x1, matrix products, local(): jnp.einsum('mkb,mcb->kmc', spectra_cos, weighted, preferred_element_type=...  3.16 us
  transfers between devices with their start and end apart: 3, of which 3 were waited for; matrix products, arithmetic and copies ran while one was open for 2% of the time, Pallas kernels for 0%

profile of v14, /device:TPU:1, one launch (start us, length us, event | category | flops | bytes accessed | tf_op | source)
XLA Modules:
  0.0 148.5 jit_solution(8789348040020727378)
XLA Ops:
  0.6 0.0 copy-start
  0.6 0.0 copy-start.6
  0.7 0.0 copy-start.7
  0.7 0.0 copy-start.3
  0.7 1.0 reshape.188
  1.7 0.1 broadcast_bitcast_fusion
  1.8 1.2 reshape.212
  2.9 12.0 %all-to-all-start = ((bf16[32,2,3072]{2,1,0:T(2,128)(2,1)}), bf16[32,2,3072]{2,1,0:T(2,128)(2,1)S(1)}, u32[]{:S(2)}, u32[]{:S(2)}) async-start(bf16[32,2,3072]{2,1,0:T(2,128)(2,1)} %reshape.212), calls=%async_computation | async-start | bytes 786432 | tf_op jit(solution)/shard_map/all_to_all | solution.py:112
  15.0 0.1 multiply_convert_fusion.1
  15.1 0.7 copy.47.table_ref
  15.8 0.1 pad.4.clone
  15.9 0.1 pad.3.clone
  16.0 0.1 fusion.14
  16.1 0.0 copy-done
  16.1 0.0 copy-done.6
  16.1 0.0 copy-done.7
  16.1 0.2 broadcast_divide_fusion
  16.3 0.0 copy-start.5
  16.3 0.0 copy-done.3
  16.3 0.3 fusion
  16.6 12.2 %all-to-all-done = bf16[32,2,3072]{2,1,0:T(2,128)(2,1)S(1)} async-done(((bf16[32,2,3072]{2,1,0:T(2,128)(2,1)}), bf16[32,2,3072]{2,1,0:T(2,128)(2,1)S(1)}, u32[]{:S(2)}, u32[]{:S(2)}) %all-to-all-start) | async-done | bytes 393248 | tf_op jit(solution)/shard_map/all_to_all | solution.py:112
  28.8 0.5 reshape.213
  29.3 1.5 copy.44
  30.7 2.5 %collective-permute-start = (bf16[16,192,64]{1,2,0:T(8,128)(2,1)}, bf16[16,192,64]{1,2,0:T(8,128)(2,1)S(1)}, u32[]{:S(2)}, u32[]{:S(2)}) collective-permute-start(bf16[16,192,64]{1,2,0:T(8,128)(2,1)} %copy.44), channel_id=1, source_target_pairs={{0,32},{32,0},{1,33},{33,1},{2,34},{34,2},{3,35},{35,3},{4,36},{36... | collective-permute-start | bytes 1179656 | tf_op jit(solution)/shard_map/ppermute | solution.py:113
  33.2 0.7 maximum_maximum_fusion.turn_ref
  33.9 0.1 fusion.24
  34.0 1.0 collective-permute-done
  35.0 1.1 broadcast_select_fusion.1
  36.1 0.3 multiply_reduce_fusion
  36.4 0.0 copy-start.8
  36.4 2.7 %convolution_convert_fusion.1.real_ref = bf16[32,192,256]{2,1,0:T(8,128)(2,1)} fusion(bf16[32,64,256]{2,1,0:T(8,128)(2,1)S(1)} %fusion, bf16[16,192,64]{1,2,0:T(8,128)(2,1)S(1)} %get-tuple-element.11, bf16[16,192,64]{1,2,0:T(8,128)(2,1)S(1)} %get-tuple-element.10), kind=kOutput, calls=%fused_computation.1 | convolution fusion | flops 203292672 | bytes 4980736 | tf_op jit(solution)/shard_map/mkc,mcb->mkb/dot_general | solution.py:123
  39.1 0.0 copy-done.5
  39.1 0.0 copy-done.8
  39.1 0.4 fusion.2
  39.5 0.9 copy.54
  40.4 2.7 %convolution_convert_fusion.imag_ref = bf16[32,192,256]{2,1,0:T(8,128)(2,1)} fusion(bf16[32,32,256]{2,1,0:T(8,128)(2,1)S(1)} %get-tuple-element.9, bf16[32,32,256]{2,1,0:T(8,128)(2,1)S(1)} %get-tuple-element.8, bf16[16,192,64]{1,2,0:T(8,128)(2,1)S(1)} %get-tuple-element.11, bf16[16,192,64]{1,2,0:T(8,128)(2,1)S(1)} %get-tuple-element.10), kind=kOutput, calls=%fused_computation | convolution fusion | flops 205389824 | bytes 4980736 | tf_op jit(solution)/shard_map/mkc,mcb->mkb/dot_general | solution.py:126
  43.2 18.5 %shard_map.77.norm_ref = f32[1,256]{1,0:T(1,128)} custom-call(bf16[128,64]{1,0:T(8,128)(2,1)} %copy.47.table_ref, bf16[32,192,256]{2,1,0:T(8,128)(2,1)} %convolution_convert_fusion.1.real_ref, bf16[32,192,256]{2,1,0:T(8,128)(2,1)} %convolution_convert_fusion.imag_ref, f32[1,49152]{1,0:T(1,128)} %bitcast.42), custom_call_target="tpu_custom_call" | custom-call | tf_op jit(solution)/shard_map/pallas_call | solution.py:141
  61.6 25.7 %shard_map.78 = (bf16[32,192,256]{2,1,0:T(8,128)(2,1)}, bf16[32,192,256]{2,1,0:T(8,128)(2,1)}, f32[1,49152]{1,0:T(1,128)}) custom-call(bf16[128,64]{1,0:T(8,128)(2,1)} %copy.47.table_ref, bf16[32,192,256]{2,1,0:T(8,128)(2,1)} %convolution_convert_fusion.1.real_ref, bf16[32,192,256]{2,1,0:T(8,128)(2,1)} %convolution_convert_fusion.imag_ref, ...), custom_call_target="tpu_custom_call" | custom-call | tf_op jit(solution)/shard_map/pallas_call | solution.py:150
  87.3 3.2 %fusion.25 = f32[32,64,192]{2,1,0:T(8,128)S(1)} fusion(bf16[32,64,256]{2,1,0:T(8,128)(2,1)S(1)} %fusion, bf16[32,192,256]{2,1,0:T(8,128)(2,1)} %get-tuple-element.5), kind=kOutput, calls=%fused_computation.55 | convolution fusion | flops 201326592 | bytes 5767168 | tf_op jit(solution)/shard_map/mkb,mcb->kmc/dot_general | solution.py:170
  90.5 0.0 copy-done.2
  90.5 1.1 convolution_add_fusion
  91.6 1.7 %copy.48 = f32[192,2048]{1,0:T(8,128)} copy(f32[192,2048]{0,1:T(8,128)S(1)} %bitcast.40) | data formatting | bytes 3145728 | tf_op jit(solution)/shard_map/reshape | solution.py:173
  93.3 0.5 broadcast.233
  93.8 0.0 copy-done.4
  93.8 1.1 reduce.5
  95.0 0.1 reshape.191
  95.0 1.8 %fusion.21 = f32[192,32]{1,0:T(8,128)} fusion(f32[192,256]{1,0:T(8,128)S(1)} %reshape.191, f32[32,256]{1,0:T(8,128)} %copy-done.5, f32[32]{0:T(128)} %param.10), kind=kOutput, calls=%fused_computation.52 | convolution fusion | flops 18890752 | bytes 254080 | tf_op jit(solution)/shard_map/dot_general | solution.py:175
  96.8 0.1 reduce_sum.46
  96.9 0.8 copy.50
  97.7 1.1 concatenate.18
  98.8 0.1 constant_dynamic-slice_fusion
  98.9 0.5 collective-permute-start.1
  99.4 2.1 %collective-permute-done.1 = f32[192,1152]{1,0:T(8,128)S(1)} collective-permute-done((f32[192,1152]{1,0:T(8,128)S(1)}, f32[192,1152]{1,0:T(8,128)S(1)}, u32[]{:S(2)}, u32[]{:S(2)}) %collective-permute-start.1) | collective-permute-done | bytes 884768 | tf_op jit(solution)/shard_map/ppermute | solution.py:186
  101.4 0.1 dynamic-slice_add_fusion
  101.6 0.1 reshape.192
  101.7 0.5 copy.51
  102.2 15.3 %all_to_all.25 = f32[8,4,6,1152]{3,0,2,1:T(8,128)S(1)} all-to-all(f32[8,4,6,1152]{3,0,2,1:T(8,128)S(1)} %copy.51), channel_id=1, replica_groups=mesh['x'=4,'core'=2,'z'=8,'y'=4] {'y'}, dimensions={1} | all-to-all | bytes 1769472 | tf_op jit(solution)/shard_map/all_to_all | solution.py:188
  117.5 0.1 copy.52
  117.6 13.0 %all_to_all.26 = f32[8,6,1152]{2,1,0:T(8,128)S(1)} all-to-all(f32[8,6,1152]{2,1,0:T(8,128)S(1)} %copy.52), channel_id=1, replica_groups=mesh['x'=4,'core'=2,'z'=8,'y'=4] {'z'}, dimensions={0} | all-to-all | bytes 442368 | tf_op jit(solution)/shard_map/all_to_all | solution.py:189
  130.7 16.2 %all-gather.1 = f32[8,6,1152]{2,1,0:T(8,128)S(1)} all-gather(f32[1,6,1152]{2,1,0:T(8,128)S(1)} %bitcast.47), channel_id=2, replica_groups=mesh['x'=4,'core'=2,'z'=8,'y'=4] {'x','core'}, dimensions={0}, use_global_device_ids=true | all-gather | bytes 248832 | tf_op jit(solution)/shard_map/all_gather | solution.py:190
  146.9 0.7 fusion.16
  147.6 0.1 div.21
  147.7 0.2 div.22
  147.9 0.7 fusion.3
  (16 shorter events, 0.2 us)
Async XLA Ops:
  0.6 15.5 %copy-start = (f32[64,32]{0,1:T(8,128)S(1)}, f32[64,32]{0,1:T(8,128)}, u32[]{:S(2)}) copy-start(f32[64,32]{0,1:T(8,128)} %param.9) | copy-start | bytes 24580
  0.6 15.5 %copy-start.6 = (f32[32]{0:T(128)S(1)}, f32[32]{0:T(128)}, u32[]{:S(2)}) copy-start(f32[32]{0:T(128)} %param.10) | copy-start | bytes 388
  0.7 15.5 %copy-start.7 = (s32[256]{0:T(256)S(1)}, s32[256]{0:T(256)}, u32[]{:S(2)}) copy-start(s32[256]{0:T(256)} %param.8) | copy-start | bytes 3076
  0.7 15.6 %copy-start.3 = (bf16[2048,256]{1,0:T(8,128)(2,1)S(1)}, bf16[2048,256]{1,0:T(8,128)(2,1)}, u32[]{:S(2)}) copy-start(bf16[2048,256]{1,0:T(8,128)(2,1)} %param.7) | copy-start | bytes 3145732
  2.9 25.8 %all-to-all-start = ((bf16[32,2,3072]{2,1,0:T(2,128)(2,1)}), bf16[32,2,3072]{2,1,0:T(2,128)(2,1)S(1)}, u32[]{:S(2)}, u32[]{:S(2)}) async-start(bf16[32,2,3072]{2,1,0:T(2,128)(2,1)} %reshape.212), calls=%async_computation | async-start | bytes 786432 | tf_op jit(solution)/shard_map/all_to_all | solution.py:112
  16.3 22.9 %copy-start.5 = (f32[32,256]{1,0:T(8,128)}, f32[32,256]{1,0:T(8,128)S(1)}, u32[]{:S(2)}) copy-start(f32[32,256]{1,0:T(8,128)S(1)} %get-tuple-element.17) | copy-start | bytes 98308
  30.7 4.2 %collective-permute-start = (bf16[16,192,64]{1,2,0:T(8,128)(2,1)}, bf16[16,192,64]{1,2,0:T(8,128)(2,1)S(1)}, u32[]{:S(2)}, u32[]{:S(2)}) collective-permute-start(bf16[16,192,64]{1,2,0:T(8,128)(2,1)} %copy.44), channel_id=1, source_target_pairs={{0,32},{32,0},{1,33},{33,1},{2,34},{34,2},{3,35},{35,3},{4,36},{36... | collective-permute-start | bytes 1179656 | tf_op jit(solution)/shard_map/ppermute | solution.py:113
  36.4 2.7 %copy-start.8 = (f32[192]{0:T(256)S(1)}, f32[192]{0:T(256)}, u32[]{:S(2)}) copy-start(f32[192]{0:T(256)} %param.11) | copy-start | bytes 2308
  87.3 3.2 %copy-start.2 = (bf16[32,192,256]{2,1,0:T(8,128)(2,1)S(1)}, bf16[32,192,256]{2,1,0:T(8,128)(2,1)}, u32[]{:S(2)}) copy-start(bf16[32,192,256]{2,1,0:T(8,128)(2,1)} %get-tuple-element.6) | copy-start | bytes 9437188
  91.6 2.2 %copy-start.4 = (f32[1,49152]{1,0:T(1,128)S(1)}, f32[1,49152]{1,0:T(1,128)}, u32[]{:S(2)}) copy-start(f32[1,49152]{1,0:T(1,128)} %get-tuple-element.7) | copy-start | bytes 589828
  93.3 4.4 %copy-start.1 = (f32[192,2048]{1,0:T(8,128)S(1)}, f32[192,2048]{1,0:T(8,128)}, u32[]{:S(2)}) copy-start(f32[192,2048]{1,0:T(8,128)} %copy.48) | copy-start | bytes 4718596
  98.9 2.5 %collective-permute-start.1 = (f32[192,1152]{1,0:T(8,128)S(1)}, f32[192,1152]{1,0:T(8,128)S(1)}, u32[]{:S(2)}, u32[]{:S(2)}) collective-permute-start(f32[192,1152]{1,0:T(8,128)S(1)} %constant_dynamic-slice_fusion), channel_id=1, source_target_pairs={{0,32},{32,0},{1,33},{33,1},{2,34},{34,2},{3,35},{35,3},{4,36},{36... | collective-permute-start | bytes 2654216 | tf_op jit(solution)/shard_map/ppermute | solution.py:186

commit v15 on v13

--- a/solution.py
+++ b/solution.py
@@ -113,6 +113,7 @@
     squares = jnp.sum(grid_rows.astype(jnp.float32) ** 2 * factor[:, None, None], axis=0)
     cycle_power = squares[:, :Q] + squares[:, Q:]
     swapped = jnp.concatenate([weighted[:, Q:], -weighted[:, :Q]], 1)
+    weighted, swapped, power_term = lax.optimization_barrier((weighted, swapped, power_term))
     rows = M
     width = classes_total * columns
     crossed_real = jnp.einsum(

time: 131 us -> 130 us (level)
    dot_general x1, matrix products: 1.12 us -> 2.48 us  [local(): jnp.einsum('mkb,mcb->kmc', spectra_sin, swapped, preferred_element_type=j...]
    unnamed x26 -> x22, local copies, waits for them, and re-layouts: 13.7 us -> 13.7 us
  transfers between devices with their start and end apart: 3 -> 3, of which waited for: 3 -> 2; matrix products, arithmetic and copies ran while one was open for 2% -> 2% of each run, Pallas kernels for 0% -> 0%
where the time goes in v15:
time: 130 us; the launch traced here: 129 us
  blocking collectives  44.5 us (34%)
  local copies, waits for them, and re-layouts  21.7 us (17%)
  Pallas kernels  20.3 us (16%)
  starting transfers between devices  15 us (12%)
  waiting for transfers between devices  15 us (12%)
  matrix products  7.1 us (5%)
  other arithmetic  4.48 us (3%)
    all_gather x1, blocking collectives, local(): own = lax.all_gather(own, GRP, axis=0, tiled=False)  16.2 us
    all_to_all x1, blocking collectives, local(): own = jnp.sum(lax.all_to_all(packed, 'y', 1, 1, tiled=True), 1)  15.3 us
    unnamed x22, local copies, waits for them, and re-layouts  13.7 us
    all_to_all x1, blocking collectives, local(): own = jnp.sum(lax.all_to_all(own, 'z', 0, 0, tiled=True), 0)  13.1 us
    all_to_all x1, waiting for transfers between devices, local(): gathered = lax.all_to_all(copies, DEV, 0, 2, tiled=True)[0]  13 us
    all_to_all x1, starting transfers between devices, local(): gathered = lax.all_to_all(copies, DEV, 0, 2, tiled=True)[0]  12 us
    pallas_call x1, Pallas kernels, local(): pl.pallas_call(functools.partial(norm_kernel, columns), grid=(steps,), in...  10.4 us
    pallas_call x1, Pallas kernels, local(): pl.pallas_call(functools.partial(spectra_kernel, columns), grid=(steps,),...  9.92 us
  transfers between devices with their start and end apart: 3, of which 2 were waited for; matrix products, arithmetic and copies ran while one was open for 2% of the time, Pallas kernels for 0%

profile of v15, /device:TPU:1, one launch (start us, length us, event | category | flops | bytes accessed | tf_op | source)
XLA Modules:
  0.0 129.2 jit_solution(9071787373466902654)
XLA Ops:
  0.6 0.0 copy-start
  0.6 0.0 copy-start.6
  0.7 0.0 copy-start.5
  0.7 1.0 reshape.200
  1.7 0.1 broadcast_bitcast_fusion
  1.8 1.2 reshape.228
  2.9 12.0 %all-to-all-start = ((bf16[32,2,3072]{2,1,0:T(2,128)(2,1)}), bf16[32,2,3072]{2,1,0:T(2,128)(2,1)S(1)}, u32[]{:S(2)}, u32[]{:S(2)}) async-start(bf16[32,2,3072]{2,1,0:T(2,128)(2,1)} %reshape.228), calls=%async_computation | async-start | bytes 786432 | tf_op jit(solution)/shard_map/all_to_all | solution.py:107
  15.0 0.0 copy-done
  15.0 0.0 copy-done.6
  15.0 0.0 copy-done.5
  15.0 0.2 fusion.19
  15.2 0.3 fusion
  15.5 0.1 fusion.14
  15.6 0.1 fusion.20
  15.6 0.1 pad_maximum_fusion
  15.7 0.1 multiply_convert_fusion.1
  15.8 13.0 %all-to-all-done = bf16[32,2,3072]{2,1,0:T(2,128)(2,1)S(1)} async-done(((bf16[32,2,3072]{2,1,0:T(2,128)(2,1)}), bf16[32,2,3072]{2,1,0:T(2,128)(2,1)S(1)}, u32[]{:S(2)}, u32[]{:S(2)}) %all-to-all-start) | async-done | bytes 393248 | tf_op jit(solution)/shard_map/all_to_all | solution.py:107
  28.8 0.5 reshape.229
  29.3 0.0 copy-start.4
  29.3 0.7 copy.44
  29.9 2.6 %collective-permute-start = (bf16[16,192,64]{1,2,0:T(8,128)(2,1)S(1)}, bf16[16,192,64]{1,2,0:T(8,128)(2,1)S(1)}, u32[]{:S(2)}, u32[]{:S(2)}) collective-permute-start(bf16[16,192,64]{1,2,0:T(8,128)(2,1)S(1)} %copy.44), channel_id=1, source_target_pairs={{0,32},{32,0},{1,33},{33,1},{2,34},{34,2},{3,35},{35,3},{4,36},{36... | collective-permute-start | bytes 1179656 | tf_op jit(solution)/shard_map/ppermute | solution.py:108
  32.5 0.7 copy.47.table_ref
  33.2 0.1 pad.4.clone
  33.3 0.1 pad.3.clone
  33.4 0.7 maximum_maximum_fusion.turn_ref
  34.1 0.0 collective-permute-done
  34.1 0.1 broadcast_select_fusion.1
  34.2 0.3 multiply_reduce_fusion
  34.5 0.0 copy-done.4
  34.5 0.4 fusion.2
  34.9 0.9 copy.56
  35.8 1.0 convolution_convert_fusion
  36.8 3.5 %copy.55 = bf16[4,8,192,256]{3,1,2,0:T(8,128)(2,1)} copy(bf16[4,8,192,256]{3,2,1,0:T(8,128)(2,1)S(1)} %bitcast.58) | data formatting | bytes 6291456
  40.3 1.0 convolution_convert_fusion.1
  41.4 3.5 %copy.54 = bf16[4,8,192,256]{3,1,2,0:T(8,128)(2,1)} copy(bf16[4,8,192,256]{3,2,1,0:T(8,128)(2,1)S(1)} %bitcast.56) | data formatting | bytes 6291456
  44.8 10.4 %shard_map.77.norm_ref = f32[1,256]{1,0:T(1,128)} custom-call(bf16[128,64]{1,0:T(8,128)(2,1)} %copy.47.table_ref, bf16[32,49152]{1,0:T(8,128)(2,1)} %bitcast.54, bf16[32,49152]{1,0:T(8,128)(2,1)} %bitcast.52, f32[1,49152]{1,0:T(1,128)} %bitcast.64), custom_call_target="tpu_custom_call" | custom-call | tf_op jit(solution)/shard_map/pallas_call | solution.py:137
  55.2 9.9 %shard_map.78 = (bf16[32,49152]{1,0:T(8,128)(2,1)}, bf16[32,49152]{1,0:T(8,128)(2,1)}, f32[1,49152]{1,0:T(1,128)}) custom-call(bf16[128,64]{1,0:T(8,128)(2,1)} %copy.47.table_ref, bf16[32,49152]{1,0:T(8,128)(2,1)} %bitcast.55, bf16[32,49152]{1,0:T(8,128)(2,1)} %bitcast.53, f32[1,49152]{1,0:T(1,128)} %bitcast.65, f32[1,256]{1,0:T(1,128)} %shard_map.77.norm_ref, ...), custom_call_target="tpu_custom_call" | custom-call | tf_op jit(solution)/shard_map/pallas_call | solution.py:146
  65.2 2.6 %copy.57 = bf16[4,8,192,256]{3,2,1,0:T(8,128)(2,1)S(1)} copy(bf16[4,8,192,256]{3,1,2,0:T(8,128)(2,1)} %bitcast.62) | data formatting | bytes 6291456
  67.8 1.1 fusion.21
  68.9 0.8 copy-done.1
  69.7 0.7 copy.58
  70.4 2.5 %convolution_add_fusion = f32[32,64,192]{2,1,0:T(8,128)} fusion(f32[32,64,192]{2,1,0:T(8,128)S(1)} %fusion.21, bf16[32,64,256]{2,1,0:T(8,128)(2,1)S(1)} %pad_maximum_fusion, bf16[32,192,256]{2,1,0:T(8,128)(2,1)S(1)} %bitcast.59), kind=kOutput, calls=%fused_computation.5 | convolution fusion | flops 201719808 | bytes 7340032 | tf_op jit(solution)/shard_map/mkb,mcb->kmc/dot_general | solution.py:170
  72.9 1.9 %copy.48 = f32[192,2048]{1,0:T(8,128)S(1)} copy(f32[192,2048]{0,1:T(8,128)} %bitcast.60) | data formatting | bytes 3145728 | tf_op jit(solution)/shard_map/reshape | solution.py:171
  74.8 0.5 broadcast.233
  75.4 1.1 reduce.5
  76.5 0.1 reshape.207
  76.5 0.9 fusion.22
  77.5 0.1 reduce_sum.46
  77.6 0.8 copy.50
  78.4 1.1 concatenate.18
  79.5 0.1 constant_dynamic-slice_fusion
  79.6 0.4 collective-permute-start.1
  80.0 2.1 %collective-permute-done.1 = f32[192,1152]{1,0:T(8,128)S(1)} collective-permute-done((f32[192,1152]{1,0:T(8,128)S(1)}, f32[192,1152]{1,0:T(8,128)S(1)}, u32[]{:S(2)}, u32[]{:S(2)}) %collective-permute-start.1) | collective-permute-done | bytes 884768 | tf_op jit(solution)/shard_map/ppermute | solution.py:184
  82.1 0.1 dynamic-slice_add_fusion
  82.2 0.1 reshape.208
  82.3 0.5 copy.51
  82.9 15.3 %all_to_all.25 = f32[8,4,6,1152]{3,0,2,1:T(8,128)S(1)} all-to-all(f32[8,4,6,1152]{3,0,2,1:T(8,128)S(1)} %copy.51), channel_id=1, replica_groups=mesh['x'=4,'core'=2,'z'=8,'y'=4] {'y'}, dimensions={1} | all-to-all | bytes 1769472 | tf_op jit(solution)/shard_map/all_to_all | solution.py:186
  98.3 0.1 copy.52
  98.3 13.1 %all_to_all.26 = f32[8,6,1152]{2,1,0:T(8,128)S(1)} all-to-all(f32[8,6,1152]{2,1,0:T(8,128)S(1)} %copy.52), channel_id=1, replica_groups=mesh['x'=4,'core'=2,'z'=8,'y'=4] {'z'}, dimensions={0} | all-to-all | bytes 442368 | tf_op jit(solution)/shard_map/all_to_all | solution.py:187
  111.4 16.2 %all-gather.1 = f32[8,6,1152]{2,1,0:T(8,128)S(1)} all-gather(f32[1,6,1152]{2,1,0:T(8,128)S(1)} %bitcast.69), channel_id=2, replica_groups=mesh['x'=4,'core'=2,'z'=8,'y'=4] {'x','core'}, dimensions={0}, use_global_device_ids=true | all-gather | bytes 248832 | tf_op jit(solution)/shard_map/all_gather | solution.py:188
  127.6 0.7 fusion.16
  128.3 0.1 div.21
  128.4 0.2 div.22
  128.6 0.7 fusion.3
  (17 shorter events, 0.2 us)
Async XLA Ops:
  0.6 14.4 %copy-start = (f32[64,32]{0,1:T(8,128)S(1)}, f32[64,32]{0,1:T(8,128)}, u32[]{:S(2)}) copy-start(f32[64,32]{0,1:T(8,128)} %param.9) | copy-start | bytes 24580
  0.6 14.3 %copy-start.6 = (f32[32]{0:T(128)S(1)}, f32[32]{0:T(128)}, u32[]{:S(2)}) copy-start(f32[32]{0:T(128)} %param.10) | copy-start | bytes 388
  0.7 14.3 %copy-start.5 = (s32[256]{0:T(256)S(1)}, s32[256]{0:T(256)}, u32[]{:S(2)}) copy-start(s32[256]{0:T(256)} %param.8) | copy-start | bytes 3076
  0.7 14.5 %copy-start.2 = (bf16[2048,256]{1,0:T(8,128)(2,1)S(1)}, bf16[2048,256]{1,0:T(8,128)(2,1)}, u32[]{:S(2)}) copy-start(bf16[2048,256]{1,0:T(8,128)(2,1)} %param.7) | copy-start | bytes 3145732
  2.9 25.8 %all-to-all-start = ((bf16[32,2,3072]{2,1,0:T(2,128)(2,1)}), bf16[32,2,3072]{2,1,0:T(2,128)(2,1)S(1)}, u32[]{:S(2)}, u32[]{:S(2)}) async-start(bf16[32,2,3072]{2,1,0:T(2,128)(2,1)} %reshape.228), calls=%async_computation | async-start | bytes 786432 | tf_op jit(solution)/shard_map/all_to_all | solution.py:107
  29.3 5.3 %copy-start.4 = (f32[192]{0:T(256)S(1)}, f32[192]{0:T(256)}, u32[]{:S(2)}) copy-start(f32[192]{0:T(256)} %param.11) | copy-start | bytes 2308
  29.9 4.2 %collective-permute-start = (bf16[16,192,64]{1,2,0:T(8,128)(2,1)S(1)}, bf16[16,192,64]{1,2,0:T(8,128)(2,1)S(1)}, u32[]{:S(2)}, u32[]{:S(2)}) collective-permute-start(bf16[16,192,64]{1,2,0:T(8,128)(2,1)S(1)} %copy.44), channel_id=1, source_target_pairs={{0,32},{32,0},{1,33},{33,1},{2,34},{34,2},{3,35},{35,3},{4,36},{36... | collective-permute-start | bytes 1179656 | tf_op jit(solution)/shard_map/ppermute | solution.py:108
  67.8 1.9 %copy-start.1 = (bf16[32,49152]{1,0:T(8,128)(2,1)S(1)}, bf16[32,49152]{1,0:T(8,128)(2,1)}, u32[]{:S(2)}) copy-start(bf16[32,49152]{1,0:T(8,128)(2,1)} %get-tuple-element.12) | copy-start | bytes 9437188
  72.9 2.4 %copy-start.3 = (f32[1,49152]{1,0:T(1,128)S(1)}, f32[1,49152]{1,0:T(1,128)}, u32[]{:S(2)}) copy-start(f32[1,49152]{1,0:T(1,128)} %get-tuple-element.13) | copy-start | bytes 589828
  79.6 2.5 %collective-permute-start.1 = (f32[192,1152]{1,0:T(8,128)S(1)}, f32[192,1152]{1,0:T(8,128)S(1)}, u32[]{:S(2)}, u32[]{:S(2)}) collective-permute-start(f32[192,1152]{1,0:T(8,128)S(1)} %constant_dynamic-slice_fusion), channel_id=1, source_target_pairs={{0,32},{32,0},{1,33},{33,1},{2,34},{34,2},{3,35},{35,3},{4,36},{36... | collective-permute-start | bytes 2654216 | tf_op jit(solution)/shard_map/ppermute | solution.py:184

commit v16 on v15

--- a/solution.py
+++ b/solution.py
@@ -105,10 +105,7 @@
     own_half = lax.dynamic_slice_in_dim(own_rows, core * freq_half, freq_half, 0)
     copies = jnp.broadcast_to(own_half[None], (dev_count,) + own_half.shape)
     gathered = lax.all_to_all(copies, DEV, 0, 2, tiled=True)[0]
-    partner = lax.ppermute(gathered, "core", [(0, 1), (1, 0)])
-    low = jnp.where(core == 0, gathered, partner)
-    high = jnp.where(core == 0, partner, gathered)
-    grid_rows = jnp.concatenate([low, high], 0)
+    grid_rows = lax.all_gather(gathered, "core", axis=0, tiled=True)
     factor = jnp.where(jnp.arange(M) == 0, 1.0, 2.0).astype(jnp.float32)
     squares = jnp.sum(grid_rows.astype(jnp.float32) ** 2 * factor[:, None, None], axis=0)
     cycle_power = squares[:, :Q] + squares[:, Q:]

time: 130 us -> 129 us (level)
  blocking collectives: 44.5 us -> 49.2 us
  waiting for transfers between devices: 15 us -> 12.2 us
  starting transfers between devices: 15 us -> 12.5 us
  matrix products: 7.1 us -> 5.74 us
    all_gather x0 -> x1, blocking collectives: none -> 4.68 us  [local(): grid_rows = lax.all_gather(gathered, 'core', axis=0, tiled=True)]
    all_to_all x1, waiting for transfers between devices: 13 us -> 10.2 us  [local(): gathered = lax.all_to_all(copies, DEV, 0, 2, tiled=True)[0]]
    ppermute x1 -> x0, starting transfers between devices: 2.58 us -> none  [local(): partner = lax.ppermute(gathered, 'core', [(0, 1), (1, 0)])]
    dot_general x1, matrix products: 2.48 us -> 1.12 us  [local(): jnp.einsum('mkb,mcb->kmc', spectra_sin, swapped, preferred_element_type=j...]
  transfers between devices with their start and end apart: 3 -> 2, of which waited for: 2 -> 2; matrix products, arithmetic and copies ran while one was open for 2% -> 3% of each run, Pallas kernels for 0% -> 0%
where the time goes in v16:
time: 129 us; the launch traced here: 128 us
  blocking collectives  49.2 us (38%)
  local copies, waits for them, and re-layouts  21.4 us (17%)
  Pallas kernels  20.4 us (16%)
  starting transfers between devices  12.5 us (10%)
  waiting for transfers between devices  12.2 us (9%)
  matrix products  5.74 us (4%)
  other arithmetic  5.6 us (4%)
    all_gather x1, blocking collectives, local(): own = lax.all_gather(own, GRP, axis=0, tiled=False)  16.1 us
    all_to_all x1, blocking collectives, local(): own = jnp.sum(lax.all_to_all(packed, 'y', 1, 1, tiled=True), 1)  15.3 us
    unnamed x22, local copies, waits for them, and re-layouts  13.7 us
    all_to_all x1, blocking collectives, local(): own = jnp.sum(lax.all_to_all(own, 'z', 0, 0, tiled=True), 0)  13.1 us
    all_to_all x1, starting transfers between devices, local(): gathered = lax.all_to_all(copies, DEV, 0, 2, tiled=True)[0]  12 us
    pallas_call x1, Pallas kernels, local(): pl.pallas_call(functools.partial(norm_kernel, columns), grid=(steps,), in...  10.4 us
    all_to_all x1, waiting for transfers between devices, local(): gathered = lax.all_to_all(copies, DEV, 0, 2, tiled=True)[0]  10.2 us
    pallas_call x1, Pallas kernels, local(): pl.pallas_call(functools.partial(spectra_kernel, columns), grid=(steps,),...  9.92 us
  transfers between devices with their start and end apart: 2, of which 2 were waited for; matrix products, arithmetic and copies ran while one was open for 3% of the time, Pallas kernels for 0%

profile of v16, /device:TPU:1, one launch (start us, length us, event | category | flops | bytes accessed | tf_op | source)
XLA Modules:
  0.0 127.9 jit_solution(8241039573399336516)
XLA Ops:
  0.6 0.0 copy-start
  0.6 0.0 copy-start.6
  0.7 0.0 copy-start.5
  0.7 0.9 reshape.200
  1.6 0.1 broadcast_bitcast_fusion
  1.7 1.2 reshape.228
  2.9 12.0 %all-to-all-start = ((bf16[32,2,3072]{2,1,0:T(2,128)(2,1)}), bf16[32,2,3072]{2,1,0:T(2,128)(2,1)S(1)}, u32[]{:S(2)}, u32[]{:S(2)}) async-start(bf16[32,2,3072]{2,1,0:T(2,128)(2,1)} %reshape.228), calls=%async_computation | async-start | bytes 786432 | tf_op jit(solution)/shard_map/all_to_all | solution.py:107
  14.9 0.0 copy-done
  14.9 0.0 copy-done.6
  14.9 0.0 copy-done.5
  14.9 0.2 fusion.17
  15.1 1.5 %fusion = bf16[32,64,256]{2,1,0:T(8,128)(2,1)S(1)} fusion(bf16[32,64,256]{2,1,0:T(8,128)(2,1)} %bitcast.69, f32[64,256]{1,0:T(8,128)S(1)} %bitcast.70), kind=kLoop, calls=%fused_computation.3 | loop fusion | flops 1572864 | bytes 2162688 | tf_op jit(solution)/shard_map/convert_element_type | solution.py:46
  16.6 0.1 fusion.18
  16.7 0.1 pad_maximum_fusion
  16.7 0.1 multiply_convert_fusion.1
  16.8 0.7 copy.37.table_ref
  17.6 0.1 pad.4.clone
  17.7 0.1 pad.3.clone
  17.7 0.1 fusion.14
  17.8 0.7 maximum_maximum_fusion.turn_ref
  18.5 10.2 %all-to-all-done = bf16[32,2,3072]{2,1,0:T(2,128)(2,1)S(1)} async-done(((bf16[32,2,3072]{2,1,0:T(2,128)(2,1)}), bf16[32,2,3072]{2,1,0:T(2,128)(2,1)S(1)}, u32[]{:S(2)}, u32[]{:S(2)}) %all-to-all-start) | async-done | bytes 393248 | tf_op jit(solution)/shard_map/all_to_all | solution.py:107
  28.7 0.5 reshape.229
  29.2 0.0 copy-start.4
  29.2 0.7 copy.35
  29.8 4.7 %all_gather.9 = bf16[32,192,64]{1,2,0:T(8,128)(2,1)S(1)} all-gather(bf16[16,192,64]{1,2,0:T(8,128)(2,1)S(1)} %copy.35), channel_id=1, replica_groups=mesh['x'=4,'core'=2,'z'=8,'y'=4] {'core'}, dimensions={0}, use_global_device_ids=true | all-gather | bytes 1179648 | tf_op jit(solution)/shard_map/all_gather | solution.py:108
  34.5 0.3 multiply_reduce_fusion
  34.8 0.0 copy-done.4
  34.8 0.4 fusion.2
  35.2 0.9 copy.46
  36.1 1.0 convolution_convert_fusion.1
  37.1 3.5 %copy.44 = bf16[4,8,192,256]{3,1,2,0:T(8,128)(2,1)} copy(bf16[4,8,192,256]{3,2,1,0:T(8,128)(2,1)S(1)} %bitcast.60) | data formatting | bytes 6291456
  40.6 1.0 convolution_convert_fusion
  41.6 3.5 %copy.45 = bf16[4,8,192,256]{3,1,2,0:T(8,128)(2,1)} copy(bf16[4,8,192,256]{3,2,1,0:T(8,128)(2,1)S(1)} %bitcast.59) | data formatting | bytes 6291456
  45.1 10.4 %shard_map.77.norm_ref = f32[1,256]{1,0:T(1,128)} custom-call(bf16[128,64]{1,0:T(8,128)(2,1)} %copy.37.table_ref, bf16[32,49152]{1,0:T(8,128)(2,1)} %bitcast.54, bf16[32,49152]{1,0:T(8,128)(2,1)} %bitcast.56, f32[1,49152]{1,0:T(1,128)} %bitcast.66), custom_call_target="tpu_custom_call" | custom-call | tf_op jit(solution)/shard_map/pallas_call | solution.py:134
  55.5 9.9 %shard_map.78 = (bf16[32,49152]{1,0:T(8,128)(2,1)}, bf16[32,49152]{1,0:T(8,128)(2,1)}, f32[1,49152]{1,0:T(1,128)}) custom-call(bf16[128,64]{1,0:T(8,128)(2,1)} %copy.37.table_ref, bf16[32,49152]{1,0:T(8,128)(2,1)} %bitcast.55, bf16[32,49152]{1,0:T(8,128)(2,1)} %bitcast.57, f32[1,49152]{1,0:T(1,128)} %bitcast.67, f32[1,256]{1,0:T(1,128)} %shard_map.77.norm_ref, ...), custom_call_target="tpu_custom_call" | custom-call | tf_op jit(solution)/shard_map/pallas_call | solution.py:143
  65.5 2.6 %copy.47 = bf16[4,8,192,256]{3,2,1,0:T(8,128)(2,1)S(1)} copy(bf16[4,8,192,256]{3,1,2,0:T(8,128)(2,1)} %bitcast.64) | data formatting | bytes 6291456
  68.1 0.0 copy-start.2
  68.1 1.1 fusion.19
  69.2 0.8 copy-done.2
  70.0 0.7 copy.48
  70.7 1.1 convolution_add_fusion
  71.9 1.7 %copy.38 = f32[192,2048]{1,0:T(8,128)} copy(f32[192,2048]{0,1:T(8,128)S(1)} %bitcast.62) | data formatting | bytes 3145728 | tf_op jit(solution)/shard_map/reshape | solution.py:168
  73.6 0.5 broadcast.233
  74.1 0.0 copy-done.3
  74.1 1.1 reduce.5
  75.2 0.1 reshape.207
  75.3 0.9 fusion.20
  76.2 0.1 reduce_sum.46
  76.3 0.8 copy.40
  77.1 1.1 concatenate.14
  78.3 0.1 constant_dynamic-slice_fusion
  78.3 0.5 collective-permute-start
  78.8 2.1 %collective-permute-done = f32[192,1152]{1,0:T(8,128)S(1)} collective-permute-done((f32[192,1152]{1,0:T(8,128)S(1)}, f32[192,1152]{1,0:T(8,128)S(1)}, u32[]{:S(2)}, u32[]{:S(2)}) %collective-permute-start) | collective-permute-done | bytes 884768 | tf_op jit(solution)/shard_map/ppermute | solution.py:181
  80.8 0.1 dynamic-slice_add_fusion
  81.0 0.1 reshape.208
  81.1 0.5 copy.41
  81.6 15.3 %all_to_all.25 = f32[8,4,6,1152]{3,0,2,1:T(8,128)S(1)} all-to-all(f32[8,4,6,1152]{3,0,2,1:T(8,128)S(1)} %copy.41), channel_id=1, replica_groups=mesh['x'=4,'core'=2,'z'=8,'y'=4] {'y'}, dimensions={1} | all-to-all | bytes 1769472 | tf_op jit(solution)/shard_map/all_to_all | solution.py:183
  97.0 0.1 copy.42
  97.0 13.1 %all_to_all.26 = f32[8,6,1152]{2,1,0:T(8,128)S(1)} all-to-all(f32[8,6,1152]{2,1,0:T(8,128)S(1)} %copy.42), channel_id=1, replica_groups=mesh['x'=4,'core'=2,'z'=8,'y'=4] {'z'}, dimensions={0} | all-to-all | bytes 442368 | tf_op jit(solution)/shard_map/all_to_all | solution.py:184
  110.1 16.1 %all-gather.1 = f32[8,6,1152]{2,1,0:T(8,128)S(1)} all-gather(f32[1,6,1152]{2,1,0:T(8,128)S(1)} %bitcast.71), channel_id=2, replica_groups=mesh['x'=4,'core'=2,'z'=8,'y'=4] {'x','core'}, dimensions={0}, use_global_device_ids=true | all-gather | bytes 248832 | tf_op jit(solution)/shard_map/all_gather | solution.py:185
  126.3 0.7 fusion.16
  127.0 0.1 div.21
  127.0 0.2 div.22
  127.3 0.7 fusion.3
  (15 shorter events, 0.2 us)
Async XLA Ops:
  0.6 14.3 %copy-start = (f32[64,32]{0,1:T(8,128)S(1)}, f32[64,32]{0,1:T(8,128)}, u32[]{:S(2)}) copy-start(f32[64,32]{0,1:T(8,128)} %param.9) | copy-start | bytes 24580
  0.6 14.3 %copy-start.6 = (f32[32]{0:T(128)S(1)}, f32[32]{0:T(128)}, u32[]{:S(2)}) copy-start(f32[32]{0:T(128)} %param.10) | copy-start | bytes 388
  0.7 14.3 %copy-start.5 = (s32[256]{0:T(256)S(1)}, s32[256]{0:T(256)}, u32[]{:S(2)}) copy-start(s32[256]{0:T(256)} %param.8) | copy-start | bytes 3076
  2.9 25.8 %all-to-all-start = ((bf16[32,2,3072]{2,1,0:T(2,128)(2,1)}), bf16[32,2,3072]{2,1,0:T(2,128)(2,1)S(1)}, u32[]{:S(2)}, u32[]{:S(2)}) async-start(bf16[32,2,3072]{2,1,0:T(2,128)(2,1)} %reshape.228), calls=%async_computation | async-start | bytes 786432 | tf_op jit(solution)/shard_map/all_to_all | solution.py:107
  29.2 5.7 %copy-start.4 = (f32[192]{0:T(256)S(1)}, f32[192]{0:T(256)}, u32[]{:S(2)}) copy-start(f32[192]{0:T(256)} %param.11) | copy-start | bytes 2308
  68.1 1.9 %copy-start.2 = (bf16[32,49152]{1,0:T(8,128)(2,1)S(1)}, bf16[32,49152]{1,0:T(8,128)(2,1)}, u32[]{:S(2)}) copy-start(bf16[32,49152]{1,0:T(8,128)(2,1)} %get-tuple-element.12) | copy-start | bytes 9437188
  71.9 2.2 %copy-start.3 = (f32[1,49152]{1,0:T(1,128)S(1)}, f32[1,49152]{1,0:T(1,128)}, u32[]{:S(2)}) copy-start(f32[1,49152]{1,0:T(1,128)} %get-tuple-element.13) | copy-start | bytes 589828
  73.6 3.5 %copy-start.1 = (f32[192,2048]{1,0:T(8,128)S(1)}, f32[192,2048]{1,0:T(8,128)}, u32[]{:S(2)}) copy-start(f32[192,2048]{1,0:T(8,128)} %copy.38) | copy-start | bytes 4718596
  78.3 2.5 %collective-permute-start = (f32[192,1152]{1,0:T(8,128)S(1)}, f32[192,1152]{1,0:T(8,128)S(1)}, u32[]{:S(2)}, u32[]{:S(2)}) collective-permute-start(f32[192,1152]{1,0:T(8,128)S(1)} %constant_dynamic-slice_fusion), channel_id=1, source_target_pairs={{0,32},{32,0},{1,33},{33,1},{2,34},{34,2},{3,35},{35,3},{4,36},{36... | collective-permute-start | bytes 2654216 | tf_op jit(solution)/shard_map/ppermute | solution.py:181

commit v17 on v16

--- a/solution.py
+++ b/solution.py
@@ -78,7 +78,7 @@
 
 
 def spectra_kernel(
-    cols, table_ref, real_ref, imag_ref, bias_ref, norm_ref, turn_ref, cos_ref, sin_ref, weight_ref
+    cols, table_ref, real_ref, imag_ref, bias_ref, norm_ref, turn_ref, spectra_ref, weight_ref
 ):
     norm_row = jnp.concatenate([norm_ref[...]] * (bias_ref.shape[1] // cols), 1)
     scores = block_scores(table_ref, real_ref, imag_ref, bias_ref)
@@ -86,9 +86,13 @@
     full = jnp.dot(
         turn_ref[...], responsibility.astype(jnp.bfloat16), preferred_element_type=jnp.float32
     )
-    rows = cos_ref.shape[0]
-    cos_ref[...] = full[:rows].astype(jnp.bfloat16)
-    sin_ref[...] = full[rows : 2 * rows].astype(jnp.bfloat16)
+    rows = spectra_ref.shape[0]
+    for j in range(full.shape[1] // cols):
+        part = full[:, j * cols : (j + 1) * cols]
+        spectra_ref[:, 2 * j * cols : (2 * j + 1) * cols] = part[:rows].astype(jnp.bfloat16)
+        spectra_ref[:, (2 * j + 1) * cols : (2 * j + 2) * cols] = part[rows : 2 * rows].astype(
+            jnp.bfloat16
+        )
     weight_ref[...] = full[2 * rows : 2 * rows + 1]
 
 
@@ -140,7 +144,7 @@
         scratch_shapes=[pltpu.VMEM((1, columns), jnp.float32)] * 2,
         compiler_params=pltpu.CompilerParams(dimension_semantics=("arbitrary",)),
     )(table, crossed_real, crossed_imag, bias)
-    spectra_cos, spectra_sin, class_weight = pl.pallas_call(
+    spectra, class_weight = pl.pallas_call(
         functools.partial(spectra_kernel, columns),
         grid=(steps,),
         in_specs=[
@@ -151,20 +155,17 @@
             pl.BlockSpec((1, columns), lambda i: (0, 0)),
             pl.BlockSpec(turn.shape, lambda i: (0, 0)),
         ],
-        out_specs=[crossed_spec, crossed_spec, row_spec],
+        out_specs=[pl.BlockSpec((rows, 2 * block), lambda i: (0, i)), row_spec],
         out_shape=[
-            jax.ShapeDtypeStruct((rows, width), jnp.bfloat16),
-            jax.ShapeDtypeStruct((rows, width), jnp.bfloat16),
+            jax.ShapeDtypeStruct((rows, 2 * width), jnp.bfloat16),
             jax.ShapeDtypeStruct((1, width), jnp.float32),
         ],
         compiler_params=pltpu.CompilerParams(dimension_semantics=("arbitrary",)),
     )(table, crossed_real, crossed_imag, bias, log_norm, turn)
 
-    spectra_cos = spectra_cos.reshape(M, classes_total, columns)
-    spectra_sin = spectra_sin.reshape(M, classes_total, columns)
-    numer_all = jnp.einsum(
-        "mkb,mcb->kmc", spectra_cos, weighted, preferred_element_type=jnp.float32
-    ) + jnp.einsum("mkb,mcb->kmc", spectra_sin, swapped, preferred_element_type=jnp.float32)
+    spectra = spectra.reshape(M, classes_total, 2 * columns)
+    paired = jnp.concatenate([weighted, swapped], 2)
+    numer_all = jnp.einsum("mkb,mcb->kmc", spectra, paired, preferred_element_type=jnp.float32)
     numer_all = numer_all.reshape(classes_total, 2 * M * Q)
     class_weight = class_weight.reshape(classes_total, columns)
     cycles_all = jnp.dot(class_weight, power_term.T, precision=lax.Precision.HIGHEST)

time: 129 us -> 131 us (1.016)
    dot_general x2 -> x1, matrix products: 2.25 us -> 3.46 us  [local(): jnp.einsum('mkb,mcb->kmc', spectra, paired, preferred_element_type=jnp.fl...]
    unnamed x22 -> x19, local copies, waits for them, and re-layouts: 13.7 us -> 14.7 us
  transfers between devices with their start and end apart: 2 -> 2, of which waited for: 2 -> 2; matrix products, arithmetic and copies ran while one was open for 3% -> 2% of each run, Pallas kernels for 0% -> 0%
where the time goes in v17:
time: 131 us; the launch traced here: 130 us
  blocking collectives  49.2 us (38%)
  local copies, waits for them, and re-layouts  22.7 us (17%)
  Pallas kernels  20.3 us (15%)
  waiting for transfers between devices  13.4 us (10%)
  starting transfers between devices  12.5 us (10%)
  matrix products  6.95 us (5%)
  other arithmetic  4.39 us (3%)
    all_gather x1, blocking collectives, local(): own = lax.all_gather(own, GRP, axis=0, tiled=False)  16.2 us
    all_to_all x1, blocking collectives, local(): own = jnp.sum(lax.all_to_all(packed, 'y', 1, 1, tiled=True), 1)  15.3 us
    unnamed x19, local copies, waits for them, and re-layouts  14.7 us
    all_to_all x1, blocking collectives, local(): own = jnp.sum(lax.all_to_all(own, 'z', 0, 0, tiled=True), 0)  13 us
    all_to_all x1, starting transfers between devices, local(): gathered = lax.all_to_all(copies, DEV, 0, 2, tiled=True)[0]  12 us
    all_to_all x1, waiting for transfers between devices, local(): gathered = lax.all_to_all(copies, DEV, 0, 2, tiled=True)[0]  11.4 us
    pallas_call x1, Pallas kernels, local(): pl.pallas_call(functools.partial(norm_kernel, columns), grid=(steps,), in...  10.4 us
    pallas_call x1, Pallas kernels, local(): pl.pallas_call(functools.partial(spectra_kernel, columns), grid=(steps,),...  9.91 us
  transfers between devices with their start and end apart: 2, of which 2 were waited for; matrix products, arithmetic and copies ran while one was open for 2% of the time, Pallas kernels for 0%

profile of v17, /device:TPU:1, one launch (start us, length us, event | category | flops | bytes accessed | tf_op | source)
XLA Modules:
  0.0 130.4 jit_solution(577396401444016873)
XLA Ops:
  0.6 0.0 copy-start
  0.6 0.0 copy-start.5
  0.7 0.0 copy-start.4
  0.7 0.0 copy-start.1
  0.7 1.0 reshape.197
  1.7 0.1 broadcast_bitcast_fusion
  1.8 1.2 reshape.224
  2.9 12.0 %all-to-all-start = ((bf16[32,2,3072]{2,1,0:T(2,128)(2,1)}), bf16[32,2,3072]{2,1,0:T(2,128)(2,1)S(1)}, u32[]{:S(2)}, u32[]{:S(2)}) async-start(bf16[32,2,3072]{2,1,0:T(2,128)(2,1)} %reshape.224), calls=%async_computation | async-start | bytes 786432 | tf_op jit(solution)/shard_map/all_to_all | solution.py:111
  15.0 0.0 copy-done
  15.0 0.0 copy-done.5
  15.0 0.0 copy-done.4
  15.0 0.2 fusion.22
  15.2 0.0 copy-done.1
  15.2 0.3 fusion.4
  15.5 0.1 fusion.23
  15.6 0.1 pad_maximum_fusion
  15.6 0.1 multiply_convert_fusion.1
  15.7 0.7 copy.37.table_ref
  16.5 0.1 pad.4.clone
  16.6 0.1 pad.3.clone
  16.6 0.1 fusion.18
  16.7 0.7 maximum_maximum_fusion.turn_ref
  17.4 11.4 %all-to-all-done = bf16[32,2,3072]{2,1,0:T(2,128)(2,1)S(1)} async-done(((bf16[32,2,3072]{2,1,0:T(2,128)(2,1)}), bf16[32,2,3072]{2,1,0:T(2,128)(2,1)S(1)}, u32[]{:S(2)}, u32[]{:S(2)}) %all-to-all-start) | async-done | bytes 393248 | tf_op jit(solution)/shard_map/all_to_all | solution.py:111
  28.8 0.5 reshape.225
  29.3 0.0 copy-start.3
  29.3 0.7 copy.35
  29.9 4.7 %all_gather.9 = bf16[32,192,64]{1,2,0:T(8,128)(2,1)S(1)} all-gather(bf16[16,192,64]{1,2,0:T(8,128)(2,1)S(1)} %copy.35), channel_id=1, replica_groups=mesh['x'=4,'core'=2,'z'=8,'y'=4] {'core'}, dimensions={0}, use_global_device_ids=true | all-gather | bytes 1179648 | tf_op jit(solution)/shard_map/all_gather | solution.py:112
  34.6 0.3 multiply_reduce_fusion
  34.9 0.0 copy-done.3
  34.9 0.4 fusion.6
  35.3 0.9 copy.46
  36.2 1.0 convolution_convert_fusion
  37.2 3.4 %copy.45 = bf16[4,8,192,256]{3,1,2,0:T(8,128)(2,1)} copy(bf16[4,8,192,256]{3,2,1,0:T(8,128)(2,1)S(1)} %bitcast.55) | data formatting | bytes 6291456
  40.6 1.0 convolution_convert_fusion.1
  41.7 3.5 %copy.44 = bf16[4,8,192,256]{3,1,2,0:T(8,128)(2,1)} copy(bf16[4,8,192,256]{3,2,1,0:T(8,128)(2,1)S(1)} %bitcast.54) | data formatting | bytes 6291456
  45.2 10.4 %shard_map.77.norm_ref = f32[1,256]{1,0:T(1,128)} custom-call(bf16[128,64]{1,0:T(8,128)(2,1)} %copy.37.table_ref, bf16[32,49152]{1,0:T(8,128)(2,1)} %bitcast.51, bf16[32,49152]{1,0:T(8,128)(2,1)} %bitcast.49, f32[1,49152]{1,0:T(1,128)} %bitcast.59), custom_call_target="tpu_custom_call" | custom-call | tf_op jit(solution)/shard_map/pallas_call | solution.py:138
  55.6 9.9 %shard_map.78 = (bf16[32,98304]{1,0:T(8,128)(2,1)}, f32[1,49152]{1,0:T(1,128)}) custom-call(bf16[128,64]{1,0:T(8,128)(2,1)} %copy.37.table_ref, bf16[32,49152]{1,0:T(8,128)(2,1)} %bitcast.52, bf16[32,49152]{1,0:T(8,128)(2,1)} %bitcast.50, f32[1,49152]{1,0:T(1,128)} %bitcast.60, f32[1,256]{1,0:T(1,128)} %shard_map.77.norm_ref, ...), custom_call_target="tpu_custom_call" | custom-call | tf_op jit(solution)/shard_map/pallas_call | solution.py:147
  65.5 5.2 %copy.47 = bf16[4,8,192,512]{3,2,1,0:T(8,128)(2,1)S(1)} copy(bf16[4,8,192,512]{3,1,2,0:T(8,128)(2,1)} %bitcast.57) | data formatting | bytes 12582912
  70.7 3.5 %fusion = f32[32,64,192]{2,1,0:T(8,128)} fusion(bf16[32,192,512]{2,1,0:T(8,128)(2,1)S(1)} %bitcast.53, bf16[32,64,256]{2,1,0:T(8,128)(2,1)S(1)} %pad_maximum_fusion, bf16[32,64,256]{2,1,0:T(8,128)(2,1)S(1)} %fusion.4), kind=kOutput, calls=%fused_computation.2 | convolution fusion | flops 406847488 | bytes 9961472 | tf_op jit(solution)/shard_map/mkb,mcb->kmc/dot_general | solution.py:168
  74.1 0.0 copy-start.2
  74.1 1.9 %copy.38 = f32[192,2048]{1,0:T(8,128)S(1)} copy(f32[192,2048]{0,1:T(8,128)} %bitcast.56) | data formatting | bytes 3145728 | tf_op jit(solution)/shard_map/reshape | solution.py:169
  76.1 0.5 broadcast.233
  76.6 0.0 copy-done.2
  76.6 1.1 reduce.5
  77.7 0.1 reshape.203
  77.8 0.9 fusion.24
  78.7 0.1 reduce_sum.46
  78.8 0.8 copy.40
  79.6 1.1 concatenate.18
  80.7 0.1 constant_dynamic-slice_fusion
  80.8 0.5 collective-permute-start
  81.3 2.1 %collective-permute-done = f32[192,1152]{1,0:T(8,128)S(1)} collective-permute-done((f32[192,1152]{1,0:T(8,128)S(1)}, f32[192,1152]{1,0:T(8,128)S(1)}, u32[]{:S(2)}, u32[]{:S(2)}) %collective-permute-start) | collective-permute-done | bytes 884768 | tf_op jit(solution)/shard_map/ppermute | solution.py:182
  83.3 0.1 dynamic-slice_add_fusion
  83.5 0.1 reshape.204
  83.6 0.5 copy.41
  84.1 15.3 %all_to_all.25 = f32[8,4,6,1152]{3,0,2,1:T(8,128)S(1)} all-to-all(f32[8,4,6,1152]{3,0,2,1:T(8,128)S(1)} %copy.41), channel_id=1, replica_groups=mesh['x'=4,'core'=2,'z'=8,'y'=4] {'y'}, dimensions={1} | all-to-all | bytes 1769472 | tf_op jit(solution)/shard_map/all_to_all | solution.py:184
  99.5 0.1 copy.42
  99.5 13.0 %all_to_all.26 = f32[8,6,1152]{2,1,0:T(8,128)S(1)} all-to-all(f32[8,6,1152]{2,1,0:T(8,128)S(1)} %copy.42), channel_id=1, replica_groups=mesh['x'=4,'core'=2,'z'=8,'y'=4] {'z'}, dimensions={0} | all-to-all | bytes 442368 | tf_op jit(solution)/shard_map/all_to_all | solution.py:185
  112.6 16.2 %all-gather.1 = f32[8,6,1152]{2,1,0:T(8,128)S(1)} all-gather(f32[1,6,1152]{2,1,0:T(8,128)S(1)} %bitcast.64), channel_id=2, replica_groups=mesh['x'=4,'core'=2,'z'=8,'y'=4] {'x','core'}, dimensions={0}, use_global_device_ids=true | all-gather | bytes 248832 | tf_op jit(solution)/shard_map/all_gather | solution.py:186
  128.8 0.7 fusion.20
  129.5 0.1 div.21
  129.6 0.2 div.22
  129.8 0.7 fusion.7
  (12 shorter events, 0.2 us)
Async XLA Ops:
  0.6 14.4 %copy-start = (f32[64,32]{0,1:T(8,128)S(1)}, f32[64,32]{0,1:T(8,128)}, u32[]{:S(2)}) copy-start(f32[64,32]{0,1:T(8,128)} %param.9) | copy-start | bytes 24580
  0.6 14.4 %copy-start.5 = (f32[32]{0:T(128)S(1)}, f32[32]{0:T(128)}, u32[]{:S(2)}) copy-start(f32[32]{0:T(128)} %param.10) | copy-start | bytes 388
  0.7 14.4 %copy-start.4 = (s32[256]{0:T(256)S(1)}, s32[256]{0:T(256)}, u32[]{:S(2)}) copy-start(s32[256]{0:T(256)} %param.8) | copy-start | bytes 3076
  0.7 14.5 %copy-start.1 = (bf16[2048,256]{1,0:T(8,128)(2,1)S(1)}, bf16[2048,256]{1,0:T(8,128)(2,1)}, u32[]{:S(2)}) copy-start(bf16[2048,256]{1,0:T(8,128)(2,1)} %param.7) | copy-start | bytes 3145732
  2.9 25.8 %all-to-all-start = ((bf16[32,2,3072]{2,1,0:T(2,128)(2,1)}), bf16[32,2,3072]{2,1,0:T(2,128)(2,1)S(1)}, u32[]{:S(2)}, u32[]{:S(2)}) async-start(bf16[32,2,3072]{2,1,0:T(2,128)(2,1)} %reshape.224), calls=%async_computation | async-start | bytes 786432 | tf_op jit(solution)/shard_map/all_to_all | solution.py:111
  29.3 5.7 %copy-start.3 = (f32[192]{0:T(256)S(1)}, f32[192]{0:T(256)}, u32[]{:S(2)}) copy-start(f32[192]{0:T(256)} %param.11) | copy-start | bytes 2308
  74.1 2.4 %copy-start.2 = (f32[1,49152]{1,0:T(1,128)S(1)}, f32[1,49152]{1,0:T(1,128)}, u32[]{:S(2)}) copy-start(f32[1,49152]{1,0:T(1,128)} %get-tuple-element.11) | copy-start | bytes 589828
  80.8 2.5 %collective-permute-start = (f32[192,1152]{1,0:T(8,128)S(1)}, f32[192,1152]{1,0:T(8,128)S(1)}, u32[]{:S(2)}, u32[]{:S(2)}) collective-permute-start(f32[192,1152]{1,0:T(8,128)S(1)} %constant_dynamic-slice_fusion), channel_id=1, source_target_pairs={{0,32},{32,0},{1,33},{33,1},{2,34},{34,2},{3,35},{35,3},{4,36},{36... | collective-permute-start | bytes 2654216 | tf_op jit(solution)/shard_map/ppermute | solution.py:182

commit v18 on v16

--- a/solution.py
+++ b/solution.py
@@ -182,9 +182,8 @@
     packed = packed.reshape(lax.axis_size("z"), lax.axis_size("y"), CLS_DEV, half)
     own = jnp.sum(lax.all_to_all(packed, "y", 1, 1, tiled=True), 1)
     own = jnp.sum(lax.all_to_all(own, "z", 0, 0, tiled=True), 0)
-    own = lax.all_gather(own, GRP, axis=0, tiled=False)
-    own = jnp.sum(own.reshape(lax.axis_size("x"), core_count, CLS_DEV, half), 0)
-    own = jnp.concatenate([own[0], own[1]], 1)
+    own = jnp.sum(lax.all_gather(own, "x", axis=0, tiled=False), 0)
+    own = lax.all_gather(own, "core", axis=1, tiled=True)
     numerator = own[:, :width]
     cycle_sum = own[:, width : width + Q]
     class_mass = own[:, width + Q]

time: 129 us -> 129 us (level)
    all_gather x1 -> x2, blocking collectives: 16.1 us -> 17 us  [the longest x1 9.46 us: local(): own = jnp.sum(lax.all_gather(own, 'x', axis=0, tiled=False), 0)]
where the time goes in v18:
time: 129 us
  blocking collectives  50 us (39%)
  local copies, waits for them, and re-layouts  21.4 us (17%)
  Pallas kernels  20.4 us (16%)
  starting transfers between devices  12.5 us (10%)
  waiting for transfers between devices  12.2 us (9%)
  matrix products  5.74 us (4%)
  other arithmetic  5.58 us (4%)
    all_to_all x1, blocking collectives, local(): own = jnp.sum(lax.all_to_all(packed, 'y', 1, 1, tiled=True), 1)  15.3 us
    unnamed x22, local copies, waits for them, and re-layouts  13.7 us
    all_to_all x1, blocking collectives, local(): own = jnp.sum(lax.all_to_all(own, 'z', 0, 0, tiled=True), 0)  13.1 us
    all_to_all x1, starting transfers between devices, local(): gathered = lax.all_to_all(copies, DEV, 0, 2, tiled=True)[0]  12 us
    pallas_call x1, Pallas kernels, local(): pl.pallas_call(functools.partial(norm_kernel, columns), grid=(steps,), in...  10.4 us
    all_to_all x1, waiting for transfers between devices, local(): gathered = lax.all_to_all(copies, DEV, 0, 2, tiled=True)[0]  10.2 us
    pallas_call x1, Pallas kernels, local(): pl.pallas_call(functools.partial(spectra_kernel, columns), grid=(steps,),...  9.92 us
    all_gather x1, blocking collectives, local(): own = jnp.sum(lax.all_gather(own, 'x', axis=0, tiled=False), 0)  9.46 us
  transfers between devices with their start and end apart: 2, of which 2 were waited for; matrix products, arithmetic and copies ran while one was open for 3% of the time, Pallas kernels for 0%

profile of v18, /device:TPU:1, one launch (start us, length us, event | category | flops | bytes accessed | tf_op | source)
XLA Modules:
  0.0 128.7 jit_solution(3362496975825717366)
XLA Ops:
  0.6 0.0 copy-start
  0.6 0.0 copy-start.6
  0.7 0.0 copy-start.5
  0.7 0.9 reshape.197
  1.6 0.1 broadcast_bitcast_fusion
  1.7 1.2 reshape.223
  2.9 12.0 %all-to-all-start = ((bf16[32,2,3072]{2,1,0:T(2,128)(2,1)}), bf16[32,2,3072]{2,1,0:T(2,128)(2,1)S(1)}, u32[]{:S(2)}, u32[]{:S(2)}) async-start(bf16[32,2,3072]{2,1,0:T(2,128)(2,1)} %reshape.223), calls=%async_computation | async-start | bytes 786432 | tf_op jit(solution)/shard_map/all_to_all | solution.py:107
  14.9 0.0 copy-done
  14.9 0.0 copy-done.6
  14.9 0.0 copy-done.5
  14.9 0.2 fusion.16
  15.1 1.5 %fusion = bf16[32,64,256]{2,1,0:T(8,128)(2,1)S(1)} fusion(bf16[32,64,256]{2,1,0:T(8,128)(2,1)} %bitcast.63, f32[64,256]{1,0:T(8,128)S(1)} %bitcast.64), kind=kLoop, calls=%fused_computation.3 | loop fusion | flops 1572864 | bytes 2162688 | tf_op jit(solution)/shard_map/convert_element_type | solution.py:46
  16.6 0.1 fusion.17
  16.7 0.1 pad_maximum_fusion
  16.7 0.1 multiply_convert_fusion.1
  16.8 0.7 copy.37.table_ref
  17.6 0.1 pad.2.clone
  17.7 0.1 pad.1.clone
  17.7 0.1 fusion.13
  17.8 0.7 maximum_maximum_fusion.turn_ref
  18.5 10.2 %all-to-all-done = bf16[32,2,3072]{2,1,0:T(2,128)(2,1)S(1)} async-done(((bf16[32,2,3072]{2,1,0:T(2,128)(2,1)}), bf16[32,2,3072]{2,1,0:T(2,128)(2,1)S(1)}, u32[]{:S(2)}, u32[]{:S(2)}) %all-to-all-start) | async-done | bytes 393248 | tf_op jit(solution)/shard_map/all_to_all | solution.py:107
  28.7 0.5 reshape.224
  29.2 0.0 copy-start.4
  29.2 0.7 copy.35
  29.8 4.7 %all_gather.12 = bf16[32,192,64]{1,2,0:T(8,128)(2,1)S(1)} all-gather(bf16[16,192,64]{1,2,0:T(8,128)(2,1)S(1)} %copy.35), channel_id=1, replica_groups=mesh['x'=4,'core'=2,'z'=8,'y'=4] {'core'}, dimensions={0}, use_global_device_ids=true | all-gather | bytes 1179648 | tf_op jit(solution)/shard_map/all_gather | solution.py:108
  34.5 0.3 multiply_reduce_fusion
  34.8 0.0 copy-done.4
  34.8 0.4 fusion.2
  35.2 0.9 copy.46
  36.1 1.0 convolution_convert_fusion.1
  37.1 3.5 %copy.44 = bf16[4,8,192,256]{3,1,2,0:T(8,128)(2,1)} copy(bf16[4,8,192,256]{3,2,1,0:T(8,128)(2,1)S(1)} %bitcast.55) | data formatting | bytes 6291456
  40.6 1.0 convolution_convert_fusion
  41.6 3.5 %copy.45 = bf16[4,8,192,256]{3,1,2,0:T(8,128)(2,1)} copy(bf16[4,8,192,256]{3,2,1,0:T(8,128)(2,1)S(1)} %bitcast.54) | data formatting | bytes 6291456
  45.1 10.4 %shard_map.77.norm_ref = f32[1,256]{1,0:T(1,128)} custom-call(bf16[128,64]{1,0:T(8,128)(2,1)} %copy.37.table_ref, bf16[32,49152]{1,0:T(8,128)(2,1)} %bitcast.49, bf16[32,49152]{1,0:T(8,128)(2,1)} %bitcast.51, f32[1,49152]{1,0:T(1,128)} %bitcast.61), custom_call_target="tpu_custom_call" | custom-call | tf_op jit(solution)/shard_map/pallas_call | solution.py:134
  55.5 9.9 %shard_map.78 = (bf16[32,49152]{1,0:T(8,128)(2,1)}, bf16[32,49152]{1,0:T(8,128)(2,1)}, f32[1,49152]{1,0:T(1,128)}) custom-call(bf16[128,64]{1,0:T(8,128)(2,1)} %copy.37.table_ref, bf16[32,49152]{1,0:T(8,128)(2,1)} %bitcast.50, bf16[32,49152]{1,0:T(8,128)(2,1)} %bitcast.52, f32[1,49152]{1,0:T(1,128)} %bitcast.62, f32[1,256]{1,0:T(1,128)} %shard_map.77.norm_ref, ...), custom_call_target="tpu_custom_call" | custom-call | tf_op jit(solution)/shard_map/pallas_call | solution.py:143
  65.5 2.6 %copy.47 = bf16[4,8,192,256]{3,2,1,0:T(8,128)(2,1)S(1)} copy(bf16[4,8,192,256]{3,1,2,0:T(8,128)(2,1)} %bitcast.59) | data formatting | bytes 6291456
  68.1 1.1 fusion.18
  69.2 0.8 copy-done.2
  70.0 0.7 copy.48
  70.7 1.1 convolution_add_fusion
  71.9 1.7 %copy.38 = f32[192,2048]{1,0:T(8,128)} copy(f32[192,2048]{0,1:T(8,128)S(1)} %bitcast.57) | data formatting | bytes 3145728 | tf_op jit(solution)/shard_map/reshape | solution.py:168
  73.6 0.5 broadcast.233
  74.1 0.0 copy-done.3
  74.1 1.1 reduce.6
  75.2 0.1 reshape.204
  75.3 0.9 fusion.19
  76.2 0.1 reduce_sum.46
  76.3 0.8 copy.40
  77.1 1.1 concatenate.11
  78.3 0.1 constant_dynamic-slice_fusion
  78.3 0.5 collective-permute-start
  78.8 2.1 %collective-permute-done = f32[192,1152]{1,0:T(8,128)S(1)} collective-permute-done((f32[192,1152]{1,0:T(8,128)S(1)}, f32[192,1152]{1,0:T(8,128)S(1)}, u32[]{:S(2)}, u32[]{:S(2)}) %collective-permute-start) | collective-permute-done | bytes 884768 | tf_op jit(solution)/shard_map/ppermute | solution.py:181
  80.8 0.1 dynamic-slice_add_fusion
  81.0 0.1 reshape.205
  81.1 0.5 copy.41
  81.6 15.3 %all_to_all.25 = f32[8,4,6,1152]{3,0,2,1:T(8,128)S(1)} all-to-all(f32[8,4,6,1152]{3,0,2,1:T(8,128)S(1)} %copy.41), channel_id=1, replica_groups=mesh['x'=4,'core'=2,'z'=8,'y'=4] {'y'}, dimensions={1} | all-to-all | bytes 1769472 | tf_op jit(solution)/shard_map/all_to_all | solution.py:183
  97.0 0.1 copy.42
  97.0 13.1 %all_to_all.26 = f32[8,6,1152]{2,1,0:T(8,128)S(1)} all-to-all(f32[8,6,1152]{2,1,0:T(8,128)S(1)} %copy.42), channel_id=1, replica_groups=mesh['x'=4,'core'=2,'z'=8,'y'=4] {'z'}, dimensions={0} | all-to-all | bytes 442368 | tf_op jit(solution)/shard_map/all_to_all | solution.py:184
  110.1 9.5 %all-gather.1 = f32[4,6,1152]{2,1,0:T(8,128)S(1)} all-gather(f32[1,6,1152]{2,1,0:T(8,128)S(1)} %bitcast.65), channel_id=2, replica_groups=mesh['x'=4,'core'=2,'z'=8,'y'=4] {'x'}, dimensions={0}, use_global_device_ids=true | all-gather | bytes 138240 | tf_op jit(solution)/shard_map/all_gather | solution.py:185
  119.6 7.5 %all_gather.15 = f32[6,2304]{1,0:T(8,128)S(1)} all-gather(f32[6,1152]{1,0:T(8,128)S(1)} %reduce_sum.49), channel_id=1, replica_groups=mesh['x'=4,'core'=2,'z'=8,'y'=4] {'core'}, dimensions={1}, use_global_device_ids=true | all-gather | bytes 82944 | tf_op jit(solution)/shard_map/all_gather | solution.py:186
  127.1 0.7 fusion.15
  127.8 0.1 div.21
  127.8 0.2 div.22
  128.1 0.7 slice_divide_fusion
  (15 shorter events, 0.1 us)
Async XLA Ops:
  0.6 14.3 %copy-start = (f32[64,32]{0,1:T(8,128)S(1)}, f32[64,32]{0,1:T(8,128)}, u32[]{:S(2)}) copy-start(f32[64,32]{0,1:T(8,128)} %param.9) | copy-start | bytes 24580
  0.6 14.3 %copy-start.6 = (f32[32]{0:T(128)S(1)}, f32[32]{0:T(128)}, u32[]{:S(2)}) copy-start(f32[32]{0:T(128)} %param.10) | copy-start | bytes 388
  0.7 14.3 %copy-start.5 = (s32[256]{0:T(256)S(1)}, s32[256]{0:T(256)}, u32[]{:S(2)}) copy-start(s32[256]{0:T(256)} %param.8) | copy-start | bytes 3076
  2.9 25.8 %all-to-all-start = ((bf16[32,2,3072]{2,1,0:T(2,128)(2,1)}), bf16[32,2,3072]{2,1,0:T(2,128)(2,1)S(1)}, u32[]{:S(2)}, u32[]{:S(2)}) async-start(bf16[32,2,3072]{2,1,0:T(2,128)(2,1)} %reshape.223), calls=%async_computation | async-start | bytes 786432 | tf_op jit(solution)/shard_map/all_to_all | solution.py:107
  29.2 5.7 %copy-start.4 = (f32[192]{0:T(256)S(1)}, f32[192]{0:T(256)}, u32[]{:S(2)}) copy-start(f32[192]{0:T(256)} %param.11) | copy-start | bytes 2308
  68.1 1.9 %copy-start.2 = (bf16[32,49152]{1,0:T(8,128)(2,1)S(1)}, bf16[32,49152]{1,0:T(8,128)(2,1)}, u32[]{:S(2)}) copy-start(bf16[32,49152]{1,0:T(8,128)(2,1)} %get-tuple-element.12) | copy-start | bytes 9437188
  71.9 2.2 %copy-start.3 = (f32[1,49152]{1,0:T(1,128)S(1)}, f32[1,49152]{1,0:T(1,128)}, u32[]{:S(2)}) copy-start(f32[1,49152]{1,0:T(1,128)} %get-tuple-element.13) | copy-start | bytes 589828
  73.6 3.5 %copy-start.1 = (f32[192,2048]{1,0:T(8,128)S(1)}, f32[192,2048]{1,0:T(8,128)}, u32[]{:S(2)}) copy-start(f32[192,2048]{1,0:T(8,128)} %copy.38) | copy-start | bytes 4718596
  78.3 2.5 %collective-permute-start = (f32[192,1152]{1,0:T(8,128)S(1)}, f32[192,1152]{1,0:T(8,128)S(1)}, u32[]{:S(2)}, u32[]{:S(2)}) collective-permute-start(f32[192,1152]{1,0:T(8,128)S(1)} %constant_dynamic-slice_fusion), channel_id=1, source_target_pairs={{0,32},{32,0},{1,33},{33,1},{2,34},{34,2},{3,35},{35,3},{4,36},{36... | collective-permute-start | bytes 2654216 | tf_op jit(solution)/shard_map/ppermute | solution.py:181

commit v19 on v16

--- a/solution.py
+++ b/solution.py
@@ -12,7 +12,7 @@
 M = 32
 R = 128
 CLS_DEV = 6
-CLS_STEP = 48
+CLS_STEP = 96
 GRP = ("x", "core")
 DEV = ("z", "y")
 

time: 129 us -> 129 us (level)
  no operation moved by 1% of the time
where the time goes in v19:
time: 129 us; the launch traced here: 128 us
  blocking collectives  49.2 us (38%)
  local copies, waits for them, and re-layouts  21.4 us (17%)
  Pallas kernels  20.8 us (16%)
  starting transfers between devices  12.5 us (10%)
  waiting for transfers between devices  12.2 us (9%)
  matrix products  5.73 us (4%)
  other arithmetic  5.6 us (4%)
    all_gather x1, blocking collectives, local(): own = lax.all_gather(own, GRP, axis=0, tiled=False)  16.1 us
    all_to_all x1, blocking collectives, local(): own = jnp.sum(lax.all_to_all(packed, 'y', 1, 1, tiled=True), 1)  15.3 us
    unnamed x22, local copies, waits for them, and re-layouts  13.7 us
    all_to_all x1, blocking collectives, local(): own = jnp.sum(lax.all_to_all(own, 'z', 0, 0, tiled=True), 0)  13.1 us
    all_to_all x1, starting transfers between devices, local(): gathered = lax.all_to_all(copies, DEV, 0, 2, tiled=True)[0]  12 us
    pallas_call x1, Pallas kernels, local(): pl.pallas_call(functools.partial(norm_kernel, columns), grid=(steps,), in...  10.7 us
    all_to_all x1, waiting for transfers between devices, local(): gathered = lax.all_to_all(copies, DEV, 0, 2, tiled=True)[0]  10.2 us
    pallas_call x1, Pallas kernels, local(): pl.pallas_call(functools.partial(spectra_kernel, columns), grid=(steps,),...  10.1 us
  transfers between devices with their start and end apart: 2, of which 2 were waited for; matrix products, arithmetic and copies ran while one was open for 3% of the time, Pallas kernels for 0%

profile of v19, /device:TPU:1, one launch (start us, length us, event | category | flops | bytes accessed | tf_op | source)
XLA Modules:
  0.0 128.4 jit_solution(16963177981390037323)
XLA Ops:
  0.6 0.0 copy-start
  0.6 0.0 copy-start.6
  0.7 0.0 copy-start.5
  0.7 0.9 reshape.200
  1.6 0.1 broadcast_bitcast_fusion
  1.7 1.2 reshape.228
  2.9 12.0 %all-to-all-start = ((bf16[32,2,3072]{2,1,0:T(2,128)(2,1)}), bf16[32,2,3072]{2,1,0:T(2,128)(2,1)S(1)}, u32[]{:S(2)}, u32[]{:S(2)}) async-start(bf16[32,2,3072]{2,1,0:T(2,128)(2,1)} %reshape.228), calls=%async_computation | async-start | bytes 786432 | tf_op jit(solution)/shard_map/all_to_all | solution.py:107
  14.9 0.0 copy-done
  14.9 0.0 copy-done.6
  14.9 0.0 copy-done.5
  14.9 0.2 fusion.17
  15.1 1.5 %fusion = bf16[32,64,256]{2,1,0:T(8,128)(2,1)S(1)} fusion(bf16[32,64,256]{2,1,0:T(8,128)(2,1)} %bitcast.69, f32[64,256]{1,0:T(8,128)S(1)} %bitcast.70), kind=kLoop, calls=%fused_computation.3 | loop fusion | flops 1572864 | bytes 2162688 | tf_op jit(solution)/shard_map/convert_element_type | solution.py:46
  16.6 0.1 fusion.18
  16.7 0.1 pad_maximum_fusion
  16.7 0.1 multiply_convert_fusion.1
  16.8 0.7 copy.37.table_ref
  17.6 0.1 pad.4.clone
  17.7 0.1 pad.3.clone
  17.7 0.1 fusion.14
  17.8 0.7 maximum_maximum_fusion.turn_ref
  18.5 10.2 %all-to-all-done = bf16[32,2,3072]{2,1,0:T(2,128)(2,1)S(1)} async-done(((bf16[32,2,3072]{2,1,0:T(2,128)(2,1)}), bf16[32,2,3072]{2,1,0:T(2,128)(2,1)S(1)}, u32[]{:S(2)}, u32[]{:S(2)}) %all-to-all-start) | async-done | bytes 393248 | tf_op jit(solution)/shard_map/all_to_all | solution.py:107
  28.7 0.5 reshape.229
  29.2 0.0 copy-start.4
  29.2 0.7 copy.35
  29.8 4.7 %all_gather.9 = bf16[32,192,64]{1,2,0:T(8,128)(2,1)S(1)} all-gather(bf16[16,192,64]{1,2,0:T(8,128)(2,1)S(1)} %copy.35), channel_id=1, replica_groups=mesh['x'=4,'core'=2,'z'=8,'y'=4] {'core'}, dimensions={0}, use_global_device_ids=true | all-gather | bytes 1179648 | tf_op jit(solution)/shard_map/all_gather | solution.py:108
  34.5 0.3 multiply_reduce_fusion
  34.8 0.0 copy-done.4
  34.8 0.4 fusion.2
  35.2 0.9 copy.46
  36.1 1.0 convolution_convert_fusion.1
  37.1 3.5 %copy.44 = bf16[4,8,192,256]{3,1,2,0:T(8,128)(2,1)} copy(bf16[4,8,192,256]{3,2,1,0:T(8,128)(2,1)S(1)} %bitcast.60) | data formatting | bytes 6291456
  40.6 1.0 convolution_convert_fusion
  41.6 3.5 %copy.45 = bf16[4,8,192,256]{3,1,2,0:T(8,128)(2,1)} copy(bf16[4,8,192,256]{3,2,1,0:T(8,128)(2,1)S(1)} %bitcast.59) | data formatting | bytes 6291456
  45.1 10.7 %shard_map.77.norm_ref = f32[1,256]{1,0:T(1,128)} custom-call(bf16[128,64]{1,0:T(8,128)(2,1)} %copy.37.table_ref, bf16[32,49152]{1,0:T(8,128)(2,1)} %bitcast.54, bf16[32,49152]{1,0:T(8,128)(2,1)} %bitcast.56, f32[1,49152]{1,0:T(1,128)} %bitcast.66), custom_call_target="tpu_custom_call" | custom-call | tf_op jit(solution)/shard_map/pallas_call | solution.py:134
  55.8 10.1 %shard_map.78 = (bf16[32,49152]{1,0:T(8,128)(2,1)}, bf16[32,49152]{1,0:T(8,128)(2,1)}, f32[1,49152]{1,0:T(1,128)}) custom-call(bf16[128,64]{1,0:T(8,128)(2,1)} %copy.37.table_ref, bf16[32,49152]{1,0:T(8,128)(2,1)} %bitcast.55, bf16[32,49152]{1,0:T(8,128)(2,1)} %bitcast.57, f32[1,49152]{1,0:T(1,128)} %bitcast.67, f32[1,256]{1,0:T(1,128)} %shard_map.77.norm_ref, ...), custom_call_target="tpu_custom_call" | custom-call | tf_op jit(solution)/shard_map/pallas_call | solution.py:143
  65.9 2.6 %copy.47 = bf16[4,8,192,256]{3,2,1,0:T(8,128)(2,1)S(1)} copy(bf16[4,8,192,256]{3,1,2,0:T(8,128)(2,1)} %bitcast.64) | data formatting | bytes 6291456
  68.6 0.0 copy-start.2
  68.6 1.1 fusion.19
  69.7 0.8 copy-done.2
  70.4 0.7 copy.48
  71.2 1.1 convolution_add_fusion
  72.3 1.7 %copy.38 = f32[192,2048]{1,0:T(8,128)} copy(f32[192,2048]{0,1:T(8,128)S(1)} %bitcast.62) | data formatting | bytes 3145728 | tf_op jit(solution)/shard_map/reshape | solution.py:168
  74.0 0.5 broadcast.233
  74.6 0.0 copy-done.3
  74.6 1.1 reduce.5
  75.7 0.1 reshape.207
  75.7 0.9 fusion.20
  76.7 0.1 reduce_sum.46
  76.8 0.8 copy.40
  77.6 1.1 concatenate.14
  78.7 0.1 constant_dynamic-slice_fusion
  78.8 0.5 collective-permute-start
  79.2 2.1 %collective-permute-done = f32[192,1152]{1,0:T(8,128)S(1)} collective-permute-done((f32[192,1152]{1,0:T(8,128)S(1)}, f32[192,1152]{1,0:T(8,128)S(1)}, u32[]{:S(2)}, u32[]{:S(2)}) %collective-permute-start) | collective-permute-done | bytes 884768 | tf_op jit(solution)/shard_map/ppermute | solution.py:181
  81.3 0.1 dynamic-slice_add_fusion
  81.4 0.1 reshape.208
  81.5 0.5 copy.41
  82.1 15.3 %all_to_all.25 = f32[8,4,6,1152]{3,0,2,1:T(8,128)S(1)} all-to-all(f32[8,4,6,1152]{3,0,2,1:T(8,128)S(1)} %copy.41), channel_id=1, replica_groups=mesh['x'=4,'core'=2,'z'=8,'y'=4] {'y'}, dimensions={1} | all-to-all | bytes 1769472 | tf_op jit(solution)/shard_map/all_to_all | solution.py:183
  97.4 0.1 copy.42
  97.5 13.1 %all_to_all.26 = f32[8,6,1152]{2,1,0:T(8,128)S(1)} all-to-all(f32[8,6,1152]{2,1,0:T(8,128)S(1)} %copy.42), channel_id=1, replica_groups=mesh['x'=4,'core'=2,'z'=8,'y'=4] {'z'}, dimensions={0} | all-to-all | bytes 442368 | tf_op jit(solution)/shard_map/all_to_all | solution.py:184
  110.6 16.1 %all-gather.1 = f32[8,6,1152]{2,1,0:T(8,128)S(1)} all-gather(f32[1,6,1152]{2,1,0:T(8,128)S(1)} %bitcast.71), channel_id=2, replica_groups=mesh['x'=4,'core'=2,'z'=8,'y'=4] {'x','core'}, dimensions={0}, use_global_device_ids=true | all-gather | bytes 248832 | tf_op jit(solution)/shard_map/all_gather | solution.py:185
  126.7 0.7 fusion.16
  127.4 0.1 div.21
  127.5 0.2 div.22
  127.7 0.7 fusion.3
  (15 shorter events, 0.2 us)
Async XLA Ops:
  0.6 14.3 %copy-start = (f32[64,32]{0,1:T(8,128)S(1)}, f32[64,32]{0,1:T(8,128)}, u32[]{:S(2)}) copy-start(f32[64,32]{0,1:T(8,128)} %param.9) | copy-start | bytes 24580
  0.6 14.3 %copy-start.6 = (f32[32]{0:T(128)S(1)}, f32[32]{0:T(128)}, u32[]{:S(2)}) copy-start(f32[32]{0:T(128)} %param.10) | copy-start | bytes 388
  0.7 14.3 %copy-start.5 = (s32[256]{0:T(256)S(1)}, s32[256]{0:T(256)}, u32[]{:S(2)}) copy-start(s32[256]{0:T(256)} %param.8) | copy-start | bytes 3076
  2.9 25.8 %all-to-all-start = ((bf16[32,2,3072]{2,1,0:T(2,128)(2,1)}), bf16[32,2,3072]{2,1,0:T(2,128)(2,1)S(1)}, u32[]{:S(2)}, u32[]{:S(2)}) async-start(bf16[32,2,3072]{2,1,0:T(2,128)(2,1)} %reshape.228), calls=%async_computation | async-start | bytes 786432 | tf_op jit(solution)/shard_map/all_to_all | solution.py:107
  29.2 5.7 %copy-start.4 = (f32[192]{0:T(256)S(1)}, f32[192]{0:T(256)}, u32[]{:S(2)}) copy-start(f32[192]{0:T(256)} %param.11) | copy-start | bytes 2308
  68.6 1.9 %copy-start.2 = (bf16[32,49152]{1,0:T(8,128)(2,1)S(1)}, bf16[32,49152]{1,0:T(8,128)(2,1)}, u32[]{:S(2)}) copy-start(bf16[32,49152]{1,0:T(8,128)(2,1)} %get-tuple-element.12) | copy-start | bytes 9437188
  72.3 2.2 %copy-start.3 = (f32[1,49152]{1,0:T(1,128)S(1)}, f32[1,49152]{1,0:T(1,128)}, u32[]{:S(2)}) copy-start(f32[1,49152]{1,0:T(1,128)} %get-tuple-element.13) | copy-start | bytes 589828
  74.0 3.5 %copy-start.1 = (f32[192,2048]{1,0:T(8,128)S(1)}, f32[192,2048]{1,0:T(8,128)}, u32[]{:S(2)}) copy-start(f32[192,2048]{1,0:T(8,128)} %copy.38) | copy-start | bytes 4718596
  78.8 2.5 %collective-permute-start = (f32[192,1152]{1,0:T(8,128)S(1)}, f32[192,1152]{1,0:T(8,128)S(1)}, u32[]{:S(2)}, u32[]{:S(2)}) collective-permute-start(f32[192,1152]{1,0:T(8,128)S(1)} %constant_dynamic-slice_fusion), channel_id=1, source_target_pairs={{0,32},{32,0},{1,33},{33,1},{2,34},{34,2},{3,35},{35,3},{4,36},{36... | collective-permute-start | bytes 2654216 | tf_op jit(solution)/shard_map/ppermute | solution.py:181

commit v20 on v16

--- a/solution.py
+++ b/solution.py
@@ -176,9 +176,8 @@
     )
     core_count = lax.axis_size("core")
     half = packed.shape[1] // core_count
-    mine = lax.dynamic_slice_in_dim(packed, core * half, half, 1)
-    other = lax.dynamic_slice_in_dim(packed, (1 - core) * half, half, 1)
-    packed = mine + lax.ppermute(other, "core", [(0, 1), (1, 0)])
+    paired = lax.all_to_all(packed.reshape(classes_total, core_count, half), "core", 1, 1, tiled=True)
+    packed = jnp.sum(paired, 1)
     packed = packed.reshape(lax.axis_size("z"), lax.axis_size("y"), CLS_DEV, half)
     own = jnp.sum(lax.all_to_all(packed, "y", 1, 1, tiled=True), 1)
     own = jnp.sum(lax.all_to_all(own, "z", 0, 0, tiled=True), 0)

time: 129 us -> 131 us (1.016)
  blocking collectives: 49.2 us -> 54.3 us
  waiting for transfers between devices: 12.2 us -> 10.2 us
    all_to_all x0 -> x1, blocking collectives: none -> 5.15 us  [local(): lax.all_to_all(packed.reshape(classes_total, core_count, half), 'core', 1...]
    ppermute x1 -> x0, waiting for transfers between devices: 2.06 us -> none  [local(): packed = mine + lax.ppermute(other, 'core', [(0, 1), (1, 0)])]
  transfers between devices with their start and end apart: 2 -> 1, of which waited for: 2 -> 1; matrix products, arithmetic and copies ran while one was open for 3% -> 3% of each run, Pallas kernels for 0% -> 0%
where the time goes in v20:
time: 131 us
  blocking collectives  54.3 us (41%)
  local copies, waits for them, and re-layouts  21.5 us (16%)
  Pallas kernels  20.4 us (16%)
  starting transfers between devices  12 us (9%)
  waiting for transfers between devices  10.2 us (8%)
  matrix products  5.74 us (4%)
  other arithmetic  5.66 us (4%)
    all_gather x1, blocking collectives, local(): own = lax.all_gather(own, GRP, axis=0, tiled=False)  16.2 us
    all_to_all x1, blocking collectives, local(): own = jnp.sum(lax.all_to_all(packed, 'y', 1, 1, tiled=True), 1)  15.3 us
    unnamed x22, local copies, waits for them, and re-layouts  13.7 us
    all_to_all x1, blocking collectives, local(): own = jnp.sum(lax.all_to_all(own, 'z', 0, 0, tiled=True), 0)  13 us
    all_to_all x1, starting transfers between devices, local(): gathered = lax.all_to_all(copies, DEV, 0, 2, tiled=True)[0]  12 us
    pallas_call x1, Pallas kernels, local(): pl.pallas_call(functools.partial(norm_kernel, columns), grid=(steps,), in...  10.4 us
    all_to_all x1, waiting for transfers between devices, local(): gathered = lax.all_to_all(copies, DEV, 0, 2, tiled=True)[0]  10.2 us
    pallas_call x1, Pallas kernels, local(): pl.pallas_call(functools.partial(spectra_kernel, columns), grid=(steps,),...  9.92 us
  transfers between devices with their start and end apart: 1, of which 1 were waited for; matrix products, arithmetic and copies ran while one was open for 3% of the time, Pallas kernels for 0%

profile of v20, /device:TPU:1, one launch (start us, length us, event | category | flops | bytes accessed | tf_op | source)
XLA Modules:
  0.0 130.7 jit_solution(3590438274103788087)
XLA Ops:
  0.6 0.0 copy-start
  0.6 0.0 copy-start.6
  0.7 0.0 copy-start.5
  0.7 0.9 reshape.203
  1.6 0.1 broadcast_bitcast_fusion
  1.7 1.2 reshape.232
  2.9 12.0 %all-to-all-start = ((bf16[32,2,3072]{2,1,0:T(2,128)(2,1)}), bf16[32,2,3072]{2,1,0:T(2,128)(2,1)S(1)}, u32[]{:S(2)}, u32[]{:S(2)}) async-start(bf16[32,2,3072]{2,1,0:T(2,128)(2,1)} %reshape.232), calls=%async_computation | async-start | bytes 786432 | tf_op jit(solution)/shard_map/all_to_all | solution.py:107
  14.9 0.0 copy-done
  14.9 0.0 copy-done.6
  14.9 0.0 copy-done.5
  14.9 0.2 fusion.17
  15.1 1.5 %fusion = bf16[32,64,256]{2,1,0:T(8,128)(2,1)S(1)} fusion(bf16[32,64,256]{2,1,0:T(8,128)(2,1)} %bitcast.75, f32[64,256]{1,0:T(8,128)S(1)} %bitcast.76), kind=kLoop, calls=%fused_computation.3 | loop fusion | flops 1572864 | bytes 2162688 | tf_op jit(solution)/shard_map/convert_element_type | solution.py:46
  16.6 0.1 fusion.18
  16.7 0.1 pad_maximum_fusion
  16.7 0.1 multiply_convert_fusion.1
  16.9 0.7 copy.50.table_ref
  17.6 0.1 pad.4.clone
  17.7 0.1 pad.3.clone
  17.7 0.1 fusion.14
  17.8 0.7 maximum_maximum_fusion.turn_ref
  18.5 10.2 %all-to-all-done = bf16[32,2,3072]{2,1,0:T(2,128)(2,1)S(1)} async-done(((bf16[32,2,3072]{2,1,0:T(2,128)(2,1)}), bf16[32,2,3072]{2,1,0:T(2,128)(2,1)S(1)}, u32[]{:S(2)}, u32[]{:S(2)}) %all-to-all-start) | async-done | bytes 393248 | tf_op jit(solution)/shard_map/all_to_all | solution.py:107
  28.7 0.5 reshape.233
  29.2 0.0 copy-start.4
  29.2 0.7 copy.48
  29.8 4.7 %all_gather.9 = bf16[32,192,64]{1,2,0:T(8,128)(2,1)S(1)} all-gather(bf16[16,192,64]{1,2,0:T(8,128)(2,1)S(1)} %copy.48), channel_id=1, replica_groups=mesh['x'=4,'core'=2,'z'=8,'y'=4] {'core'}, dimensions={0}, use_global_device_ids=true | all-gather | bytes 1179648 | tf_op jit(solution)/shard_map/all_gather | solution.py:108
  34.5 0.3 multiply_reduce_fusion
  34.8 0.0 copy-done.4
  34.8 0.4 fusion.2
  35.2 0.9 copy.64
  36.1 1.0 convolution_convert_fusion.1
  37.1 3.5 %copy.62 = bf16[4,8,192,256]{3,1,2,0:T(8,128)(2,1)} copy(bf16[4,8,192,256]{3,2,1,0:T(8,128)(2,1)S(1)} %bitcast.64) | data formatting | bytes 6291456
  40.6 1.0 convolution_convert_fusion
  41.6 3.5 %copy.63 = bf16[4,8,192,256]{3,1,2,0:T(8,128)(2,1)} copy(bf16[4,8,192,256]{3,2,1,0:T(8,128)(2,1)S(1)} %bitcast.63) | data formatting | bytes 6291456
  45.1 10.4 %shard_map.77.norm_ref = f32[1,256]{1,0:T(1,128)} custom-call(bf16[128,64]{1,0:T(8,128)(2,1)} %copy.50.table_ref, bf16[32,49152]{1,0:T(8,128)(2,1)} %bitcast.58, bf16[32,49152]{1,0:T(8,128)(2,1)} %bitcast.60, f32[1,49152]{1,0:T(1,128)} %bitcast.72), custom_call_target="tpu_custom_call" | custom-call | tf_op jit(solution)/shard_map/pallas_call | solution.py:134
  55.5 9.9 %shard_map.78 = (bf16[32,49152]{1,0:T(8,128)(2,1)}, bf16[32,49152]{1,0:T(8,128)(2,1)}, f32[1,49152]{1,0:T(1,128)}) custom-call(bf16[128,64]{1,0:T(8,128)(2,1)} %copy.50.table_ref, bf16[32,49152]{1,0:T(8,128)(2,1)} %bitcast.59, bf16[32,49152]{1,0:T(8,128)(2,1)} %bitcast.61, f32[1,49152]{1,0:T(1,128)} %bitcast.73, f32[1,256]{1,0:T(1,128)} %shard_map.77.norm_ref, ...), custom_call_target="tpu_custom_call" | custom-call | tf_op jit(solution)/shard_map/pallas_call | solution.py:143
  65.5 2.6 %copy.65 = bf16[4,8,192,256]{3,2,1,0:T(8,128)(2,1)S(1)} copy(bf16[4,8,192,256]{3,1,2,0:T(8,128)(2,1)} %bitcast.70) | data formatting | bytes 6291456
  68.1 0.0 copy-start.2
  68.1 1.1 fusion.19
  69.2 0.8 copy-done.2
  70.0 0.7 copy.66
  70.7 1.1 convolution_add_fusion
  71.9 1.7 %copy.51 = f32[192,2048]{1,0:T(8,128)} copy(f32[192,2048]{0,1:T(8,128)S(1)} %bitcast.66) | data formatting | bytes 3145728 | tf_op jit(solution)/shard_map/reshape | solution.py:168
  73.6 0.5 broadcast.233
  74.1 0.0 copy-done.3
  74.1 1.1 reduce.5
  75.2 0.1 reshape.210
  75.3 0.9 fusion.20
  76.2 0.1 reduce_sum.55
  76.3 0.8 copy.53
  77.1 0.0 copy-done.1
  77.1 1.1 concatenate.14
  78.3 0.1 copy.68
  78.4 5.2 %all_to_all.30 = f32[192,2,1152]{2,0,1:T(8,128)S(1)} all-to-all(f32[192,2,1152]{2,0,1:T(8,128)S(1)} %bitcast.68), channel_id=1, replica_groups=mesh['x'=4,'core'=2,'z'=8,'y'=4] {'core'}, dimensions={1} | all-to-all | bytes 3538944 | tf_op jit(solution)/shard_map/all_to_all | solution.py:179
  83.5 0.2 reduce_sum.56
  83.7 0.1 reshape.212
  83.9 0.5 copy.57
  84.4 15.3 %all_to_all.31 = f32[8,4,6,1152]{3,0,2,1:T(8,128)S(1)} all-to-all(f32[8,4,6,1152]{3,0,2,1:T(8,128)S(1)} %copy.57), channel_id=1, replica_groups=mesh['x'=4,'core'=2,'z'=8,'y'=4] {'y'}, dimensions={1} | all-to-all | bytes 1769472 | tf_op jit(solution)/shard_map/all_to_all | solution.py:182
  99.8 0.1 copy.58
  99.8 13.0 %all_to_all.32 = f32[8,6,1152]{2,1,0:T(8,128)S(1)} all-to-all(f32[8,6,1152]{2,1,0:T(8,128)S(1)} %copy.58), channel_id=1, replica_groups=mesh['x'=4,'core'=2,'z'=8,'y'=4] {'z'}, dimensions={0} | all-to-all | bytes 442368 | tf_op jit(solution)/shard_map/all_to_all | solution.py:183
  112.8 16.2 %all-gather.1 = f32[8,6,1152]{2,1,0:T(8,128)S(1)} all-gather(f32[1,6,1152]{2,1,0:T(8,128)S(1)} %bitcast.77), channel_id=2, replica_groups=mesh['x'=4,'core'=2,'z'=8,'y'=4] {'x','core'}, dimensions={0}, use_global_device_ids=true | all-gather | bytes 248832 | tf_op jit(solution)/shard_map/all_gather | solution.py:184
  129.0 0.7 fusion.16
  129.7 0.1 div.21
  129.8 0.2 div.22
  130.0 0.7 fusion.3
  (14 shorter events, 0.2 us)
Async XLA Ops:
  0.6 14.3 %copy-start = (f32[64,32]{0,1:T(8,128)S(1)}, f32[64,32]{0,1:T(8,128)}, u32[]{:S(2)}) copy-start(f32[64,32]{0,1:T(8,128)} %param.9) | copy-start | bytes 24580
  0.6 14.3 %copy-start.6 = (f32[32]{0:T(128)S(1)}, f32[32]{0:T(128)}, u32[]{:S(2)}) copy-start(f32[32]{0:T(128)} %param.10) | copy-start | bytes 388
  0.7 14.3 %copy-start.5 = (s32[256]{0:T(256)S(1)}, s32[256]{0:T(256)}, u32[]{:S(2)}) copy-start(s32[256]{0:T(256)} %param.8) | copy-start | bytes 3076
  2.9 25.8 %all-to-all-start = ((bf16[32,2,3072]{2,1,0:T(2,128)(2,1)}), bf16[32,2,3072]{2,1,0:T(2,128)(2,1)S(1)}, u32[]{:S(2)}, u32[]{:S(2)}) async-start(bf16[32,2,3072]{2,1,0:T(2,128)(2,1)} %reshape.232), calls=%async_computation | async-start | bytes 786432 | tf_op jit(solution)/shard_map/all_to_all | solution.py:107
  29.2 5.7 %copy-start.4 = (f32[192]{0:T(256)S(1)}, f32[192]{0:T(256)}, u32[]{:S(2)}) copy-start(f32[192]{0:T(256)} %param.11) | copy-start | bytes 2308
  68.1 1.9 %copy-start.2 = (bf16[32,49152]{1,0:T(8,128)(2,1)S(1)}, bf16[32,49152]{1,0:T(8,128)(2,1)}, u32[]{:S(2)}) copy-start(bf16[32,49152]{1,0:T(8,128)(2,1)} %get-tuple-element.12) | copy-start | bytes 9437188
  71.9 2.2 %copy-start.3 = (f32[1,49152]{1,0:T(1,128)S(1)}, f32[1,49152]{1,0:T(1,128)}, u32[]{:S(2)}) copy-start(f32[1,49152]{1,0:T(1,128)} %get-tuple-element.13) | copy-start | bytes 589828
  73.6 3.5 %copy-start.1 = (f32[192,2048]{1,0:T(8,128)S(1)}, f32[192,2048]{1,0:T(8,128)}, u32[]{:S(2)}) copy-start(f32[192,2048]{1,0:T(8,128)} %copy.51) | copy-start | bytes 4718596

commit v21 on v19

--- a/solution.py
+++ b/solution.py
@@ -12,7 +12,7 @@
 M = 32
 R = 128
 CLS_DEV = 6
-CLS_STEP = 96
+CLS_STEP = 64
 GRP = ("x", "core")
 DEV = ("z", "y")
 

time: 129 us -> 129 us (level)
  no operation moved by 1% of the time
where the time goes in v21:
time: 129 us; the launch traced here: 128 us
  blocking collectives  49.2 us (38%)
  local copies, waits for them, and re-layouts  21.4 us (17%)
  Pallas kernels  20.5 us (16%)
  starting transfers between devices  12.5 us (10%)
  waiting for transfers between devices  12.2 us (9%)
  matrix products  5.73 us (4%)
  other arithmetic  5.6 us (4%)
    all_gather x1, blocking collectives, local(): own = lax.all_gather(own, GRP, axis=0, tiled=False)  16.2 us
    all_to_all x1, blocking collectives, local(): own = jnp.sum(lax.all_to_all(packed, 'y', 1, 1, tiled=True), 1)  15.3 us
    unnamed x22, local copies, waits for them, and re-layouts  13.7 us
    all_to_all x1, blocking collectives, local(): own = jnp.sum(lax.all_to_all(own, 'z', 0, 0, tiled=True), 0)  13 us
    all_to_all x1, starting transfers between devices, local(): gathered = lax.all_to_all(copies, DEV, 0, 2, tiled=True)[0]  12 us
    pallas_call x1, Pallas kernels, local(): pl.pallas_call(functools.partial(norm_kernel, columns), grid=(steps,), in...  10.5 us
    all_to_all x1, waiting for transfers between devices, local(): gathered = lax.all_to_all(copies, DEV, 0, 2, tiled=True)[0]  10.2 us
    pallas_call x1, Pallas kernels, local(): pl.pallas_call(functools.partial(spectra_kernel, columns), grid=(steps,),...  10 us
  transfers between devices with their start and end apart: 2, of which 2 were waited for; matrix products, arithmetic and copies ran while one was open for 3% of the time, Pallas kernels for 0%

profile of v21, /device:TPU:1, one launch (start us, length us, event | category | flops | bytes accessed | tf_op | source)
XLA Modules:
  0.0 128.1 jit_solution(3480429598645488536)
XLA Ops:
  0.6 0.0 copy-start
  0.6 0.0 copy-start.6
  0.7 0.0 copy-start.5
  0.7 0.9 reshape.200
  1.6 0.1 broadcast_bitcast_fusion
  1.7 1.2 reshape.228
  2.9 12.0 %all-to-all-start = ((bf16[32,2,3072]{2,1,0:T(2,128)(2,1)}), bf16[32,2,3072]{2,1,0:T(2,128)(2,1)S(1)}, u32[]{:S(2)}, u32[]{:S(2)}) async-start(bf16[32,2,3072]{2,1,0:T(2,128)(2,1)} %reshape.228), calls=%async_computation | async-start | bytes 786432 | tf_op jit(solution)/shard_map/all_to_all | solution.py:107
  14.9 0.0 copy-done
  14.9 0.0 copy-done.6
  14.9 0.0 copy-done.5
  14.9 0.2 fusion.17
  15.1 1.5 %fusion = bf16[32,64,256]{2,1,0:T(8,128)(2,1)S(1)} fusion(bf16[32,64,256]{2,1,0:T(8,128)(2,1)} %bitcast.69, f32[64,256]{1,0:T(8,128)S(1)} %bitcast.70), kind=kLoop, calls=%fused_computation.3 | loop fusion | flops 1572864 | bytes 2162688 | tf_op jit(solution)/shard_map/convert_element_type | solution.py:46
  16.6 0.1 fusion.18
  16.7 0.1 pad_maximum_fusion
  16.7 0.1 multiply_convert_fusion.1
  16.8 0.7 copy.37.table_ref
  17.6 0.1 pad.4.clone
  17.7 0.1 pad.3.clone
  17.7 0.1 fusion.14
  17.8 0.7 maximum_maximum_fusion.turn_ref
  18.5 10.2 %all-to-all-done = bf16[32,2,3072]{2,1,0:T(2,128)(2,1)S(1)} async-done(((bf16[32,2,3072]{2,1,0:T(2,128)(2,1)}), bf16[32,2,3072]{2,1,0:T(2,128)(2,1)S(1)}, u32[]{:S(2)}, u32[]{:S(2)}) %all-to-all-start) | async-done | bytes 393248 | tf_op jit(solution)/shard_map/all_to_all | solution.py:107
  28.7 0.5 reshape.229
  29.2 0.0 copy-start.4
  29.2 0.7 copy.35
  29.8 4.7 %all_gather.9 = bf16[32,192,64]{1,2,0:T(8,128)(2,1)S(1)} all-gather(bf16[16,192,64]{1,2,0:T(8,128)(2,1)S(1)} %copy.35), channel_id=1, replica_groups=mesh['x'=4,'core'=2,'z'=8,'y'=4] {'core'}, dimensions={0}, use_global_device_ids=true | all-gather | bytes 1179648 | tf_op jit(solution)/shard_map/all_gather | solution.py:108
  34.5 0.3 multiply_reduce_fusion
  34.8 0.0 copy-done.4
  34.8 0.4 fusion.2
  35.2 0.9 copy.46
  36.1 1.0 convolution_convert_fusion.1
  37.1 3.5 %copy.44 = bf16[4,8,192,256]{3,1,2,0:T(8,128)(2,1)} copy(bf16[4,8,192,256]{3,2,1,0:T(8,128)(2,1)S(1)} %bitcast.60) | data formatting | bytes 6291456
  40.6 1.0 convolution_convert_fusion
  41.6 3.5 %copy.45 = bf16[4,8,192,256]{3,1,2,0:T(8,128)(2,1)} copy(bf16[4,8,192,256]{3,2,1,0:T(8,128)(2,1)S(1)} %bitcast.59) | data formatting | bytes 6291456
  45.1 10.5 %shard_map.77.norm_ref = f32[1,256]{1,0:T(1,128)} custom-call(bf16[128,64]{1,0:T(8,128)(2,1)} %copy.37.table_ref, bf16[32,49152]{1,0:T(8,128)(2,1)} %bitcast.54, bf16[32,49152]{1,0:T(8,128)(2,1)} %bitcast.56, f32[1,49152]{1,0:T(1,128)} %bitcast.66), custom_call_target="tpu_custom_call" | custom-call | tf_op jit(solution)/shard_map/pallas_call | solution.py:134
  55.6 10.0 %shard_map.78 = (bf16[32,49152]{1,0:T(8,128)(2,1)}, bf16[32,49152]{1,0:T(8,128)(2,1)}, f32[1,49152]{1,0:T(1,128)}) custom-call(bf16[128,64]{1,0:T(8,128)(2,1)} %copy.37.table_ref, bf16[32,49152]{1,0:T(8,128)(2,1)} %bitcast.55, bf16[32,49152]{1,0:T(8,128)(2,1)} %bitcast.57, f32[1,49152]{1,0:T(1,128)} %bitcast.67, f32[1,256]{1,0:T(1,128)} %shard_map.77.norm_ref, ...), custom_call_target="tpu_custom_call" | custom-call | tf_op jit(solution)/shard_map/pallas_call | solution.py:143
  65.6 2.6 %copy.47 = bf16[4,8,192,256]{3,2,1,0:T(8,128)(2,1)S(1)} copy(bf16[4,8,192,256]{3,1,2,0:T(8,128)(2,1)} %bitcast.64) | data formatting | bytes 6291456
  68.2 0.0 copy-start.2
  68.3 1.1 fusion.19
  69.4 0.8 copy-done.2
  70.1 0.7 copy.48
  70.9 1.1 convolution_add_fusion
  72.0 1.7 %copy.38 = f32[192,2048]{1,0:T(8,128)} copy(f32[192,2048]{0,1:T(8,128)S(1)} %bitcast.62) | data formatting | bytes 3145728 | tf_op jit(solution)/shard_map/reshape | solution.py:168
  73.7 0.5 broadcast.233
  74.2 0.0 copy-done.3
  74.2 1.1 reduce.5
  75.4 0.1 reshape.207
  75.4 0.9 fusion.20
  76.3 0.1 reduce_sum.46
  76.5 0.8 copy.40
  77.3 1.1 concatenate.14
  78.4 0.1 constant_dynamic-slice_fusion
  78.5 0.5 collective-permute-start
  78.9 2.1 %collective-permute-done = f32[192,1152]{1,0:T(8,128)S(1)} collective-permute-done((f32[192,1152]{1,0:T(8,128)S(1)}, f32[192,1152]{1,0:T(8,128)S(1)}, u32[]{:S(2)}, u32[]{:S(2)}) %collective-permute-start) | collective-permute-done | bytes 884768 | tf_op jit(solution)/shard_map/ppermute | solution.py:181
  81.0 0.1 dynamic-slice_add_fusion
  81.1 0.1 reshape.208
  81.2 0.5 copy.41
  81.8 15.3 %all_to_all.25 = f32[8,4,6,1152]{3,0,2,1:T(8,128)S(1)} all-to-all(f32[8,4,6,1152]{3,0,2,1:T(8,128)S(1)} %copy.41), channel_id=1, replica_groups=mesh['x'=4,'core'=2,'z'=8,'y'=4] {'y'}, dimensions={1} | all-to-all | bytes 1769472 | tf_op jit(solution)/shard_map/all_to_all | solution.py:183
  97.1 0.1 copy.42
  97.2 13.0 %all_to_all.26 = f32[8,6,1152]{2,1,0:T(8,128)S(1)} all-to-all(f32[8,6,1152]{2,1,0:T(8,128)S(1)} %copy.42), channel_id=1, replica_groups=mesh['x'=4,'core'=2,'z'=8,'y'=4] {'z'}, dimensions={0} | all-to-all | bytes 442368 | tf_op jit(solution)/shard_map/all_to_all | solution.py:184
  110.2 16.2 %all-gather.1 = f32[8,6,1152]{2,1,0:T(8,128)S(1)} all-gather(f32[1,6,1152]{2,1,0:T(8,128)S(1)} %bitcast.71), channel_id=2, replica_groups=mesh['x'=4,'core'=2,'z'=8,'y'=4] {'x','core'}, dimensions={0}, use_global_device_ids=true | all-gather | bytes 248832 | tf_op jit(solution)/shard_map/all_gather | solution.py:185
  126.5 0.7 fusion.16
  127.2 0.1 div.21
  127.2 0.2 div.22
  127.5 0.7 fusion.3
  (15 shorter events, 0.2 us)
Async XLA Ops:
  0.6 14.3 %copy-start = (f32[64,32]{0,1:T(8,128)S(1)}, f32[64,32]{0,1:T(8,128)}, u32[]{:S(2)}) copy-start(f32[64,32]{0,1:T(8,128)} %param.9) | copy-start | bytes 24580
  0.6 14.3 %copy-start.6 = (f32[32]{0:T(128)S(1)}, f32[32]{0:T(128)}, u32[]{:S(2)}) copy-start(f32[32]{0:T(128)} %param.10) | copy-start | bytes 388
  0.7 14.3 %copy-start.5 = (s32[256]{0:T(256)S(1)}, s32[256]{0:T(256)}, u32[]{:S(2)}) copy-start(s32[256]{0:T(256)} %param.8) | copy-start | bytes 3076
  2.9 25.8 %all-to-all-start = ((bf16[32,2,3072]{2,1,0:T(2,128)(2,1)}), bf16[32,2,3072]{2,1,0:T(2,128)(2,1)S(1)}, u32[]{:S(2)}, u32[]{:S(2)}) async-start(bf16[32,2,3072]{2,1,0:T(2,128)(2,1)} %reshape.228), calls=%async_computation | async-start | bytes 786432 | tf_op jit(solution)/shard_map/all_to_all | solution.py:107
  29.2 5.7 %copy-start.4 = (f32[192]{0:T(256)S(1)}, f32[192]{0:T(256)}, u32[]{:S(2)}) copy-start(f32[192]{0:T(256)} %param.11) | copy-start | bytes 2308
  68.2 1.9 %copy-start.2 = (bf16[32,49152]{1,0:T(8,128)(2,1)S(1)}, bf16[32,49152]{1,0:T(8,128)(2,1)}, u32[]{:S(2)}) copy-start(bf16[32,49152]{1,0:T(8,128)(2,1)} %get-tuple-element.12) | copy-start | bytes 9437188
  72.0 2.2 %copy-start.3 = (f32[1,49152]{1,0:T(1,128)S(1)}, f32[1,49152]{1,0:T(1,128)}, u32[]{:S(2)}) copy-start(f32[1,49152]{1,0:T(1,128)} %get-tuple-element.13) | copy-start | bytes 589828
  73.7 3.5 %copy-start.1 = (f32[192,2048]{1,0:T(8,128)S(1)}, f32[192,2048]{1,0:T(8,128)}, u32[]{:S(2)}) copy-start(f32[192,2048]{1,0:T(8,128)} %copy.38) | copy-start | bytes 4718596
  78.5 2.5 %collective-permute-start = (f32[192,1152]{1,0:T(8,128)S(1)}, f32[192,1152]{1,0:T(8,128)S(1)}, u32[]{:S(2)}, u32[]{:S(2)}) collective-permute-start(f32[192,1152]{1,0:T(8,128)S(1)} %constant_dynamic-slice_fusion), channel_id=1, source_target_pairs={{0,32},{32,0},{1,33},{33,1},{2,34},{34,2},{3,35},{35,3},{4,36},{36... | collective-permute-start | bytes 2654216 | tf_op jit(solution)/shard_map/ppermute | solution.py:181
